TPU v7x, 512 devices: a whole 4x8x8 slice. The times are simulated.
512 devices in a mesh: rev: 8 (over z_lo, x), bin: 64 (over y, z_hi, core).
Axes of the slice: x: 4, y: 8, z: 8 (z_hi: 4, z_lo: 2; z = z_hi * 2 + z_lo), core: 2. Of those that a mesh axis runs over, the one named last changes fastest.
Arguments:
- snapshots: float32 [8, 512, 3, 24, 8, 128], P('rev', 'bin'), may hold values from -6 to 6
- phase_index: int32 [8, 512], P('rev', 'bin'), may hold values from 0 to 255, as said below
Outputs:
- stress_terms: float32 [4, 6, 256, 24, 8, 128], P(None, None, 'bin', 'rev')
- mean_velocity: float32 [3, 256, 24, 8, 128], P(None, 'bin', 'rev')
Inputs may be any that keep to these rules, and one draw needn't show every extreme that they name: `phase_index`: the rows b * 8 to (b + 1) * 8 - 1 of a revolution shard name bins b * 4 to (b + 1) * 4 - 1 only, and each of these bins at least once.
All inputs are finite; a program needn't handle non-finite values.
Results may differ from a plain program's by a relative error of at most 0.00017.
Values sent between devices are 32-bit elements; how exact they have to be, the bound alone decides.
No kernel may reach another device: no remote copies, remote signals or barrier semaphores. Data moves between devices by JAX's collectives and lax.ppermute only.
A program may use at most 64 MiB of HBM per device.

v0:
```python
import jax
import jax.numpy as jnp
from jax import lax
from jax.sharding import PartitionSpec as P

PHASES = 256


viscosity = 0.2
stress_pairs = ((0, 0), (0, 1), (0, 2), (1, 1), (1, 2), (2, 2))


def padded_2(cells, sides, width):
    for axis, dim in sides:
        count = lax.axis_size(axis)
        head = lax.slice_in_dim(cells, 0, width, axis=dim)
        tail = lax.slice_in_dim(cells, cells.shape[dim] - width, cells.shape[dim], axis=dim)
        cells = jnp.concatenate(
            [
                lax.ppermute(tail, axis, [(i, (i + 1) % count) for i in range(count)]),
                cells,
                lax.ppermute(head, axis, [((i + 1) % count, i) for i in range(count)]),
            ],
            axis=dim,
        )
    return cells


def pair_index(first, second):
    low, high = (min(first, second), max(first, second))
    return stress_pairs.index((low, high))


def binned(frames, weights):
    vel_x, vel_y, vel_z = (frames[:, 0], frames[:, 1], frames[:, 2])
    stacked = jnp.stack(
        [
            jnp.ones_like(vel_x),
            vel_x,
            vel_y,
            vel_z,
            vel_x * vel_x,
            vel_x * vel_y,
            vel_x * vel_z,
            vel_y * vel_y,
            vel_y * vel_z,
            vel_z * vel_z,
        ],
        axis=1,
    )
    return jnp.einsum("ps,sfxyz->xfpyz", weights, stacked, precision=lax.Precision.HIGHEST)


def first_diff(shifted):
    return (
        0.75 * (shifted(1) - shifted(-1))
        - 0.15 * (shifted(2) - shifted(-2))
        + (shifted(3) - shifted(-3)) / 60.0
    )


def second_diff(shifted, centre):
    return (
        -49.0 / 18.0 * centre
        + 1.5 * (shifted(1) + shifted(-1))
        - 0.15 * (shifted(2) + shifted(-2))
        + (shifted(3) + shifted(-3)) / 90.0
    )


def finish_terms(owned):
    planes, bins_dev = (owned.shape[0], owned.shape[2])
    samples = owned[:, 0]
    velocity = [owned[:, 1 + comp] / samples for comp in range(3)]
    stresses = [
        owned[:, 4 + slot] / samples - velocity[pair[0]] * velocity[pair[1]]
        for slot, pair in enumerate(stress_pairs)
    ]
    fields = jnp.stack(velocity + stresses, axis=1)
    padded = padded_2(fields, (("rev", 0), ("bin", 2)), 3)

    def along(component, dim, centre):
        source = padded[:, component]
        if dim == 0:
            return lambda amount: source[3 + amount : 3 + amount + planes, 3 : 3 + bins_dev]
        if dim == 3:
            return lambda amount: source[3 : 3 + planes, 3 + amount : 3 + amount + bins_dev]
        return lambda amount: jnp.roll(centre, -amount, dim + 1)

    grad_u = [
        [first_diff(along(comp, dim, velocity[comp])) for dim in range(3)] for comp in range(3)
    ]
    unsteady, convect, produce, diffuse = ([], [], [], [])
    for slot, pair in enumerate(stress_pairs):
        first, second = pair
        stress = stresses[slot]
        unsteady.append(first_diff(along(3 + slot, 3, stress)))
        grads = [first_diff(along(3 + slot, dim, stress)) for dim in range(3)]
        convect.append(velocity[0] * grads[0] + velocity[1] * grads[1] + velocity[2] * grads[2])
        summed = jnp.zeros_like(stress)
        for dim in range(3):
            summed = (
                summed
                + stresses[pair_index(first, dim)] * grad_u[second][dim]
                + stresses[pair_index(second, dim)] * grad_u[first][dim]
            )
        produce.append(-summed)
        diffuse.append(
            viscosity
            * (
                second_diff(along(3 + slot, 0, stress), stress)
                + second_diff(along(3 + slot, 1, stress), stress)
                + second_diff(along(3 + slot, 2, stress), stress)
            )
        )
    terms_all = jnp.stack(
        [jnp.stack(unsteady), jnp.stack(convect), jnp.stack(produce), jnp.stack(diffuse)]
    )
    return (
        jnp.transpose(terms_all, (0, 1, 3, 2, 4, 5)),
        jnp.transpose(jnp.stack(velocity), (0, 2, 1, 3, 4)),
    )


def shards(snapshots, phase_index):
    frames = snapshots[0]
    bins_dev = PHASES // lax.axis_size("bin")
    planes = frames.shape[2] // lax.axis_size("rev")
    local_bins = phase_index[0] - lax.axis_index("bin") * bins_dev
    one_hot = (local_bins[None, :] == jnp.arange(bins_dev, dtype=jnp.int32)[:, None]).astype(
        jnp.float32
    )
    summed = lax.psum(binned(frames, one_hot), "rev")
    owned = lax.dynamic_slice_in_dim(summed, lax.axis_index("rev") * planes, planes, 0)
    return finish_terms(owned)


def solution(mesh):
    in_specs = (P("rev", "bin", None, None, None, None), P("rev", "bin"))
    out_specs = (P(None, None, "bin", "rev", None, None), P(None, "bin", "rev", None, None))
    return jax.shard_map(shards, mesh=mesh, in_specs=in_specs, out_specs=out_specs, check_vma=False)
```

profile of v0, /device:TPU:31, one launch (start us, length us, event | category | flops | bytes accessed | tf_op | source)
XLA Modules:
  0.0 230.9 jit_solution(12959993338759327280)
XLA Ops:
  7.2 1.0 broadcast_dynamic-update-slice_fusion
  8.2 3.0 %copy.18 = f32[1,8,3,24,8,128]{5,1,4,3,2,0:T(8,128)S(1)} copy(f32[1,8,3,24,8,128]{5,4,3,2,1,0:T(8,128)} %param.2) | data formatting | bytes 4718592 | tf_op args[0]
  11.2 2.8 %constant_dynamic-update-slice_fusion = f32[8,10,24,8,128]{4,0,3,2,1:T(8,128)} fusion(f32[8,10,24,8,128]{4,0,3,2,1:T(8,128)} %broadcast_dynamic-update-slice_fusion, f32[1,8,3,24,8,128]{5,4,3,2,1,0:T(8,128)S(1)} %copy-done), kind=kLoop, calls=%fused_computation.22 | loop fusion | bytes 4718592
  14.0 0.9 multiply_dynamic-update-slice_fusion.5
  15.0 1.0 multiply_dynamic-update-slice_fusion.4
  16.0 1.0 multiply_dynamic-update-slice_fusion.3
  17.0 0.9 multiply_dynamic-update-slice_fusion.2
  17.9 1.0 multiply_dynamic-update-slice_fusion.1
  18.9 1.0 multiply_dynamic-update-slice_fusion
  20.0 9.0 %convolution_bitcast_fusion = f32[24,10,4,8,128]{4,2,3,0,1:T(4,128)} fusion(f32[8,10,24,8,128]{4,0,3,2,1:T(8,128)} %multiply_dynamic-update-slice_fusion, s32[8]{0:T(128)S(1)} %subtract_bitcast_fusion), kind=kOutput, calls=%fused_computation.2 | convolution fusion | flops 94371872 | bytes 11796512 | tf_op jit(solution)/shard_map/ps,sfxyz->xfpyz/dot_general | solution.py:51
  29.0 113.4 %all-reduce.2.cloned.1.call-done = f32[24,10,4,8,128]{4,2,3,0,1:T(4,128)} async-done(((f32[24,10,4,8,128]{4,2,3,0,1:T(4,128)}), f32[24,10,4,8,128]{4,2,3,0,1:T(4,128)}) %all-reduce.2.cloned.1.call-update) | async-done | bytes 3932176 | tf_op jit(solution)/shard_map/psum | solution.py:133
  142.4 0.8 constant_dynamic-update-slice_fusion.9
  143.2 0.9 constant_dynamic-update-slice_fusion.8
  144.1 0.9 constant_dynamic-update-slice_fusion.7
  144.9 0.9 constant_dynamic-update-slice_fusion.6
  145.8 0.9 constant_dynamic-update-slice_fusion.5
  146.7 0.9 constant_dynamic-update-slice_fusion.4
  147.5 0.9 constant_dynamic-update-slice_fusion.3
  148.4 0.9 constant_dynamic-update-slice_fusion.2
  149.2 0.9 constant_dynamic-update-slice_fusion.1
  150.1 4.4 %collective-permute-start = (f32[3,9,4,8,128]{4,2,3,0,1:T(4,128)S(1)}, f32[3,9,4,8,128]{4,2,3,0,1:T(4,128)S(1)}, u32[]{:S(2)}, u32[]{:S(2)}) collective-permute-start(f32[3,9,4,8,128]{4,2,3,0,1:T(4,128)S(1)} %constant_dynamic-update-slice_fusion.1), channel_id=1, source_target_pairs={{0,64},{64,128},{128,192},{192,256},{256,320},{320,384},{384,448},... | collective-permute-start | bytes 1327112 | tf_op jit(solution)/shard_map/ppermute | solution.py:20
  154.5 1.9 collective-permute-start.1
  158.0 5.1 %collective-permute-done = f32[3,9,4,8,128]{4,2,3,0,1:T(4,128)S(1)} collective-permute-done((f32[3,9,4,8,128]{4,2,3,0,1:T(4,128)S(1)}, f32[3,9,4,8,128]{4,2,3,0,1:T(4,128)S(1)}, u32[]{:S(2)}, u32[]{:S(2)}) %collective-permute-start) | collective-permute-done | bytes 442400 | tf_op jit(solution)/shard_map/ppermute | solution.py:20
  163.2 5.9 %collective-permute-done.1 = f32[3,9,4,8,128]{4,2,3,0,1:T(4,128)S(1)} collective-permute-done((f32[3,9,4,8,128]{4,2,3,0,1:T(4,128)S(1)}, f32[3,9,4,8,128]{4,2,3,0,1:T(4,128)S(1)}, u32[]{:S(2)}, u32[]{:S(2)}) %collective-permute-start.1) | collective-permute-done | bytes 442400 | tf_op jit(solution)/shard_map/ppermute | solution.py:22
  169.1 0.3 pad_maximum_fusion.1
  169.4 0.8 fusion.99
  170.3 6.2 %collective-permute-start.2 = (f32[9,9,3,8,128]{4,3,2,1,0:T(8,128)S(1)}, f32[9,9,3,8,128]{4,3,2,1,0:T(8,128)S(1)}, u32[]{:S(2)}, u32[]{:S(2)}) collective-permute-start(f32[9,9,3,8,128]{4,3,2,1,0:T(8,128)S(1)} %copy.8), channel_id=1, source_target_pairs={{0,1},{1,2},{2,3},{3,4},{4,5},{5,6},{6,7},{7,8},{8,9},{9,10},{10,1... | collective-permute-start | bytes 2985992 | tf_op jit(solution)/shard_map/ppermute | solution.py:20
  176.7 2.1 collective-permute-start.3
  178.8 0.7 copy.13
  179.9 15.0 %collective-permute-done.2 = f32[9,9,3,8,128]{4,3,2,1,0:T(8,128)S(1)} collective-permute-done((f32[9,9,3,8,128]{4,3,2,1,0:T(8,128)S(1)}, f32[9,9,3,8,128]{4,3,2,1,0:T(8,128)S(1)}, u32[]{:S(2)}, u32[]{:S(2)}) %collective-permute-start.2) | collective-permute-done | bytes 995360 | tf_op jit(solution)/shard_map/ppermute | solution.py:20
  194.9 0.4 copy.10
  195.3 13.2 %collective-permute-done.3 = f32[9,9,3,8,128]{4,3,2,1,0:T(8,128)S(1)} collective-permute-done((f32[9,9,3,8,128]{4,3,2,1,0:T(8,128)S(1)}, f32[9,9,3,8,128]{4,3,2,1,0:T(8,128)S(1)}, u32[]{:S(2)}, u32[]{:S(2)}) %collective-permute-start.3) | collective-permute-done | bytes 995360 | tf_op jit(solution)/shard_map/ppermute | solution.py:22
  208.4 0.4 copy.11
  208.8 1.6 pad_maximum_fusion
  210.4 0.7 slice_bitcast_fusion.3
  211.0 1.3 constant_dynamic-update-slice_fusion.27
  213.8 1.3 constant_dynamic-update-slice_fusion.26
  216.0 1.2 constant_dynamic-update-slice_fusion.25
  218.9 0.3 constant_dynamic-update-slice_fusion.20
  219.6 0.3 constant_dynamic-update-slice_fusion.19
  220.3 0.3 constant_dynamic-update-slice_fusion.18
  220.7 0.3 constant_dynamic-update-slice_fusion.30
  221.1 0.3 constant_dynamic-update-slice_fusion.17
  221.4 0.3 constant_dynamic-update-slice_fusion.29
  221.8 0.3 constant_dynamic-update-slice_fusion.16
  222.2 0.3 constant_dynamic-update-slice_fusion.28
  222.5 0.4 maximum_bitcast_fusion
  222.9 1.1 copy.12
  (107 shorter events, 6.6 us)
Async XLA Ops:
  7.2 4.1 %copy-start = (f32[1,8,3,24,8,128]{5,4,3,2,1,0:T(8,128)S(1)}, f32[1,8,3,24,8,128]{5,4,3,2,1,0:T(8,128)}, u32[]{:S(2)}) copy-start(f32[1,8,3,24,8,128]{5,4,3,2,1,0:T(8,128)} %param.2) | copy-start | bytes 7077892
  7.2 135.2 %all-reduce.2.cloned.1.call-start = ((), (), s32[]{:S(2)}) async-start(), calls=%async_computation | async-start | bytes 7864320 | tf_op jit(solution)/shard_map/psum | solution.py:133
  16.0 4.0 %copy-start.1 = (s32[1,8]{1,0:T(1,128)S(1)}, s32[1,8]{1,0:T(1,128)}, u32[]{:S(2)}) copy-start(s32[1,8]{1,0:T(1,128)} %param.3) | copy-start | bytes 100
  150.1 13.1 %collective-permute-start = (f32[3,9,4,8,128]{4,2,3,0,1:T(4,128)S(1)}, f32[3,9,4,8,128]{4,2,3,0,1:T(4,128)S(1)}, u32[]{:S(2)}, u32[]{:S(2)}) collective-permute-start(f32[3,9,4,8,128]{4,2,3,0,1:T(4,128)S(1)} %constant_dynamic-update-slice_fusion.1), channel_id=1, source_target_pairs={{0,64},{64,128},{128,192},{192,256},{256,320},{320,384},{384,448},... | collective-permute-start | bytes 1327112 | tf_op jit(solution)/shard_map/ppermute | solution.py:20
  154.5 14.6 %collective-permute-start.1 = (f32[3,9,4,8,128]{4,2,3,0,1:T(4,128)S(1)}, f32[3,9,4,8,128]{4,2,3,0,1:T(4,128)S(1)}, u32[]{:S(2)}, u32[]{:S(2)}) collective-permute-start(f32[3,9,4,8,128]{4,2,3,0,1:T(4,128)S(1)} %constant_dynamic-update-slice_fusion.1), channel_id=1, source_target_pairs={{64,0},{128,64},{192,128},{256,192},{320,256},{384,320},{448,384},... | collective-permute-start | bytes 1327112 | tf_op jit(solution)/shard_map/ppermute | solution.py:22
  170.3 24.5 %collective-permute-start.2 = (f32[9,9,3,8,128]{4,3,2,1,0:T(8,128)S(1)}, f32[9,9,3,8,128]{4,3,2,1,0:T(8,128)S(1)}, u32[]{:S(2)}, u32[]{:S(2)}) collective-permute-start(f32[9,9,3,8,128]{4,3,2,1,0:T(8,128)S(1)} %copy.8), channel_id=1, source_target_pairs={{0,1},{1,2},{2,3},{3,4},{4,5},{5,6},{6,7},{7,8},{8,9},{9,10},{10,1... | collective-permute-start | bytes 2985992 | tf_op jit(solution)/shard_map/ppermute | solution.py:20
  176.7 31.8 %collective-permute-start.3 = (f32[9,9,3,8,128]{4,3,2,1,0:T(8,128)S(1)}, f32[9,9,3,8,128]{4,3,2,1,0:T(8,128)S(1)}, u32[]{:S(2)}, u32[]{:S(2)}) collective-permute-start(f32[9,9,3,8,128]{4,3,2,1,0:T(8,128)S(1)} %copy.9), channel_id=1, source_target_pairs={{1,0},{2,1},{3,2},{4,3},{5,4},{6,5},{7,6},{8,7},{9,8},{10,9},{11,1... | collective-permute-start | bytes 2985992 | tf_op jit(solution)/shard_map/ppermute | solution.py:22
Sparse Core Ops, SparseCore 0:
  29.1 113.1 all-reduce.1
where the time goes:
time: 232 us; the launch traced here: 231 us
  waiting for transfers between devices  153 us (66%)
  other arithmetic  24.4 us (11%)
  local copies, waits for them, and re-layouts  15.3 us (7%)
  between operations  14.8 us (6%)
  starting transfers between devices  14.7 us (6%)
  matrix products  9 us (4%)
    psum x1, waiting for transfers between devices, shards(): summed = lax.psum(binned(frames, one_hot), 'rev')  113 us
    ppermute x2, waiting for transfers between devices, padded_2(): lax.ppermute(tail, axis, [(i, (i + 1) % count) for i in range(count)])  20.1 us
    unnamed x33, other arithmetic  19.4 us
    ppermute x2, waiting for transfers between devices, padded_2(): lax.ppermute(head, axis, [((i + 1) % count, i) for i in range(count)])  19.1 us
    ppermute x2, starting transfers between devices, padded_2(): lax.ppermute(tail, axis, [(i, (i + 1) % count) for i in range(count)])  10.6 us
    dot_general x1, matrix products, binned(): jnp.einsum('ps,sfxyz->xfpyz', weights, stacked, precision=lax.Precision.H...  9 us
    unnamed x9, local copies, waits for them, and re-layouts  8.58 us
  transfers between devices with their start and end apart: 5, of which 5 were waited for; matrix products, arithmetic and copies ran while one was open for 1% of the time, Pallas kernels for 0%

commit v1 on v0

v1 whole, which is shorter than its diff:
```python
import jax
import jax.numpy as jnp
from jax import lax
from jax.experimental import pallas as pl
from jax.experimental.pallas import tpu as pltpu
from jax.sharding import PartitionSpec as P

PHASES = 256

viscosity = 0.2
stress_pairs = ((0, 0), (0, 1), (0, 2), (1, 1), (1, 2), (2, 2))


def pair_index(first, second):
    low, high = (min(first, second), max(first, second))
    return stress_pairs.index((low, high))


def bin_kernel(bins_ref, counts_ref, x_ref, o_ref, acc_ref):
    snaps, _, planes = x_ref.shape[0], x_ref.shape[1], x_ref.shape[2]
    bins = acc_ref.shape[0]
    acc_ref[...] = jnp.zeros(acc_ref.shape, jnp.float32)

    def body(s, carry):
        b = bins_ref[s]
        for p in range(planes):
            u = x_ref[s, 0, p]
            v = x_ref[s, 1, p]
            w = x_ref[s, 2, p]
            moments = (u, v, w, u * u, u * v, u * w, v * v, v * w, w * w)
            for k in range(9):
                acc_ref[b, k, p] = acc_ref[b, k, p] + moments[k]
        return carry

    lax.fori_loop(0, snaps, body, 0)

    for b in range(bins):
        count = counts_ref[b]
        for p in range(planes):
            vel = [acc_ref[b, c, p] / count for c in range(3)]
            for c in range(3):
                o_ref[c, b, p] = vel[c]
            for slot, (i, j) in enumerate(stress_pairs):
                o_ref[3 + slot, b, p] = acc_ref[b, 3 + slot, p] / count - vel[i] * vel[j]


def binned_fields(frames, local_bins, counts):
    snaps, _, planes, ny, nz = frames.shape
    bins = counts.shape[0]
    return pl.pallas_call(
        bin_kernel,
        out_shape=jax.ShapeDtypeStruct((9, bins, planes, ny, nz), jnp.float32),
        in_specs=[
            pl.BlockSpec(memory_space=pltpu.SMEM),
            pl.BlockSpec(memory_space=pltpu.SMEM),
            pl.BlockSpec(memory_space=pltpu.VMEM),
        ],
        out_specs=pl.BlockSpec(memory_space=pltpu.VMEM),
        scratch_shapes=[pltpu.VMEM((bins, 9, planes, ny, nz), jnp.float32)],
        cost_estimate=pl.CostEstimate(
            flops=snaps * planes * ny * nz * 15,
            bytes_accessed=frames.size * 4 + 9 * bins * planes * ny * nz * 4,
            transcendentals=0,
        ),
    )(local_bins, counts, frames)


def first_diff(shifted):
    return (
        0.75 * (shifted(1) - shifted(-1))
        - 0.15 * (shifted(2) - shifted(-2))
        + (shifted(3) - shifted(-3)) / 60.0
    )


def second_diff(shifted, centre):
    return (
        -49.0 / 18.0 * centre
        + 1.5 * (shifted(1) + shifted(-1))
        - 0.15 * (shifted(2) + shifted(-2))
        + (shifted(3) + shifted(-3)) / 90.0
    )


def ring(axis, step):
    count = lax.axis_size(axis)
    return [(i, (i + step) % count) for i in range(count)]


def finish_terms(fields):
    bins_dev, planes = fields.shape[1], fields.shape[2]
    from_left = lax.ppermute(fields, "rev", ring("rev", 1))
    from_right = lax.ppermute(fields, "rev", ring("rev", -1))
    stress_all = fields[3:]
    from_prev = lax.ppermute(stress_all[:, bins_dev - 3 :], "bin", ring("bin", 1))
    from_next = lax.ppermute(stress_all[:, :3], "bin", ring("bin", -1))
    padded_x = jnp.concatenate([from_left, fields, from_right], axis=2)
    padded_p = jnp.concatenate([from_prev, stress_all, from_next], axis=1)

    velocity = [fields[c] for c in range(3)]
    stresses = [fields[3 + m] for m in range(6)]

    def along(component, dim, centre):
        if dim == 0:
            source = padded_x[component]
            return lambda amount: source[:, planes + amount : 2 * planes + amount]
        if dim == 3:
            source = padded_p[component - 3]
            return lambda amount: source[3 + amount : 3 + amount + bins_dev]
        return lambda amount: jnp.roll(centre, -amount, dim + 1)

    grad_u = [
        [first_diff(along(comp, dim, velocity[comp])) for dim in range(3)] for comp in range(3)
    ]
    unsteady, convect, produce, diffuse = ([], [], [], [])
    for slot, pair in enumerate(stress_pairs):
        first, second = pair
        stress = stresses[slot]
        unsteady.append(first_diff(along(3 + slot, 3, stress)))
        grads = [first_diff(along(3 + slot, dim, stress)) for dim in range(3)]
        convect.append(velocity[0] * grads[0] + velocity[1] * grads[1] + velocity[2] * grads[2])
        summed = jnp.zeros_like(stress)
        for dim in range(3):
            summed = (
                summed
                + stresses[pair_index(first, dim)] * grad_u[second][dim]
                + stresses[pair_index(second, dim)] * grad_u[first][dim]
            )
        produce.append(-summed)
        diffuse.append(
            viscosity
            * (
                second_diff(along(3 + slot, 0, stress), stress)
                + second_diff(along(3 + slot, 1, stress), stress)
                + second_diff(along(3 + slot, 2, stress), stress)
            )
        )
    terms_all = jnp.stack(
        [jnp.stack(unsteady), jnp.stack(convect), jnp.stack(produce), jnp.stack(diffuse)]
    )
    return terms_all, fields[:3]


def shards(snapshots, phase_index):
    bins_dev = PHASES // lax.axis_size("bin")
    frames = lax.all_to_all(snapshots[0], "rev", 2, 0, tiled=True)
    phases = lax.all_gather(phase_index[0], "rev", tiled=True)
    local_bins = jnp.clip(phases - lax.axis_index("bin") * bins_dev, 0, bins_dev - 1)
    one_hot = local_bins[None, :] == jnp.arange(bins_dev, dtype=jnp.int32)[:, None]
    counts = jnp.sum(one_hot.astype(jnp.float32), axis=1)
    fields = binned_fields(frames, local_bins, counts)
    return finish_terms(fields)


def solution(mesh):
    in_specs = (P("rev", "bin", None, None, None, None), P("rev", "bin"))
    out_specs = (P(None, None, "bin", "rev", None, None), P(None, "bin", "rev", None, None))
    return jax.shard_map(shards, mesh=mesh, in_specs=in_specs, out_specs=out_specs, check_vma=False)
```

time: 232 us -> 87.4 us (0.38)
  the two profiles are of different devices: /device:TPU:31 before, /device:TPU:25 now
where the time goes in v1:
time: 87.4 us; the launch traced here: 86.9 us
  blocking collectives  31.4 us (36%)
  starting transfers between devices  21.9 us (25%)
  local copies, waits for them, and re-layouts  12.8 us (15%)
  waiting for transfers between devices  10.4 us (12%)
  other arithmetic  5.02 us (6%)
  Pallas kernels  3.42 us (4%)
  between operations  1.93 us (2%)
    unnamed x1, blocking collectives  31.4 us
    ppermute x1, starting transfers between devices, finish_terms(): lax.ppermute(stress_all[:, bins_dev - 3:], 'bin', ring('bin', 1))  8.77 us
    ppermute x1, waiting for transfers between devices, finish_terms(): from_next = lax.ppermute(stress_all[:, :3], 'bin', ring('bin', -1))  7.73 us
    all_to_all x1, starting transfers between devices, shards(): frames = lax.all_to_all(snapshots[0], 'rev', 2, 0, tiled=True)  5.96 us
    unnamed x9, local copies, waits for them, and re-layouts  5.09 us
    slice x96, local copies, waits for them, and re-layouts, along(): return lambda amount: jnp.roll(centre, -amount, dim + 1)  4.45 us
    pallas_call x1, Pallas kernels, binned_fields(): pl.pallas_call(bin_kernel, out_shape=jax.ShapeDtypeStruct((9, bins, plane...  3.42 us
    ppermute x1, starting transfers between devices, finish_terms(): from_left = lax.ppermute(fields, 'rev', ring('rev', 1))  3.36 us
  transfers between devices with their start and end apart: 5, of which 2 were waited for; matrix products, arithmetic and copies ran while one was open for 6% of the time, Pallas kernels for 0%

profile of v1, /device:TPU:25, one launch (start us, length us, event | category | flops | bytes accessed | tf_op | source)
XLA Modules:
  0.0 86.9 jit_solution(13710663853364190110)
XLA Ops:
  0.6 3.3 %copy.10 = f32[1,8,3,24,8,128]{5,4,2,1,3,0:T(8,128)} copy(f32[1,8,3,24,8,128]{5,4,3,2,1,0:T(8,128)} %param.2) | data formatting | bytes 4718592 | tf_op args[0]
  4.0 6.0 %all-to-all-start = ((f32[8,3,24,8,128]{4,3,1,0,2:T(8,128)}), f32[8,3,24,8,128]{4,3,1,0,2:T(8,128)S(1)}, u32[]{:S(2)}, u32[]{:S(2)}) async-start(f32[8,3,24,8,128]{4,3,1,0,2:T(8,128)} %bitcast.189), calls=%async_computation | async-start | bytes 4718592 | tf_op jit(solution)/shard_map/all_to_all | solution.py:146
  9.9 1.3 %dynamic-slice = u32[1]{0:T(128)} dynamic-slice(u32[512]{0:T(512)} %constant.81, u32[]{:T(128)S(6)} %add.717), dynamic_slice_sizes={1} | dynamic-slice | bytes 12
  11.9 0.1 bitcast_dynamic-update-slice_fusion
  12.0 31.4 %all-reduce = s32[64]{0:T(128)S(1)} all-reduce(s32[64]{0:T(128)S(1)} %bitcast_dynamic-update-slice_fusion), channel_id=2, replica_groups=mesh['rev'=8,'bin'=64] {'rev'}, use_global_device_ids=true, to_apply=%add | all-reduce | flops 64 | bytes 512
  43.4 0.7 convert_reduce_fusion.counts_ref
  44.1 1.5 %copy.8 = f32[8,3,8,3,8,128]{5,4,3,1,0,2:T(8,128)} copy(f32[8,3,8,3,8,128]{5,4,1,0,3,2:T(8,128)S(1)} %bitcast.188) | data formatting | bytes 4718592 | tf_op jit(solution)/shard_map/all_to_all | solution.py:146
  45.6 3.4 %shard_map.41 = f32[9,4,3,8,128]{4,3,2,1,0:T(8,128)} custom-call(s32[64]{0:T(128)} %copy-done.1, f32[4]{0:T(128)} %convert_reduce_fusion.counts_ref, f32[64,3,3,8,128]{4,3,2,1,0:T(8,128)} %bitcast.190), custom_call_target="tpu_custom_call" | custom-call | flops 2949120 | bytes 2801664 | tf_op jit(solution)/shard_map/pallas_call | solution.py:50
  49.1 1.9 %collective-permute-start.3 = (f32[9,4,3,8,128]{4,3,2,1,0:T(8,128)}, f32[9,4,3,8,128]{4,3,2,1,0:T(8,128)S(1)}, u32[]{:S(2)}, u32[]{:S(2)}) collective-permute-start(f32[9,4,3,8,128]{4,3,2,1,0:T(8,128)} %shard_map.41), channel_id=1, source_target_pairs={{0,448},{64,0},{128,64},{192,128},{256,192},{320,256},{384,320},{4... | collective-permute-start | bytes 1327112 | tf_op jit(solution)/shard_map/ppermute | solution.py:93
  51.0 3.4 %collective-permute-start.2 = (f32[9,4,3,8,128]{4,3,2,1,0:T(8,128)}, f32[9,4,3,8,128]{4,3,2,1,0:T(8,128)S(1)}, u32[]{:S(2)}, u32[]{:S(2)}) collective-permute-start(f32[9,4,3,8,128]{4,3,2,1,0:T(8,128)} %shard_map.41), channel_id=1, source_target_pairs={{0,64},{64,128},{128,192},{192,256},{256,320},{320,384},{384,448},... | collective-permute-start | bytes 1327112 | tf_op jit(solution)/shard_map/ppermute | solution.py:92
  54.4 0.9 slice_bitcast_fusion.14
  55.5 0.1 fusion.170
  55.7 0.1 fusion.168
  56.0 0.1 fusion.147
  56.0 0.1 fusion.148
  56.1 0.1 fusion.145
  56.2 0.1 fusion.146
  56.3 0.1 fusion.143
  56.4 0.1 fusion.144
  56.5 0.4 copy-done
  57.0 0.7 slice.1997
  57.6 8.8 %collective-permute-start.1 = (f32[6,3,3,8,128]{4,3,2,1,0:T(8,128)S(1)}, f32[6,3,3,8,128]{4,3,2,1,0:T(8,128)S(1)}, u32[]{:S(2)}, u32[]{:S(2)}) collective-permute-start(f32[6,3,3,8,128]{4,3,2,1,0:T(8,128)S(1)} %get-tuple-element.24), channel_id=1, source_target_pairs={{0,1},{1,2},{2,3},{3,4},{4,5},{5,6},{6,7},{7,8},{8,9},{9,10},{10,1... | collective-permute-start | bytes 663560 | tf_op jit(solution)/shard_map/ppermute | solution.py:95
  66.4 1.9 %collective-permute-start = (f32[6,3,3,8,128]{4,3,2,1,0:T(8,128)S(1)}, f32[6,3,3,8,128]{4,3,2,1,0:T(8,128)S(1)}, u32[]{:S(2)}, u32[]{:S(2)}) collective-permute-start(f32[6,3,3,8,128]{4,3,2,1,0:T(8,128)S(1)} %get-tuple-element.23), channel_id=1, source_target_pairs={{0,63},{1,0},{2,1},{3,2},{4,3},{5,4},{6,5},{7,6},{8,7},{9,8},{10,9... | collective-permute-start | bytes 663560 | tf_op jit(solution)/shard_map/ppermute | solution.py:96
  68.4 2.7 %collective-permute-done.1 = f32[6,3,3,8,128]{4,3,2,1,0:T(8,128)S(1)} collective-permute-done((f32[6,3,3,8,128]{4,3,2,1,0:T(8,128)S(1)}, f32[6,3,3,8,128]{4,3,2,1,0:T(8,128)S(1)}, u32[]{:S(2)}, u32[]{:S(2)}) %collective-permute-start.1) | collective-permute-done | bytes 221216 | tf_op jit(solution)/shard_map/ppermute | solution.py:95
  71.0 7.7 %collective-permute-done = f32[6,3,3,8,128]{4,3,2,1,0:T(8,128)S(1)} collective-permute-done((f32[6,3,3,8,128]{4,3,2,1,0:T(8,128)S(1)}, f32[6,3,3,8,128]{4,3,2,1,0:T(8,128)S(1)}, u32[]{:S(2)}, u32[]{:S(2)}) %collective-permute-start) | collective-permute-done | bytes 221216 | tf_op jit(solution)/shard_map/ppermute | solution.py:96
  78.9 0.1 pad_maximum_fusion
  79.0 0.1 slice_bitcast_fusion
  79.1 0.2 constant_dynamic-update-slice_fusion.17
  79.3 0.2 constant_dynamic-update-slice_fusion.16
  79.6 0.2 constant_dynamic-update-slice_fusion.15
  80.3 0.1 fusion.242
  80.4 0.1 fusion.240
  81.0 0.1 fusion.227
  81.6 0.1 fusion.216
  82.6 0.1 fusion.193
  83.5 0.2 constant_dynamic-update-slice_fusion.23
  83.7 0.2 constant_dynamic-update-slice_fusion.11
  83.9 0.2 constant_dynamic-update-slice_fusion.22
  84.1 0.2 constant_dynamic-update-slice_fusion.10
  84.3 0.2 constant_dynamic-update-slice_fusion.21
  84.5 0.2 constant_dynamic-update-slice_fusion.9
  84.6 0.2 constant_dynamic-update-slice_fusion.20
  84.8 0.2 constant_dynamic-update-slice_fusion.8
  85.0 0.2 constant_dynamic-update-slice_fusion.19
  85.2 0.2 constant_dynamic-update-slice_fusion.7
  85.4 0.2 constant_dynamic-update-slice_fusion.18
  85.6 0.2 constant_dynamic-update-slice_fusion.6
  85.8 1.1 %pad_maximum_fusion.1 = f32[4,6,4,3,8,128]{5,4,3,2,1,0:T(8,128)} fusion(f32[1,6,4,3,8,128]{5,4,3,2,1,0:T(8,128)S(1)} %bitcast.194, f32[1,6,4,3,8,128]{5,4,3,2,1,0:T(8,128)S(1)} %bitcast.192, f32[1,6,4,3,8,128]{5,4,3,2,1,0:T(8,128)S(1)} %bitcast.191, f32[1,6,4,3,8,128]{5,4,3,2,1,0:T(8,128)S(1)} %bitcast.193), kind=kLoop, calls=%fused_computation.70 | loop fusion | flops 884736 | bytes 2359296 | tf_op jit(solution)/shard_map/stack | solution.py:138
  (104 shorter events, 3.6 us)
Async XLA Ops:
  4.0 7.9 %copy-start.2 = (s32[1,8]{1,0:T(1,128)S(1)}, s32[1,8]{1,0:T(1,128)}, u32[]{:S(2)}) copy-start(s32[1,8]{1,0:T(1,128)} %param.3) | copy-start | bytes 100
  4.0 40.1 %all-to-all-start = ((f32[8,3,24,8,128]{4,3,1,0,2:T(8,128)}), f32[8,3,24,8,128]{4,3,1,0,2:T(8,128)S(1)}, u32[]{:S(2)}, u32[]{:S(2)}) async-start(f32[8,3,24,8,128]{4,3,1,0,2:T(8,128)} %bitcast.189), calls=%async_computation | async-start | bytes 4718592 | tf_op jit(solution)/shard_map/all_to_all | solution.py:146
  43.4 2.2 %copy-start.1 = (s32[64]{0:T(128)}, s32[64]{0:T(128)S(1)}, u32[]{:S(2)}) copy-start(s32[64]{0:T(128)S(1)} %subtract_clamp_fusion.bins_ref) | copy-start | bytes 772
  49.1 29.9 %collective-permute-start.3 = (f32[9,4,3,8,128]{4,3,2,1,0:T(8,128)}, f32[9,4,3,8,128]{4,3,2,1,0:T(8,128)S(1)}, u32[]{:S(2)}, u32[]{:S(2)}) collective-permute-start(f32[9,4,3,8,128]{4,3,2,1,0:T(8,128)} %shard_map.41), channel_id=1, source_target_pairs={{0,448},{64,0},{128,64},{192,128},{256,192},{320,256},{384,320},{4... | collective-permute-start | bytes 1327112 | tf_op jit(solution)/shard_map/ppermute | solution.py:93
  51.0 28.0 %collective-permute-start.2 = (f32[9,4,3,8,128]{4,3,2,1,0:T(8,128)}, f32[9,4,3,8,128]{4,3,2,1,0:T(8,128)S(1)}, u32[]{:S(2)}, u32[]{:S(2)}) collective-permute-start(f32[9,4,3,8,128]{4,3,2,1,0:T(8,128)} %shard_map.41), channel_id=1, source_target_pairs={{0,64},{64,128},{128,192},{192,256},{256,320},{320,384},{384,448},... | collective-permute-start | bytes 1327112 | tf_op jit(solution)/shard_map/ppermute | solution.py:92
  55.9 1.0 %copy-start = (f32[9,4,3,8,128]{4,3,2,1,0:T(8,128)S(1)}, f32[9,4,3,8,128]{4,3,2,1,0:T(8,128)}, u32[]{:S(2)}) copy-start(f32[9,4,3,8,128]{4,3,2,1,0:T(8,128)} %shard_map.41) | copy-start | bytes 1327108
  57.6 13.4 %collective-permute-start.1 = (f32[6,3,3,8,128]{4,3,2,1,0:T(8,128)S(1)}, f32[6,3,3,8,128]{4,3,2,1,0:T(8,128)S(1)}, u32[]{:S(2)}, u32[]{:S(2)}) collective-permute-start(f32[6,3,3,8,128]{4,3,2,1,0:T(8,128)S(1)} %get-tuple-element.24), channel_id=1, source_target_pairs={{0,1},{1,2},{2,3},{3,4},{4,5},{5,6},{6,7},{7,8},{8,9},{9,10},{10,1... | collective-permute-start | bytes 663560 | tf_op jit(solution)/shard_map/ppermute | solution.py:95
  66.4 12.3 %collective-permute-start = (f32[6,3,3,8,128]{4,3,2,1,0:T(8,128)S(1)}, f32[6,3,3,8,128]{4,3,2,1,0:T(8,128)S(1)}, u32[]{:S(2)}, u32[]{:S(2)}) collective-permute-start(f32[6,3,3,8,128]{4,3,2,1,0:T(8,128)S(1)} %get-tuple-element.23), channel_id=1, source_target_pairs={{0,63},{1,0},{2,1},{3,2},{4,3},{5,4},{6,5},{7,6},{8,7},{9,8},{10,9... | collective-permute-start | bytes 663560 | tf_op jit(solution)/shard_map/ppermute | solution.py:96

commit v2 on v1

--- a/solution.py
+++ b/solution.py
@@ -17,16 +17,19 @@
 
 
 def bin_kernel(bins_ref, counts_ref, x_ref, o_ref, acc_ref):
-    snaps, _, planes = x_ref.shape[0], x_ref.shape[1], x_ref.shape[2]
-    bins = acc_ref.shape[0]
+    bins, _, planes = acc_ref.shape[0], acc_ref.shape[1], acc_ref.shape[2]
+    per_src = (x_ref.shape[1] - 1) // (3 * planes)
+    snaps = x_ref.shape[0] * per_src
     acc_ref[...] = jnp.zeros(acc_ref.shape, jnp.float32)
 
     def body(s, carry):
         b = bins_ref[s]
+        src = s // per_src
+        base = (s % per_src) * (3 * planes)
         for p in range(planes):
-            u = x_ref[s, 0, p]
-            v = x_ref[s, 1, p]
-            w = x_ref[s, 2, p]
+            u = x_ref[src, base + p]
+            v = x_ref[src, base + planes + p]
+            w = x_ref[src, base + 2 * planes + p]
             moments = (u, v, w, u * u, u * v, u * w, v * v, v * w, w * w)
             for k in range(9):
                 acc_ref[b, k, p] = acc_ref[b, k, p] + moments[k]
@@ -44,9 +47,10 @@
                 o_ref[3 + slot, b, p] = acc_ref[b, 3 + slot, p] / count - vel[i] * vel[j]
 
 
-def binned_fields(frames, local_bins, counts):
-    snaps, _, planes, ny, nz = frames.shape
+def binned_fields(received, local_bins, counts, planes):
+    n_src, rows, ny, nz = received.shape
     bins = counts.shape[0]
+    snaps = local_bins.shape[0]
     return pl.pallas_call(
         bin_kernel,
         out_shape=jax.ShapeDtypeStruct((9, bins, planes, ny, nz), jnp.float32),
@@ -59,10 +63,10 @@
         scratch_shapes=[pltpu.VMEM((bins, 9, planes, ny, nz), jnp.float32)],
         cost_estimate=pl.CostEstimate(
             flops=snaps * planes * ny * nz * 15,
-            bytes_accessed=frames.size * 4 + 9 * bins * planes * ny * nz * 4,
+            bytes_accessed=received.size * 4 + 9 * bins * planes * ny * nz * 4,
             transcendentals=0,
         ),
-    )(local_bins, counts, frames)
+    )(local_bins, counts, received)
 
 
 def first_diff(shifted):
@@ -143,12 +147,21 @@
 
 def shards(snapshots, phase_index):
     bins_dev = PHASES // lax.axis_size("bin")
-    frames = lax.all_to_all(snapshots[0], "rev", 2, 0, tiled=True)
-    phases = lax.all_gather(phase_index[0], "rev", tiled=True)
+    n_rev = lax.axis_size("rev")
+    frames = snapshots[0]
+    snaps, comps, nx, ny, nz = frames.shape
+    planes = nx // n_rev
+    by_dest = frames.reshape(snaps, comps, n_rev, planes, ny, nz)
+    by_dest = jnp.transpose(by_dest, (2, 0, 1, 3, 4, 5)).reshape(n_rev, snaps * comps * planes, ny, nz)
+    phase_row = jnp.pad(phase_index[0].astype(jnp.float32), (0, nz - snaps))
+    phase_slab = jnp.broadcast_to(phase_row[None, None, None, :], (n_rev, 1, ny, nz))
+    payload = jnp.concatenate([by_dest, phase_slab], axis=1)
+    received = lax.all_to_all(payload, "rev", 0, 0, tiled=True)
+    phases = received[:, -1, 0, :snaps].reshape(-1).astype(jnp.int32)
     local_bins = jnp.clip(phases - lax.axis_index("bin") * bins_dev, 0, bins_dev - 1)
     one_hot = local_bins[None, :] == jnp.arange(bins_dev, dtype=jnp.int32)[:, None]
     counts = jnp.sum(one_hot.astype(jnp.float32), axis=1)
-    fields = binned_fields(frames, local_bins, counts)
+    fields = binned_fields(received, local_bins, counts, planes)
     return finish_terms(fields)
 
 

time: 87.4 us -> 82.6 us (0.945)
  the two profiles are of different devices: /device:TPU:25 before, /device:TPU:7 now
where the time goes in v2:
time: 82.6 us; the launch traced here: 82.2 us
  waiting for transfers between devices  37.6 us (46%)
  starting transfers between devices  23.4 us (28%)
  local copies, waits for them, and re-layouts  8.83 us (11%)
  other arithmetic  7.41 us (9%)
  Pallas kernels  3.7 us (4%)
  between operations  1.29 us (2%)
    all_to_all x1, waiting for transfers between devices, shards(): received = lax.all_to_all(payload, 'rev', 0, 0, tiled=True)  27.3 us
    ppermute x1, waiting for transfers between devices, finish_terms(): from_next = lax.ppermute(stress_all[:, :3], 'bin', ring('bin', -1))  9.36 us
    ppermute x1, starting transfers between devices, finish_terms(): lax.ppermute(stress_all[:, bins_dev - 3:], 'bin', ring('bin', 1))  8.03 us
    all_to_all x1, starting transfers between devices, shards(): received = lax.all_to_all(payload, 'rev', 0, 0, tiled=True)  6.02 us
    ppermute x1, starting transfers between devices, finish_terms(): from_left = lax.ppermute(fields, 'rev', ring('rev', 1))  5.47 us
    slice x96, local copies, waits for them, and re-layouts, along(): return lambda amount: jnp.roll(centre, -amount, dim + 1)  4.45 us
    pallas_call x1, Pallas kernels, binned_fields(): pl.pallas_call(bin_kernel, out_shape=jax.ShapeDtypeStruct((9, bins, plane...  3.7 us
    unnamed x20, other arithmetic  2.7 us
  transfers between devices with their start and end apart: 5, of which 3 were waited for; matrix products, arithmetic and copies ran while one was open for 3% of the time, Pallas kernels for 0%

profile of v2, /device:TPU:7, one launch (start us, length us, event | category | flops | bytes accessed | tf_op | source)
XLA Modules:
  0.0 82.2 jit_solution(8686387243350994959)
XLA Ops:
  0.6 0.7 convert_bitcast_fusion
  1.3 1.8 %copy.5 = f32[8,3,8,3,8,128]{5,4,3,1,0,2:T(8,128)S(1)} copy(f32[8,3,8,3,8,128]{5,4,3,2,1,0:T(8,128)} %bitcast.185) | data formatting | bytes 4718592 | tf_op jit(solution)/shard_map/reshape;squeeze | solution.py:154
  3.2 1.5 %pad_maximum_fusion = f32[8,73,8,128]{3,2,1,0:T(8,128)} fusion(f32[8,1,8,128]{3,2,1,0:T(8,128)S(1)} %broadcast_in_dim.2, f32[8,72,8,128]{3,2,1,0:T(8,128)S(1)} %bitcast.184), kind=kLoop, calls=%fused_computation | loop fusion | flops 598016 | bytes 4784128 | tf_op jit(solution)/shard_map/concatenate | solution.py:158
  4.7 6.0 %all-to-all-start = ((f32[8,73,8,128]{3,2,1,0:T(8,128)}), f32[8,73,8,128]{3,2,1,0:T(8,128)S(1)}, u32[]{:S(2)}, u32[]{:S(2)}) async-start(f32[8,73,8,128]{3,2,1,0:T(8,128)} %pad_maximum_fusion), calls=%async_computation | async-start | bytes 4784128 | tf_op jit(solution)/shard_map/all_to_all | solution.py:159
  10.7 27.3 %all-to-all-done.x_ref = f32[8,73,8,128]{3,2,1,0:T(8,128)S(1)} async-done(((f32[8,73,8,128]{3,2,1,0:T(8,128)}), f32[8,73,8,128]{3,2,1,0:T(8,128)S(1)}, u32[]{:S(2)}, u32[]{:S(2)}) %all-to-all-start) | async-done | bytes 2392096 | tf_op jit(solution)/shard_map/all_to_all | solution.py:159
  38.1 0.9 %convert_reduce_fusion.counts_ref = f32[4]{0:T(128)} fusion(s32[64]{0:T(128)S(1)} %min.12.bins_ref), kind=kLoop, calls=%fused_computation.357 | loop fusion | flops 764 | bytes 272 | tf_op jit(solution)/shard_map/reduce_sum | solution.py:163
  39.0 0.4 copy-done.1
  39.4 3.7 %shard_map.41 = f32[9,4,3,8,128]{4,3,2,1,0:T(8,128)} custom-call(s32[64]{0:T(128)} %copy-done.2, f32[4]{0:T(128)} %convert_reduce_fusion.counts_ref, f32[8,73,8,128]{3,2,1,0:T(8,128)} %copy-done.1), custom_call_target="tpu_custom_call" | custom-call | flops 2949120 | bytes 2834432 | tf_op jit(solution)/shard_map/pallas_call | solution.py:54
  43.1 1.9 %collective-permute-start.3 = (f32[9,4,3,8,128]{4,3,2,1,0:T(8,128)}, f32[9,4,3,8,128]{4,3,2,1,0:T(8,128)S(1)}, u32[]{:S(2)}, u32[]{:S(2)}) collective-permute-start(f32[9,4,3,8,128]{4,3,2,1,0:T(8,128)} %shard_map.41), channel_id=1, source_target_pairs={{0,448},{64,0},{128,64},{192,128},{256,192},{320,256},{384,320},{4... | collective-permute-start | bytes 1327112 | tf_op jit(solution)/shard_map/ppermute | solution.py:97
  45.0 5.5 %collective-permute-start.2 = (f32[9,4,3,8,128]{4,3,2,1,0:T(8,128)}, f32[9,4,3,8,128]{4,3,2,1,0:T(8,128)S(1)}, u32[]{:S(2)}, u32[]{:S(2)}) collective-permute-start(f32[9,4,3,8,128]{4,3,2,1,0:T(8,128)} %shard_map.41), channel_id=1, source_target_pairs={{0,64},{64,128},{128,192},{192,256},{256,320},{320,384},{384,448},... | collective-permute-start | bytes 1327112 | tf_op jit(solution)/shard_map/ppermute | solution.py:96
  50.5 0.9 %slice_bitcast_fusion.14 = (f32[4,3,8,128]{3,2,1,0:T(8,128)S(1)}, f32[4,3,8,128]{3,2,1,0:T(8,128)S(1)}, f32[4,3,8,128]{3,2,1,0:T(8,128)S(1)}) fusion(f32[9,4,3,8,128]{4,3,2,1,0:T(8,128)} %shard_map.41), kind=kLoop, calls=%fused_computation.225 | loop fusion | bytes 294912 | tf_op jit(solution)/shard_map/squeeze | solution.py:104
  51.8 0.1 fusion.171
  52.1 0.1 fusion.150
  52.1 0.1 fusion.151
  52.2 0.1 fusion.148
  52.3 0.1 fusion.149
  52.4 0.1 fusion.146
  52.5 0.1 fusion.147
  52.6 0.4 copy-done
  53.1 0.7 slice.2002
  53.7 8.0 %collective-permute-start.1 = (f32[6,3,3,8,128]{4,3,2,1,0:T(8,128)S(1)}, f32[6,3,3,8,128]{4,3,2,1,0:T(8,128)S(1)}, u32[]{:S(2)}, u32[]{:S(2)}) collective-permute-start(f32[6,3,3,8,128]{4,3,2,1,0:T(8,128)S(1)} %get-tuple-element.24), channel_id=1, source_target_pairs={{0,1},{1,2},{2,3},{3,4},{4,5},{5,6},{6,7},{7,8},{8,9},{9,10},{10,1... | collective-permute-start | bytes 663560 | tf_op jit(solution)/shard_map/ppermute | solution.py:99
  61.8 1.9 %collective-permute-start = (f32[6,3,3,8,128]{4,3,2,1,0:T(8,128)S(1)}, f32[6,3,3,8,128]{4,3,2,1,0:T(8,128)S(1)}, u32[]{:S(2)}, u32[]{:S(2)}) collective-permute-start(f32[6,3,3,8,128]{4,3,2,1,0:T(8,128)S(1)} %get-tuple-element.23), channel_id=1, source_target_pairs={{0,63},{1,0},{2,1},{3,2},{4,3},{5,4},{6,5},{7,6},{8,7},{9,8},{10,9... | collective-permute-start | bytes 663560 | tf_op jit(solution)/shard_map/ppermute | solution.py:100
  63.7 1.0 %collective-permute-done.1 = f32[6,3,3,8,128]{4,3,2,1,0:T(8,128)S(1)} collective-permute-done((f32[6,3,3,8,128]{4,3,2,1,0:T(8,128)S(1)}, f32[6,3,3,8,128]{4,3,2,1,0:T(8,128)S(1)}, u32[]{:S(2)}, u32[]{:S(2)}) %collective-permute-start.1) | collective-permute-done | bytes 221216 | tf_op jit(solution)/shard_map/ppermute | solution.py:99
  64.7 9.4 %collective-permute-done = f32[6,3,3,8,128]{4,3,2,1,0:T(8,128)S(1)} collective-permute-done((f32[6,3,3,8,128]{4,3,2,1,0:T(8,128)S(1)}, f32[6,3,3,8,128]{4,3,2,1,0:T(8,128)S(1)}, u32[]{:S(2)}, u32[]{:S(2)}) %collective-permute-start) | collective-permute-done | bytes 221216 | tf_op jit(solution)/shard_map/ppermute | solution.py:100
  74.2 0.1 pad_maximum_fusion.1
  74.3 0.1 slice_bitcast_fusion
  74.4 0.2 constant_dynamic-update-slice_fusion.17
  74.6 0.2 constant_dynamic-update-slice_fusion.16
  74.9 0.2 constant_dynamic-update-slice_fusion.15
  76.1 0.1 fusion.232
  76.8 0.1 fusion.221
  77.3 0.1 fusion.208
  77.4 0.1 fusion.206
  78.0 0.1 fusion.197
  78.1 0.1 fusion.195
  78.8 0.2 constant_dynamic-update-slice_fusion.23
  79.0 0.2 constant_dynamic-update-slice_fusion.11
  79.2 0.2 constant_dynamic-update-slice_fusion.22
  79.4 0.2 constant_dynamic-update-slice_fusion.10
  79.6 0.2 constant_dynamic-update-slice_fusion.21
  79.7 0.2 constant_dynamic-update-slice_fusion.9
  79.9 0.2 constant_dynamic-update-slice_fusion.20
  80.1 0.2 constant_dynamic-update-slice_fusion.8
  80.3 0.2 constant_dynamic-update-slice_fusion.19
  80.5 0.2 constant_dynamic-update-slice_fusion.7
  80.7 0.2 constant_dynamic-update-slice_fusion.18
  80.9 0.2 constant_dynamic-update-slice_fusion.6
  81.1 1.1 %pad_maximum_fusion.2 = f32[4,6,4,3,8,128]{5,4,3,2,1,0:T(8,128)} fusion(f32[1,6,4,3,8,128]{5,4,3,2,1,0:T(8,128)S(1)} %bitcast.189, f32[1,6,4,3,8,128]{5,4,3,2,1,0:T(8,128)S(1)} %bitcast.187, f32[1,6,4,3,8,128]{5,4,3,2,1,0:T(8,128)S(1)} %bitcast.186, f32[1,6,4,3,8,128]{5,4,3,2,1,0:T(8,128)S(1)} %bitcast.188), kind=kLoop, calls=%fused_computation.70 | loop fusion | flops 884736 | bytes 2359296 | tf_op jit(solution)/shard_map/stack | solution.py:142
  (104 shorter events, 3.7 us)
Async XLA Ops:
  4.7 33.3 %all-to-all-start = ((f32[8,73,8,128]{3,2,1,0:T(8,128)}), f32[8,73,8,128]{3,2,1,0:T(8,128)S(1)}, u32[]{:S(2)}, u32[]{:S(2)}) async-start(f32[8,73,8,128]{3,2,1,0:T(8,128)} %pad_maximum_fusion), calls=%async_computation | async-start | bytes 4784128 | tf_op jit(solution)/shard_map/all_to_all | solution.py:159
  38.0 1.4 %copy-start.1 = (f32[8,73,8,128]{3,2,1,0:T(8,128)}, f32[8,73,8,128]{3,2,1,0:T(8,128)S(1)}, u32[]{:S(2)}) copy-start(f32[8,73,8,128]{3,2,1,0:T(8,128)S(1)} %all-to-all-done.x_ref) | copy-start | bytes 7176196
  38.1 1.3 %copy-start.2 = (s32[64]{0:T(128)}, s32[64]{0:T(128)S(1)}, u32[]{:S(2)}) copy-start(s32[64]{0:T(128)S(1)} %min.12.bins_ref) | copy-start | bytes 772
  43.1 31.1 %collective-permute-start.3 = (f32[9,4,3,8,128]{4,3,2,1,0:T(8,128)}, f32[9,4,3,8,128]{4,3,2,1,0:T(8,128)S(1)}, u32[]{:S(2)}, u32[]{:S(2)}) collective-permute-start(f32[9,4,3,8,128]{4,3,2,1,0:T(8,128)} %shard_map.41), channel_id=1, source_target_pairs={{0,448},{64,0},{128,64},{192,128},{256,192},{320,256},{384,320},{4... | collective-permute-start | bytes 1327112 | tf_op jit(solution)/shard_map/ppermute | solution.py:97
  45.0 29.2 %collective-permute-start.2 = (f32[9,4,3,8,128]{4,3,2,1,0:T(8,128)}, f32[9,4,3,8,128]{4,3,2,1,0:T(8,128)S(1)}, u32[]{:S(2)}, u32[]{:S(2)}) collective-permute-start(f32[9,4,3,8,128]{4,3,2,1,0:T(8,128)} %shard_map.41), channel_id=1, source_target_pairs={{0,64},{64,128},{128,192},{192,256},{256,320},{320,384},{384,448},... | collective-permute-start | bytes 1327112 | tf_op jit(solution)/shard_map/ppermute | solution.py:96
  52.0 1.0 %copy-start = (f32[9,4,3,8,128]{4,3,2,1,0:T(8,128)S(1)}, f32[9,4,3,8,128]{4,3,2,1,0:T(8,128)}, u32[]{:S(2)}) copy-start(f32[9,4,3,8,128]{4,3,2,1,0:T(8,128)} %shard_map.41) | copy-start | bytes 1327108
  53.7 10.9 %collective-permute-start.1 = (f32[6,3,3,8,128]{4,3,2,1,0:T(8,128)S(1)}, f32[6,3,3,8,128]{4,3,2,1,0:T(8,128)S(1)}, u32[]{:S(2)}, u32[]{:S(2)}) collective-permute-start(f32[6,3,3,8,128]{4,3,2,1,0:T(8,128)S(1)} %get-tuple-element.24), channel_id=1, source_target_pairs={{0,1},{1,2},{2,3},{3,4},{4,5},{5,6},{6,7},{7,8},{8,9},{9,10},{10,1... | collective-permute-start | bytes 663560 | tf_op jit(solution)/shard_map/ppermute | solution.py:99
  61.8 12.3 %collective-permute-start = (f32[6,3,3,8,128]{4,3,2,1,0:T(8,128)S(1)}, f32[6,3,3,8,128]{4,3,2,1,0:T(8,128)S(1)}, u32[]{:S(2)}, u32[]{:S(2)}) collective-permute-start(f32[6,3,3,8,128]{4,3,2,1,0:T(8,128)S(1)} %get-tuple-element.23), channel_id=1, source_target_pairs={{0,63},{1,0},{2,1},{3,2},{4,3},{5,4},{6,5},{7,6},{8,7},{9,8},{10,9... | collective-permute-start | bytes 663560 | tf_op jit(solution)/shard_map/ppermute | solution.py:100

commit v3 on v2

v3 whole, which is shorter than its diff:
```python
import jax
import jax.numpy as jnp
from jax import lax
from jax.experimental import pallas as pl
from jax.experimental.pallas import tpu as pltpu
from jax.sharding import PartitionSpec as P

PHASES = 256
HALO = 3

viscosity = 0.2
stress_pairs = ((0, 0), (0, 1), (0, 2), (1, 1), (1, 2), (2, 2))


def pair_index(first, second):
    low, high = (min(first, second), max(first, second))
    return stress_pairs.index((low, high))


def bin_kernel(bins_ref, counts_ref, x_ref, o_ref, head_ref, tail_ref, acc_ref):
    bins, _, planes = acc_ref.shape[0], acc_ref.shape[1], acc_ref.shape[2]
    per_src = (x_ref.shape[1] - 1) // (3 * planes)
    snaps = x_ref.shape[0] * per_src
    acc_ref[...] = jnp.zeros(acc_ref.shape, jnp.float32)

    def body(s, carry):
        b = bins_ref[s]
        src = s // per_src
        base = (s % per_src) * (3 * planes)
        for p in range(planes):
            u = x_ref[src, base + p]
            v = x_ref[src, base + planes + p]
            w = x_ref[src, base + 2 * planes + p]
            moments = (u, v, w, u * u, u * v, u * w, v * v, v * w, w * w)
            for k in range(9):
                acc_ref[b, k, p] = acc_ref[b, k, p] + moments[k]
        return carry

    lax.fori_loop(0, snaps, body, 0)

    for b in range(bins):
        count = counts_ref[b]
        for p in range(planes):
            vel = [acc_ref[b, c, p] / count for c in range(3)]
            for c in range(3):
                o_ref[c, b, p] = vel[c]
            for slot, (i, j) in enumerate(stress_pairs):
                stress = acc_ref[b, 3 + slot, p] / count - vel[i] * vel[j]
                o_ref[3 + slot, b, p] = stress
                if b < HALO:
                    head_ref[slot, b, p] = stress
                if b >= bins - HALO:
                    tail_ref[slot, b - (bins - HALO), p] = stress


def binned_fields(received, local_bins, counts, planes):
    n_src, rows, ny, nz = received.shape
    bins = counts.shape[0]
    snaps = local_bins.shape[0]
    return pl.pallas_call(
        bin_kernel,
        out_shape=(
            jax.ShapeDtypeStruct((9, bins, planes, ny, nz), jnp.float32),
            jax.ShapeDtypeStruct((6, HALO, planes, ny, nz), jnp.float32),
            jax.ShapeDtypeStruct((6, HALO, planes, ny, nz), jnp.float32),
        ),
        in_specs=[
            pl.BlockSpec(memory_space=pltpu.SMEM),
            pl.BlockSpec(memory_space=pltpu.SMEM),
            pl.BlockSpec(memory_space=pltpu.VMEM),
        ],
        out_specs=(
            pl.BlockSpec(memory_space=pltpu.VMEM),
            pl.BlockSpec(memory_space=pltpu.VMEM),
            pl.BlockSpec(memory_space=pltpu.VMEM),
        ),
        scratch_shapes=[pltpu.VMEM((bins, 9, planes, ny, nz), jnp.float32)],
        cost_estimate=pl.CostEstimate(
            flops=snaps * planes * ny * nz * 15,
            bytes_accessed=received.size * 4 + 9 * bins * planes * ny * nz * 4,
            transcendentals=0,
        ),
    )(local_bins, counts, received)


def first_diff(shifted):
    return (
        0.75 * (shifted(1) - shifted(-1))
        - 0.15 * (shifted(2) - shifted(-2))
        + (shifted(3) - shifted(-3)) / 60.0
    )


def second_diff(shifted, centre):
    return (
        -49.0 / 18.0 * centre
        + 1.5 * (shifted(1) + shifted(-1))
        - 0.15 * (shifted(2) + shifted(-2))
        + (shifted(3) + shifted(-3)) / 90.0
    )


def ring(axis, step):
    count = lax.axis_size(axis)
    return [(i, (i + step) % count) for i in range(count)]


def stencil_kernel(f_ref, fl_ref, fr_ref, rp_ref, rn_ref, terms_ref, vel_ref):
    _, bins, planes, ny, nz = f_ref.shape

    def at(comp, b, x):
        if 0 <= x < planes:
            if 0 <= b < bins:
                return f_ref[comp, b, x]
            if b < 0:
                return rp_ref[comp - 3, b + HALO, x]
            return rn_ref[comp - 3, b - bins, x]
        if x < 0:
            return fl_ref[comp, b, x + planes]
        return fr_ref[comp, b, x - planes]

    def rolled(value, axis, size):
        table = {k: pltpu.roll(value, (-k) % size, axis) for k in (1, 2, 3, -1, -2, -3)}
        return lambda amount: table[amount]

    for b in range(bins):
        for x in range(planes):
            velocity = [f_ref[c, b, x] for c in range(3)]
            stresses = [f_ref[3 + m, b, x] for m in range(6)]
            for c in range(3):
                vel_ref[c, b, x] = velocity[c]
            grad_u = [
                [
                    first_diff(lambda k, c=c: at(c, b, x + k)),
                    first_diff(rolled(velocity[c], 0, ny)),
                    first_diff(rolled(velocity[c], 1, nz)),
                ]
                for c in range(3)
            ]
            for slot, (first, second) in enumerate(stress_pairs):
                comp = 3 + slot
                stress = stresses[slot]
                along_x = lambda k, comp=comp: at(comp, b, x + k)
                along_y = rolled(stress, 0, ny)
                along_z = rolled(stress, 1, nz)
                terms_ref[0, slot, b, x] = first_diff(lambda k, comp=comp: at(comp, b + k, x))
                grads = [first_diff(along_x), first_diff(along_y), first_diff(along_z)]
                terms_ref[1, slot, b, x] = (
                    velocity[0] * grads[0] + velocity[1] * grads[1] + velocity[2] * grads[2]
                )
                summed = jnp.zeros_like(stress)
                for dim in range(3):
                    summed = (
                        summed
                        + stresses[pair_index(first, dim)] * grad_u[second][dim]
                        + stresses[pair_index(second, dim)] * grad_u[first][dim]
                    )
                terms_ref[2, slot, b, x] = -summed
                terms_ref[3, slot, b, x] = viscosity * (
                    second_diff(along_x, stress)
                    + second_diff(along_y, stress)
                    + second_diff(along_z, stress)
                )


def finish_terms(fields, head, tail):
    _, bins_dev, planes, ny, nz = fields.shape
    from_left = lax.ppermute(fields, "rev", ring("rev", 1))
    from_right = lax.ppermute(fields, "rev", ring("rev", -1))
    from_prev = lax.ppermute(tail, "bin", ring("bin", 1))
    from_next = lax.ppermute(head, "bin", ring("bin", -1))
    cells = bins_dev * planes * ny * nz
    vmem = pl.BlockSpec(memory_space=pltpu.VMEM)
    return pl.pallas_call(
        stencil_kernel,
        out_shape=(
            jax.ShapeDtypeStruct((4, 6, bins_dev, planes, ny, nz), jnp.float32),
            jax.ShapeDtypeStruct((3, bins_dev, planes, ny, nz), jnp.float32),
        ),
        in_specs=[vmem] * 5,
        out_specs=(vmem, vmem),
        cost_estimate=pl.CostEstimate(
            flops=cells * 700,
            bytes_accessed=(3 * fields.size + 2 * head.size + 27 * cells) * 4,
            transcendentals=0,
        ),
    )(fields, from_left, from_right, from_prev, from_next)


def shards(snapshots, phase_index):
    bins_dev = PHASES // lax.axis_size("bin")
    n_rev = lax.axis_size("rev")
    frames = snapshots[0]
    snaps, comps, nx, ny, nz = frames.shape
    planes = nx // n_rev
    by_dest = frames.reshape(snaps, comps, n_rev, planes, ny, nz)
    by_dest = jnp.transpose(by_dest, (2, 0, 1, 3, 4, 5)).reshape(n_rev, snaps * comps * planes, ny, nz)
    phase_row = jnp.pad(phase_index[0].astype(jnp.float32), (0, nz - snaps))
    phase_slab = jnp.broadcast_to(phase_row[None, None, None, :], (n_rev, 1, ny, nz))
    payload = jnp.concatenate([by_dest, phase_slab], axis=1)
    received = lax.all_to_all(payload, "rev", 0, 0, tiled=True)
    phases = received[:, -1, 0, :snaps].reshape(-1).astype(jnp.int32)
    local_bins = jnp.clip(phases - lax.axis_index("bin") * bins_dev, 0, bins_dev - 1)
    one_hot = local_bins[None, :] == jnp.arange(bins_dev, dtype=jnp.int32)[:, None]
    counts = jnp.sum(one_hot.astype(jnp.float32), axis=1)
    fields, head, tail = binned_fields(received, local_bins, counts, planes)
    return finish_terms(fields, head, tail)


def solution(mesh):
    in_specs = (P("rev", "bin", None, None, None, None), P("rev", "bin"))
    out_specs = (P(None, None, "bin", "rev", None, None), P(None, "bin", "rev", None, None))
    return jax.shard_map(shards, mesh=mesh, in_specs=in_specs, out_specs=out_specs, check_vma=False)
```

time: 82.6 us -> 76 us (0.920)
  the two profiles are of different devices: /device:TPU:7 before, /device:TPU:249 now
where the time goes in v3:
time: 76 us; the launch traced here: 75.7 us
  waiting for transfers between devices  39.4 us (52%)
  starting transfers between devices  21.9 us (29%)
  Pallas kernels  7.28 us (10%)
  local copies, waits for them, and re-layouts  4.07 us (5%)
  other arithmetic  2.37 us (3%)
    all_to_all x1, waiting for transfers between devices, shards(): received = lax.all_to_all(payload, 'rev', 0, 0, tiled=True)  29.1 us
    ppermute x1, waiting for transfers between devices, finish_terms(): from_next = lax.ppermute(head, 'bin', ring('bin', -1))  8.99 us
    ppermute x1, starting transfers between devices, finish_terms(): from_prev = lax.ppermute(tail, 'bin', ring('bin', 1))  7.36 us
    all_to_all x1, starting transfers between devices, shards(): received = lax.all_to_all(payload, 'rev', 0, 0, tiled=True)  5.2 us
    ppermute x1, starting transfers between devices, finish_terms(): from_right = lax.ppermute(fields, 'rev', ring('rev', -1))  4.61 us
    pallas_call x1, Pallas kernels, binned_fields(): pl.pallas_call(bin_kernel, out_shape=(jax.ShapeDtypeStruct((9, bins, plan...  3.86 us
    pallas_call x1, Pallas kernels, finish_terms(): pl.pallas_call(stencil_kernel, out_shape=(jax.ShapeDtypeStruct((4, 6, bin...  3.42 us
    ppermute x1, starting transfers between devices, finish_terms(): from_left = lax.ppermute(fields, 'rev', ring('rev', 1))  2.77 us
  transfers between devices with their start and end apart: 5, of which 3 were waited for; matrix products, arithmetic and copies ran while one was open for 0% of the time, Pallas kernels for 0%

profile of v3, /device:TPU:249, one launch (start us, length us, event | category | flops | bytes accessed | tf_op | source)
XLA Modules:
  0.0 75.7 jit_solution(16700168959648798557)
XLA Ops:
  0.6 0.0 copy-start.6
  0.6 1.8 %copy.5 = f32[8,3,8,3,8,128]{5,4,3,1,0,2:T(8,128)S(1)} copy(f32[8,3,8,3,8,128]{5,4,3,2,1,0:T(8,128)} %bitcast.7) | data formatting | bytes 4718592 | tf_op jit(solution)/shard_map/reshape;squeeze | solution.py:196
  2.5 0.0 copy-done.6
  2.5 1.6 %pad_maximum_fusion = f32[8,73,8,128]{3,2,1,0:T(8,128)} fusion(f32[8,1,8,128]{3,2,1,0:T(8,128)S(1)} %broadcast_in_dim.2, f32[8,72,8,128]{3,2,1,0:T(8,128)S(1)} %bitcast.6), kind=kLoop, calls=%fused_computation | loop fusion | flops 598016 | bytes 4784128 | tf_op jit(solution)/shard_map/concatenate | solution.py:200
  4.1 5.2 %all-to-all-start = ((f32[8,73,8,128]{3,2,1,0:T(8,128)}), f32[8,73,8,128]{3,2,1,0:T(8,128)S(1)}, u32[]{:S(2)}, u32[]{:S(2)}) async-start(f32[8,73,8,128]{3,2,1,0:T(8,128)} %pad_maximum_fusion), calls=%async_computation | async-start | bytes 4784128 | tf_op jit(solution)/shard_map/all_to_all | solution.py:201
  9.3 29.1 %all-to-all-done.x_ref = f32[8,73,8,128]{3,2,1,0:T(8,128)S(1)} async-done(((f32[8,73,8,128]{3,2,1,0:T(8,128)}), f32[8,73,8,128]{3,2,1,0:T(8,128)S(1)}, u32[]{:S(2)}, u32[]{:S(2)}) %all-to-all-start) | async-done | bytes 2392096 | tf_op jit(solution)/shard_map/all_to_all | solution.py:201
  38.4 0.0 copy-start
  38.4 0.1 min.12.bins_ref
  38.5 0.0 copy-start.5
  38.5 0.8 %convert_reduce_fusion.counts_ref = f32[4]{0:T(128)} fusion(s32[64]{0:T(128)S(1)} %min.12.bins_ref), kind=kLoop, calls=%fused_computation.5 | loop fusion | flops 764 | bytes 272 | tf_op jit(solution)/shard_map/reduce_sum | solution.py:205
  39.3 0.5 copy-done
  39.8 0.0 copy-done.5
  39.8 3.9 %shard_map.41 = (f32[9,4,3,8,128]{4,3,2,1,0:T(8,128)}, f32[6,3,3,8,128]{4,3,2,1,0:T(8,128)}, f32[6,3,3,8,128]{4,3,2,1,0:T(8,128)}) custom-call(s32[64]{0:T(128)} %copy-done.5, f32[4]{0:T(128)} %convert_reduce_fusion.counts_ref, f32[8,73,8,128]{3,2,1,0:T(8,128)} %copy-done), custom_call_target="tpu_custom_call" | custom-call | flops 2949120 | bytes 2834432 | tf_op jit(solution)/shard_map/pallas_call | solution.py:60
  43.7 2.8 %collective-permute-start = (f32[9,4,3,8,128]{4,3,2,1,0:T(8,128)}, f32[9,4,3,8,128]{4,3,2,1,0:T(8,128)S(1)}, u32[]{:S(2)}, u32[]{:S(2)}) collective-permute-start(f32[9,4,3,8,128]{4,3,2,1,0:T(8,128)} %get-tuple-element.5.f_ref), channel_id=1, source_target_pairs={{0,64},{64,128},{128,192},{192,256},{256,320},{320,384},{384,448},... | collective-permute-start | bytes 1327112 | tf_op jit(solution)/shard_map/ppermute | solution.py:168
  46.4 4.6 %collective-permute-start.1 = (f32[9,4,3,8,128]{4,3,2,1,0:T(8,128)}, f32[9,4,3,8,128]{4,3,2,1,0:T(8,128)S(1)}, u32[]{:S(2)}, u32[]{:S(2)}) collective-permute-start(f32[9,4,3,8,128]{4,3,2,1,0:T(8,128)} %get-tuple-element.5.f_ref), channel_id=1, source_target_pairs={{0,448},{64,0},{128,64},{192,128},{256,192},{320,256},{384,320},{4... | collective-permute-start | bytes 1327112 | tf_op jit(solution)/shard_map/ppermute | solution.py:169
  51.1 7.4 %collective-permute-start.2 = (f32[6,3,3,8,128]{4,3,2,1,0:T(8,128)}, f32[6,3,3,8,128]{4,3,2,1,0:T(8,128)S(1)}, u32[]{:S(2)}, u32[]{:S(2)}) collective-permute-start(f32[6,3,3,8,128]{4,3,2,1,0:T(8,128)} %get-tuple-element.6), channel_id=1, source_target_pairs={{0,1},{1,2},{2,3},{3,4},{4,5},{5,6},{6,7},{7,8},{8,9},{9,10},{10,1... | collective-permute-start | bytes 663560 | tf_op jit(solution)/shard_map/ppermute | solution.py:170
  58.4 1.9 %collective-permute-start.3 = (f32[6,3,3,8,128]{4,3,2,1,0:T(8,128)}, f32[6,3,3,8,128]{4,3,2,1,0:T(8,128)S(1)}, u32[]{:S(2)}, u32[]{:S(2)}) collective-permute-start(f32[6,3,3,8,128]{4,3,2,1,0:T(8,128)} %get-tuple-element.7), channel_id=1, source_target_pairs={{0,63},{1,0},{2,1},{3,2},{4,3},{5,4},{6,5},{7,6},{8,7},{9,8},{10,9... | collective-permute-start | bytes 663560 | tf_op jit(solution)/shard_map/ppermute | solution.py:171
  60.4 1.3 %collective-permute-done.2.rp_ref = f32[6,3,3,8,128]{4,3,2,1,0:T(8,128)S(1)} collective-permute-done((f32[6,3,3,8,128]{4,3,2,1,0:T(8,128)}, f32[6,3,3,8,128]{4,3,2,1,0:T(8,128)S(1)}, u32[]{:S(2)}, u32[]{:S(2)}) %collective-permute-start.2) | collective-permute-done | bytes 221216 | tf_op jit(solution)/shard_map/ppermute | solution.py:170
  61.6 0.0 copy-start.3
  61.6 9.0 %collective-permute-done.3.rn_ref = f32[6,3,3,8,128]{4,3,2,1,0:T(8,128)S(1)} collective-permute-done((f32[6,3,3,8,128]{4,3,2,1,0:T(8,128)}, f32[6,3,3,8,128]{4,3,2,1,0:T(8,128)S(1)}, u32[]{:S(2)}, u32[]{:S(2)}) %collective-permute-start.3) | collective-permute-done | bytes 221216 | tf_op jit(solution)/shard_map/ppermute | solution.py:171
  70.6 0.0 copy-start.4
  70.6 0.0 collective-permute-done.fl_ref
  70.6 0.0 copy-start.1
  70.6 0.0 collective-permute-done.1.fr_ref
  70.6 0.0 copy-done.3
  70.7 0.7 copy-done.4
  71.3 0.1 copy-done.1
  71.5 0.0 copy-start.2
  71.5 0.8 %copy-done.2 = f32[9,4,3,8,128]{4,3,2,1,0:T(8,128)} copy-done((f32[9,4,3,8,128]{4,3,2,1,0:T(8,128)}, f32[9,4,3,8,128]{4,3,2,1,0:T(8,128)S(1)}, u32[]{:S(2)}) %copy-start.2) | copy-done | bytes 442392
  72.3 3.4 %shard_map.42 = (f32[4,6,4,3,8,128]{5,4,3,2,1,0:T(8,128)}, f32[3,4,3,8,128]{4,3,2,1,0:T(8,128)}) custom-call(f32[9,4,3,8,128]{4,3,2,1,0:T(8,128)} %get-tuple-element.5.f_ref, f32[9,4,3,8,128]{4,3,2,1,0:T(8,128)} %copy-done.1, f32[9,4,3,8,128]{4,3,2,1,0:T(8,128)} %copy-done.2, f32[6,3,3,8,128]{4,3,2,1,0:T(8,128)} %copy-done.3, f32[6,3,3,8,128]{4,3,2,1,0:T(8,128)} %copy-done.4), custom_call_target="tpu_custom_call" | custom-call | flops 8601600 | bytes 3096576 | tf_op jit(solution)/shard_map/pallas_call | solution.py:174
  (4 shorter events, 0.0 us)
Async XLA Ops:
  0.6 1.9 %copy-start.6 = (s32[1,8]{1,0:T(1,128)S(1)}, s32[1,8]{1,0:T(1,128)}, u32[]{:S(2)}) copy-start(s32[1,8]{1,0:T(1,128)} %param.3) | copy-start | bytes 100
  4.1 34.3 %all-to-all-start = ((f32[8,73,8,128]{3,2,1,0:T(8,128)}), f32[8,73,8,128]{3,2,1,0:T(8,128)S(1)}, u32[]{:S(2)}, u32[]{:S(2)}) async-start(f32[8,73,8,128]{3,2,1,0:T(8,128)} %pad_maximum_fusion), calls=%async_computation | async-start | bytes 4784128 | tf_op jit(solution)/shard_map/all_to_all | solution.py:201
  38.4 1.4 %copy-start = (f32[8,73,8,128]{3,2,1,0:T(8,128)}, f32[8,73,8,128]{3,2,1,0:T(8,128)S(1)}, u32[]{:S(2)}) copy-start(f32[8,73,8,128]{3,2,1,0:T(8,128)S(1)} %all-to-all-done.x_ref) | copy-start | bytes 7176196
  38.5 1.3 %copy-start.5 = (s32[64]{0:T(128)}, s32[64]{0:T(128)S(1)}, u32[]{:S(2)}) copy-start(s32[64]{0:T(128)S(1)} %min.12.bins_ref) | copy-start | bytes 772
  43.7 27.0 %collective-permute-start = (f32[9,4,3,8,128]{4,3,2,1,0:T(8,128)}, f32[9,4,3,8,128]{4,3,2,1,0:T(8,128)S(1)}, u32[]{:S(2)}, u32[]{:S(2)}) collective-permute-start(f32[9,4,3,8,128]{4,3,2,1,0:T(8,128)} %get-tuple-element.5.f_ref), channel_id=1, source_target_pairs={{0,64},{64,128},{128,192},{192,256},{256,320},{320,384},{384,448},... | collective-permute-start | bytes 1327112 | tf_op jit(solution)/shard_map/ppermute | solution.py:168
  46.4 24.2 %collective-permute-start.1 = (f32[9,4,3,8,128]{4,3,2,1,0:T(8,128)}, f32[9,4,3,8,128]{4,3,2,1,0:T(8,128)S(1)}, u32[]{:S(2)}, u32[]{:S(2)}) collective-permute-start(f32[9,4,3,8,128]{4,3,2,1,0:T(8,128)} %get-tuple-element.5.f_ref), channel_id=1, source_target_pairs={{0,448},{64,0},{128,64},{192,128},{256,192},{320,256},{384,320},{4... | collective-permute-start | bytes 1327112 | tf_op jit(solution)/shard_map/ppermute | solution.py:169
  51.1 10.6 %collective-permute-start.2 = (f32[6,3,3,8,128]{4,3,2,1,0:T(8,128)}, f32[6,3,3,8,128]{4,3,2,1,0:T(8,128)S(1)}, u32[]{:S(2)}, u32[]{:S(2)}) collective-permute-start(f32[6,3,3,8,128]{4,3,2,1,0:T(8,128)} %get-tuple-element.6), channel_id=1, source_target_pairs={{0,1},{1,2},{2,3},{3,4},{4,5},{5,6},{6,7},{7,8},{8,9},{9,10},{10,1... | collective-permute-start | bytes 663560 | tf_op jit(solution)/shard_map/ppermute | solution.py:170
  58.4 12.2 %collective-permute-start.3 = (f32[6,3,3,8,128]{4,3,2,1,0:T(8,128)}, f32[6,3,3,8,128]{4,3,2,1,0:T(8,128)S(1)}, u32[]{:S(2)}, u32[]{:S(2)}) collective-permute-start(f32[6,3,3,8,128]{4,3,2,1,0:T(8,128)} %get-tuple-element.7), channel_id=1, source_target_pairs={{0,63},{1,0},{2,1},{3,2},{4,3},{5,4},{6,5},{7,6},{8,7},{9,8},{10,9... | collective-permute-start | bytes 663560 | tf_op jit(solution)/shard_map/ppermute | solution.py:171
  61.6 9.0 %copy-start.3 = (f32[6,3,3,8,128]{4,3,2,1,0:T(8,128)}, f32[6,3,3,8,128]{4,3,2,1,0:T(8,128)S(1)}, u32[]{:S(2)}) copy-start(f32[6,3,3,8,128]{4,3,2,1,0:T(8,128)S(1)} %collective-permute-done.2.rp_ref) | copy-start | bytes 663556
  70.6 0.7 copy-start.4
  70.6 0.8 %copy-start.1 = (f32[9,4,3,8,128]{4,3,2,1,0:T(8,128)}, f32[9,4,3,8,128]{4,3,2,1,0:T(8,128)S(1)}, u32[]{:S(2)}) copy-start(f32[9,4,3,8,128]{4,3,2,1,0:T(8,128)S(1)} %collective-permute-done.fl_ref) | copy-start | bytes 1327108
  71.5 0.8 %copy-start.2 = (f32[9,4,3,8,128]{4,3,2,1,0:T(8,128)}, f32[9,4,3,8,128]{4,3,2,1,0:T(8,128)S(1)}, u32[]{:S(2)}) copy-start(f32[9,4,3,8,128]{4,3,2,1,0:T(8,128)S(1)} %collective-permute-done.1.fr_ref) | copy-start | bytes 1327108

commit v4 on v3

--- a/solution.py
+++ b/solution.py
@@ -17,35 +17,48 @@
     return stress_pairs.index((low, high))
 
 
-def bin_kernel(bins_ref, counts_ref, x_ref, o_ref, head_ref, tail_ref, acc_ref):
-    bins, _, planes = acc_ref.shape[0], acc_ref.shape[1], acc_ref.shape[2]
+def bin_kernel(bins_ref, x_ref, o_ref, head_ref, tail_ref, order_ref, bounds_ref):
+    bins, planes, ny, nz = o_ref.shape[1], o_ref.shape[2], o_ref.shape[3], o_ref.shape[4]
     per_src = (x_ref.shape[1] - 1) // (3 * planes)
     snaps = x_ref.shape[0] * per_src
-    acc_ref[...] = jnp.zeros(acc_ref.shape, jnp.float32)
-
-    def body(s, carry):
-        b = bins_ref[s]
-        src = s // per_src
-        base = (s % per_src) * (3 * planes)
+
+    position = jnp.int32(0)
+    for b in range(bins):
+        bounds_ref[b] = position
+
+        def place(s, pos, b=b):
+            order_ref[pos] = s
+            return pos + (bins_ref[s] == b).astype(jnp.int32)
+
+        position = lax.fori_loop(0, snaps, place, position)
+    bounds_ref[bins] = position
+
+    for b in range(bins):
+
+        def gather(i, carry):
+            s = order_ref[i]
+            src = s // per_src
+            base = (s % per_src) * (3 * planes)
+            sums, count = carry
+            new = []
+            for p in range(planes):
+                u = x_ref[src, base + p]
+                v = x_ref[src, base + planes + p]
+                w = x_ref[src, base + 2 * planes + p]
+                moments = (u, v, w, u * u, u * v, u * w, v * v, v * w, w * w)
+                new.extend(sums[9 * p + k] + moments[k] for k in range(9))
+            return tuple(new), count + 1.0
+
+        zero = jnp.zeros((ny, nz), jnp.float32)
+        sums, count = lax.fori_loop(
+            bounds_ref[b], bounds_ref[b + 1], gather, (tuple([zero] * (9 * planes)), zero)
+        )
         for p in range(planes):
-            u = x_ref[src, base + p]
-            v = x_ref[src, base + planes + p]
-            w = x_ref[src, base + 2 * planes + p]
-            moments = (u, v, w, u * u, u * v, u * w, v * v, v * w, w * w)
-            for k in range(9):
-                acc_ref[b, k, p] = acc_ref[b, k, p] + moments[k]
-        return carry
-
-    lax.fori_loop(0, snaps, body, 0)
-
-    for b in range(bins):
-        count = counts_ref[b]
-        for p in range(planes):
-            vel = [acc_ref[b, c, p] / count for c in range(3)]
+            vel = [sums[9 * p + c] / count for c in range(3)]
             for c in range(3):
                 o_ref[c, b, p] = vel[c]
             for slot, (i, j) in enumerate(stress_pairs):
-                stress = acc_ref[b, 3 + slot, p] / count - vel[i] * vel[j]
+                stress = sums[9 * p + 3 + slot] / count - vel[i] * vel[j]
                 o_ref[3 + slot, b, p] = stress
                 if b < HALO:
                     head_ref[slot, b, p] = stress
@@ -53,10 +66,10 @@
                     tail_ref[slot, b - (bins - HALO), p] = stress
 
 
-def binned_fields(received, local_bins, counts, planes):
+def binned_fields(received, local_bins, bins, planes):
     n_src, rows, ny, nz = received.shape
-    bins = counts.shape[0]
     snaps = local_bins.shape[0]
+    vmem = pl.BlockSpec(memory_space=pltpu.VMEM)
     return pl.pallas_call(
         bin_kernel,
         out_shape=(
@@ -64,23 +77,15 @@
             jax.ShapeDtypeStruct((6, HALO, planes, ny, nz), jnp.float32),
             jax.ShapeDtypeStruct((6, HALO, planes, ny, nz), jnp.float32),
         ),
-        in_specs=[
-            pl.BlockSpec(memory_space=pltpu.SMEM),
-            pl.BlockSpec(memory_space=pltpu.SMEM),
-            pl.BlockSpec(memory_space=pltpu.VMEM),
-        ],
-        out_specs=(
-            pl.BlockSpec(memory_space=pltpu.VMEM),
-            pl.BlockSpec(memory_space=pltpu.VMEM),
-            pl.BlockSpec(memory_space=pltpu.VMEM),
-        ),
-        scratch_shapes=[pltpu.VMEM((bins, 9, planes, ny, nz), jnp.float32)],
+        in_specs=[pl.BlockSpec(memory_space=pltpu.SMEM), vmem],
+        out_specs=(vmem, vmem, vmem),
+        scratch_shapes=[pltpu.SMEM((snaps + 1,), jnp.int32), pltpu.SMEM((bins + 1,), jnp.int32)],
         cost_estimate=pl.CostEstimate(
             flops=snaps * planes * ny * nz * 15,
             bytes_accessed=received.size * 4 + 9 * bins * planes * ny * nz * 4,
             transcendentals=0,
         ),
-    )(local_bins, counts, received)
+    )(local_bins, received)
 
 
 def first_diff(shifted):
@@ -201,9 +206,7 @@
     received = lax.all_to_all(payload, "rev", 0, 0, tiled=True)
     phases = received[:, -1, 0, :snaps].reshape(-1).astype(jnp.int32)
     local_bins = jnp.clip(phases - lax.axis_index("bin") * bins_dev, 0, bins_dev - 1)
-    one_hot = local_bins[None, :] == jnp.arange(bins_dev, dtype=jnp.int32)[:, None]
-    counts = jnp.sum(one_hot.astype(jnp.float32), axis=1)
-    fields, head, tail = binned_fields(received, local_bins, counts, planes)
+    fields, head, tail = binned_fields(received, local_bins, bins_dev, planes)
     return finish_terms(fields, head, tail)
 
 

time: 76 us -> 78 us (1.026)
  Pallas kernels: 7.28 us -> 9.26 us
    pallas_call x1, Pallas kernels: 3.86 us -> 5.84 us  [binned_fields(): pl.pallas_call(bin_kernel, out_shape=(jax.ShapeDtypeStruct((9, bins, plan...]
    unnamed x14 -> x12, local copies, waits for them, and re-layouts: 2.14 us -> 2.3 us
where the time goes in v4:
time: 78 us; the launch traced here: 77.7 us
  waiting for transfers between devices  39.4 us (51%)
  starting transfers between devices  21.9 us (28%)
  Pallas kernels  9.26 us (12%)
  local copies, waits for them, and re-layouts  4.84 us (6%)
  other arithmetic  1.61 us (2%)
    all_to_all x1, waiting for transfers between devices, shards(): received = lax.all_to_all(payload, 'rev', 0, 0, tiled=True)  29.1 us
    ppermute x1, waiting for transfers between devices, finish_terms(): from_next = lax.ppermute(head, 'bin', ring('bin', -1))  8.99 us
    ppermute x1, starting transfers between devices, finish_terms(): from_prev = lax.ppermute(tail, 'bin', ring('bin', 1))  7.36 us
    pallas_call x1, Pallas kernels, binned_fields(): pl.pallas_call(bin_kernel, out_shape=(jax.ShapeDtypeStruct((9, bins, plan...  5.84 us
    all_to_all x1, starting transfers between devices, shards(): received = lax.all_to_all(payload, 'rev', 0, 0, tiled=True)  5.2 us
    ppermute x1, starting transfers between devices, finish_terms(): from_right = lax.ppermute(fields, 'rev', ring('rev', -1))  4.61 us
    pallas_call x1, Pallas kernels, finish_terms(): pl.pallas_call(stencil_kernel, out_shape=(jax.ShapeDtypeStruct((4, 6, bin...  3.42 us
    ppermute x1, starting transfers between devices, finish_terms(): from_left = lax.ppermute(fields, 'rev', ring('rev', 1))  2.77 us
  transfers between devices with their start and end apart: 5, of which 3 were waited for; matrix products, arithmetic and copies ran while one was open for 0% of the time, Pallas kernels for 0%

profile of v4, /device:TPU:249, one launch (start us, length us, event | category | flops | bytes accessed | tf_op | source)
XLA Modules:
  0.0 77.7 jit_solution(14286029205390979842)
XLA Ops:
  0.6 0.0 copy-start.5
  0.6 1.8 %copy.4 = f32[8,3,8,3,8,128]{5,4,3,1,0,2:T(8,128)S(1)} copy(f32[8,3,8,3,8,128]{5,4,3,2,1,0:T(8,128)} %bitcast.7) | data formatting | bytes 4718592 | tf_op jit(solution)/shard_map/reshape;squeeze | solution.py:201
  2.5 0.0 copy-done.5
  2.5 1.6 %pad_maximum_fusion = f32[8,73,8,128]{3,2,1,0:T(8,128)} fusion(f32[8,1,8,128]{3,2,1,0:T(8,128)S(1)} %broadcast_in_dim.2, f32[8,72,8,128]{3,2,1,0:T(8,128)S(1)} %bitcast.6), kind=kLoop, calls=%fused_computation | loop fusion | flops 598016 | bytes 4784128 | tf_op jit(solution)/shard_map/concatenate | solution.py:205
  4.1 5.2 %all-to-all-start = ((f32[8,73,8,128]{3,2,1,0:T(8,128)}), f32[8,73,8,128]{3,2,1,0:T(8,128)S(1)}, u32[]{:S(2)}, u32[]{:S(2)}) async-start(f32[8,73,8,128]{3,2,1,0:T(8,128)} %pad_maximum_fusion), calls=%async_computation | async-start | bytes 4784128 | tf_op jit(solution)/shard_map/all_to_all | solution.py:206
  9.3 29.1 %all-to-all-done.x_ref = f32[8,73,8,128]{3,2,1,0:T(8,128)S(1)} async-done(((f32[8,73,8,128]{3,2,1,0:T(8,128)}), f32[8,73,8,128]{3,2,1,0:T(8,128)S(1)}, u32[]{:S(2)}, u32[]{:S(2)}) %all-to-all-start) | async-done | bytes 2392096 | tf_op jit(solution)/shard_map/all_to_all | solution.py:206
  38.4 0.0 copy-start
  38.4 0.7 min.12.bins_ref
  39.1 0.7 copy-done
  39.8 5.8 %shard_map.41 = (f32[9,4,3,8,128]{4,3,2,1,0:T(8,128)}, f32[6,3,3,8,128]{4,3,2,1,0:T(8,128)}, f32[6,3,3,8,128]{4,3,2,1,0:T(8,128)}) custom-call(s32[64]{0:T(128)} %min.12.bins_ref, f32[8,73,8,128]{3,2,1,0:T(8,128)} %copy-done), custom_call_target="tpu_custom_call" | custom-call | flops 2949120 | bytes 2834432 | tf_op jit(solution)/shard_map/pallas_call | solution.py:73
  45.7 2.8 %collective-permute-start = (f32[9,4,3,8,128]{4,3,2,1,0:T(8,128)}, f32[9,4,3,8,128]{4,3,2,1,0:T(8,128)S(1)}, u32[]{:S(2)}, u32[]{:S(2)}) collective-permute-start(f32[9,4,3,8,128]{4,3,2,1,0:T(8,128)} %get-tuple-element.5.f_ref), channel_id=1, source_target_pairs={{0,64},{64,128},{128,192},{192,256},{256,320},{320,384},{384,448},... | collective-permute-start | bytes 1327112 | tf_op jit(solution)/shard_map/ppermute | solution.py:173
  48.5 4.6 %collective-permute-start.1 = (f32[9,4,3,8,128]{4,3,2,1,0:T(8,128)}, f32[9,4,3,8,128]{4,3,2,1,0:T(8,128)S(1)}, u32[]{:S(2)}, u32[]{:S(2)}) collective-permute-start(f32[9,4,3,8,128]{4,3,2,1,0:T(8,128)} %get-tuple-element.5.f_ref), channel_id=1, source_target_pairs={{0,448},{64,0},{128,64},{192,128},{256,192},{320,256},{384,320},{4... | collective-permute-start | bytes 1327112 | tf_op jit(solution)/shard_map/ppermute | solution.py:174
  53.1 7.4 %collective-permute-start.2 = (f32[6,3,3,8,128]{4,3,2,1,0:T(8,128)}, f32[6,3,3,8,128]{4,3,2,1,0:T(8,128)S(1)}, u32[]{:S(2)}, u32[]{:S(2)}) collective-permute-start(f32[6,3,3,8,128]{4,3,2,1,0:T(8,128)} %get-tuple-element.6), channel_id=1, source_target_pairs={{0,1},{1,2},{2,3},{3,4},{4,5},{5,6},{6,7},{7,8},{8,9},{9,10},{10,1... | collective-permute-start | bytes 663560 | tf_op jit(solution)/shard_map/ppermute | solution.py:175
  60.4 1.9 %collective-permute-start.3 = (f32[6,3,3,8,128]{4,3,2,1,0:T(8,128)}, f32[6,3,3,8,128]{4,3,2,1,0:T(8,128)S(1)}, u32[]{:S(2)}, u32[]{:S(2)}) collective-permute-start(f32[6,3,3,8,128]{4,3,2,1,0:T(8,128)} %get-tuple-element.7), channel_id=1, source_target_pairs={{0,63},{1,0},{2,1},{3,2},{4,3},{5,4},{6,5},{7,6},{8,7},{9,8},{10,9... | collective-permute-start | bytes 663560 | tf_op jit(solution)/shard_map/ppermute | solution.py:176
  62.4 1.3 %collective-permute-done.2.rp_ref = f32[6,3,3,8,128]{4,3,2,1,0:T(8,128)S(1)} collective-permute-done((f32[6,3,3,8,128]{4,3,2,1,0:T(8,128)}, f32[6,3,3,8,128]{4,3,2,1,0:T(8,128)S(1)}, u32[]{:S(2)}, u32[]{:S(2)}) %collective-permute-start.2) | collective-permute-done | bytes 221216 | tf_op jit(solution)/shard_map/ppermute | solution.py:175
  63.7 0.0 copy-start.3
  63.7 9.0 %collective-permute-done.3.rn_ref = f32[6,3,3,8,128]{4,3,2,1,0:T(8,128)S(1)} collective-permute-done((f32[6,3,3,8,128]{4,3,2,1,0:T(8,128)}, f32[6,3,3,8,128]{4,3,2,1,0:T(8,128)S(1)}, u32[]{:S(2)}, u32[]{:S(2)}) %collective-permute-start.3) | collective-permute-done | bytes 221216 | tf_op jit(solution)/shard_map/ppermute | solution.py:176
  72.6 0.0 copy-start.4
  72.6 0.0 collective-permute-done.fl_ref
  72.6 0.0 copy-start.1
  72.7 0.0 collective-permute-done.1.fr_ref
  72.7 0.0 copy-done.3
  72.7 0.7 copy-done.4
  73.3 0.1 copy-done.1
  73.5 0.0 copy-start.2
  73.5 0.8 copy-done.2
  74.2 3.4 %shard_map.42 = (f32[4,6,4,3,8,128]{5,4,3,2,1,0:T(8,128)}, f32[3,4,3,8,128]{4,3,2,1,0:T(8,128)}) custom-call(f32[9,4,3,8,128]{4,3,2,1,0:T(8,128)} %get-tuple-element.5.f_ref, f32[9,4,3,8,128]{4,3,2,1,0:T(8,128)} %copy-done.1, f32[9,4,3,8,128]{4,3,2,1,0:T(8,128)} %copy-done.2, f32[6,3,3,8,128]{4,3,2,1,0:T(8,128)} %copy-done.3, f32[6,3,3,8,128]{4,3,2,1,0:T(8,128)} %copy-done.4), custom_call_target="tpu_custom_call" | custom-call | flops 8601600 | bytes 3096576 | tf_op jit(solution)/shard_map/pallas_call | solution.py:179
  (4 shorter events, 0.0 us)
Async XLA Ops:
  0.6 1.9 %copy-start.5 = (s32[1,8]{1,0:T(1,128)S(1)}, s32[1,8]{1,0:T(1,128)}, u32[]{:S(2)}) copy-start(s32[1,8]{1,0:T(1,128)} %param.3) | copy-start | bytes 100
  4.1 34.3 %all-to-all-start = ((f32[8,73,8,128]{3,2,1,0:T(8,128)}), f32[8,73,8,128]{3,2,1,0:T(8,128)S(1)}, u32[]{:S(2)}, u32[]{:S(2)}) async-start(f32[8,73,8,128]{3,2,1,0:T(8,128)} %pad_maximum_fusion), calls=%async_computation | async-start | bytes 4784128 | tf_op jit(solution)/shard_map/all_to_all | solution.py:206
  38.4 1.4 %copy-start = (f32[8,73,8,128]{3,2,1,0:T(8,128)}, f32[8,73,8,128]{3,2,1,0:T(8,128)S(1)}, u32[]{:S(2)}) copy-start(f32[8,73,8,128]{3,2,1,0:T(8,128)S(1)} %all-to-all-done.x_ref) | copy-start | bytes 7176196
  45.7 27.0 %collective-permute-start = (f32[9,4,3,8,128]{4,3,2,1,0:T(8,128)}, f32[9,4,3,8,128]{4,3,2,1,0:T(8,128)S(1)}, u32[]{:S(2)}, u32[]{:S(2)}) collective-permute-start(f32[9,4,3,8,128]{4,3,2,1,0:T(8,128)} %get-tuple-element.5.f_ref), channel_id=1, source_target_pairs={{0,64},{64,128},{128,192},{192,256},{256,320},{320,384},{384,448},... | collective-permute-start | bytes 1327112 | tf_op jit(solution)/shard_map/ppermute | solution.py:173
  48.5 24.2 %collective-permute-start.1 = (f32[9,4,3,8,128]{4,3,2,1,0:T(8,128)}, f32[9,4,3,8,128]{4,3,2,1,0:T(8,128)S(1)}, u32[]{:S(2)}, u32[]{:S(2)}) collective-permute-start(f32[9,4,3,8,128]{4,3,2,1,0:T(8,128)} %get-tuple-element.5.f_ref), channel_id=1, source_target_pairs={{0,448},{64,0},{128,64},{192,128},{256,192},{320,256},{384,320},{4... | collective-permute-start | bytes 1327112 | tf_op jit(solution)/shard_map/ppermute | solution.py:174
  53.1 10.6 %collective-permute-start.2 = (f32[6,3,3,8,128]{4,3,2,1,0:T(8,128)}, f32[6,3,3,8,128]{4,3,2,1,0:T(8,128)S(1)}, u32[]{:S(2)}, u32[]{:S(2)}) collective-permute-start(f32[6,3,3,8,128]{4,3,2,1,0:T(8,128)} %get-tuple-element.6), channel_id=1, source_target_pairs={{0,1},{1,2},{2,3},{3,4},{4,5},{5,6},{6,7},{7,8},{8,9},{9,10},{10,1... | collective-permute-start | bytes 663560 | tf_op jit(solution)/shard_map/ppermute | solution.py:175
  60.4 12.2 %collective-permute-start.3 = (f32[6,3,3,8,128]{4,3,2,1,0:T(8,128)}, f32[6,3,3,8,128]{4,3,2,1,0:T(8,128)S(1)}, u32[]{:S(2)}, u32[]{:S(2)}) collective-permute-start(f32[6,3,3,8,128]{4,3,2,1,0:T(8,128)} %get-tuple-element.7), channel_id=1, source_target_pairs={{0,63},{1,0},{2,1},{3,2},{4,3},{5,4},{6,5},{7,6},{8,7},{9,8},{10,9... | collective-permute-start | bytes 663560 | tf_op jit(solution)/shard_map/ppermute | solution.py:176
  63.7 9.0 %copy-start.3 = (f32[6,3,3,8,128]{4,3,2,1,0:T(8,128)}, f32[6,3,3,8,128]{4,3,2,1,0:T(8,128)S(1)}, u32[]{:S(2)}) copy-start(f32[6,3,3,8,128]{4,3,2,1,0:T(8,128)S(1)} %collective-permute-done.2.rp_ref) | copy-start | bytes 663556
  72.6 0.7 copy-start.4
  72.6 0.8 %copy-start.1 = (f32[9,4,3,8,128]{4,3,2,1,0:T(8,128)}, f32[9,4,3,8,128]{4,3,2,1,0:T(8,128)S(1)}, u32[]{:S(2)}) copy-start(f32[9,4,3,8,128]{4,3,2,1,0:T(8,128)S(1)} %collective-permute-done.fl_ref) | copy-start | bytes 1327108
  73.5 0.8 copy-start.2

commit v5 on v3

--- a/solution.py
+++ b/solution.py
@@ -81,6 +81,36 @@
             transcendentals=0,
         ),
     )(local_bins, counts, received)
+
+
+def pack_kernel(phase_ref, x_ref, o_ref):
+    snaps, comps, _, ny, nz = x_ref.shape
+    n_dest, rows = o_ref.shape[0], o_ref.shape[1]
+    planes = (rows - 1) // (snaps * comps)
+    for d in range(n_dest):
+        for s in range(snaps):
+            for c in range(comps):
+                o_ref[d, pl.ds((s * comps + c) * planes, planes)] = x_ref[s, c, pl.ds(d * planes, planes)]
+    lane = lax.broadcasted_iota(jnp.int32, (ny, nz), 1)
+    row = jnp.zeros((ny, nz), jnp.float32)
+    for s in range(snaps):
+        row = jnp.where(lane == s, phase_ref[s], row)
+    for d in range(n_dest):
+        o_ref[d, rows - 1] = row
+
+
+def packed_payload(frames, phases, n_dest):
+    snaps, comps, nx, ny, nz = frames.shape
+    rows = snaps * comps * (nx // n_dest) + 1
+    return pl.pallas_call(
+        pack_kernel,
+        out_shape=jax.ShapeDtypeStruct((n_dest, rows, ny, nz), jnp.float32),
+        in_specs=[pl.BlockSpec(memory_space=pltpu.SMEM), pl.BlockSpec(memory_space=pltpu.VMEM)],
+        out_specs=pl.BlockSpec(memory_space=pltpu.VMEM),
+        cost_estimate=pl.CostEstimate(
+            flops=0, bytes_accessed=2 * frames.size * 4, transcendentals=0
+        ),
+    )(phases, frames)
 
 
 def first_diff(shifted):
@@ -193,11 +223,7 @@
     frames = snapshots[0]
     snaps, comps, nx, ny, nz = frames.shape
     planes = nx // n_rev
-    by_dest = frames.reshape(snaps, comps, n_rev, planes, ny, nz)
-    by_dest = jnp.transpose(by_dest, (2, 0, 1, 3, 4, 5)).reshape(n_rev, snaps * comps * planes, ny, nz)
-    phase_row = jnp.pad(phase_index[0].astype(jnp.float32), (0, nz - snaps))
-    phase_slab = jnp.broadcast_to(phase_row[None, None, None, :], (n_rev, 1, ny, nz))
-    payload = jnp.concatenate([by_dest, phase_slab], axis=1)
+    payload = packed_payload(frames, phase_index[0].astype(jnp.float32), n_rev)
     received = lax.all_to_all(payload, "rev", 0, 0, tiled=True)
     phases = received[:, -1, 0, :snaps].reshape(-1).astype(jnp.int32)
     local_bins = jnp.clip(phases - lax.axis_index("bin") * bins_dev, 0, bins_dev - 1)

time: 76 us -> 77 us (1.013)
  Pallas kernels: 7.28 us -> 10.5 us
  local copies, waits for them, and re-layouts: 4.07 us -> 2.18 us
    pallas_call x0 -> x1, Pallas kernels: none -> 3.25 us  [packed_payload(): pl.pallas_call(pack_kernel, out_shape=jax.ShapeDtypeStruct((n_dest, rows,...]
    another operation x1 -> x0, local copies, waits for them, and re-layouts: 1.84 us -> none  [shards(): by_dest = frames.reshape(snaps, comps, n_rev, planes, ny, nz)]
    concatenate x1 -> x0, other arithmetic: 1.57 us -> none  [shards(): payload = jnp.concatenate([by_dest, phase_slab], axis=1)]
    convert_element_type x1, other arithmetic: 0.01 us -> 1.17 us  [shards(): payload = packed_payload(frames, phase_index[0].astype(jnp.float32), n_rev)]
    unnamed x14 -> x12, local copies, waits for them, and re-layouts: 2.14 us -> 2.1 us
where the time goes in v5:
time: 77 us; the launch traced here: 76.6 us
  waiting for transfers between devices  39.4 us (51%)
  starting transfers between devices  21.9 us (28%)
  Pallas kernels  10.5 us (14%)
  local copies, waits for them, and re-layouts  2.18 us (3%)
  other arithmetic  2 us (3%)
    all_to_all x1, waiting for transfers between devices, shards(): received = lax.all_to_all(payload, 'rev', 0, 0, tiled=True)  29.1 us
    ppermute x1, waiting for transfers between devices, finish_terms(): from_next = lax.ppermute(head, 'bin', ring('bin', -1))  8.99 us
    ppermute x1, starting transfers between devices, finish_terms(): from_prev = lax.ppermute(tail, 'bin', ring('bin', 1))  7.36 us
    all_to_all x1, starting transfers between devices, shards(): received = lax.all_to_all(payload, 'rev', 0, 0, tiled=True)  5.2 us
    ppermute x1, starting transfers between devices, finish_terms(): from_right = lax.ppermute(fields, 'rev', ring('rev', -1))  4.61 us
    pallas_call x1, Pallas kernels, binned_fields(): pl.pallas_call(bin_kernel, out_shape=(jax.ShapeDtypeStruct((9, bins, plan...  3.87 us
    pallas_call x1, Pallas kernels, finish_terms(): pl.pallas_call(stencil_kernel, out_shape=(jax.ShapeDtypeStruct((4, 6, bin...  3.42 us
    pallas_call x1, Pallas kernels, packed_payload(): pl.pallas_call(pack_kernel, out_shape=jax.ShapeDtypeStruct((n_dest, rows,...  3.25 us
  transfers between devices with their start and end apart: 5, of which 3 were waited for; matrix products, arithmetic and copies ran while one was open for 0% of the time, Pallas kernels for 0%

profile of v5, /device:TPU:249, one launch (start us, length us, event | category | flops | bytes accessed | tf_op | source)
XLA Modules:
  0.0 76.6 jit_solution(5856983180055587064)
XLA Ops:
  0.6 1.2 %convert_bitcast_fusion.phase_ref = f32[8]{0:T(128)} fusion(s32[1,8]{1,0:T(1,128)} %param.3), kind=kLoop, calls=%fused_computation.6 | loop fusion | flops 8 | bytes 64 | tf_op jit(solution)/shard_map/convert_element_type | solution.py:226
  1.8 3.2 %shard_map.41 = f32[8,73,8,128]{3,2,1,0:T(8,128)} custom-call(f32[8]{0:T(128)} %convert_bitcast_fusion.phase_ref, f32[8,3,24,8,128]{4,3,2,1,0:T(8,128)} %bitcast.3), custom_call_target="tpu_custom_call" | custom-call | bytes 4718592 | tf_op jit(solution)/shard_map/pallas_call | solution.py:105
  5.0 5.2 %all-to-all-start = ((f32[8,73,8,128]{3,2,1,0:T(8,128)}), f32[8,73,8,128]{3,2,1,0:T(8,128)S(1)}, u32[]{:S(2)}, u32[]{:S(2)}) async-start(f32[8,73,8,128]{3,2,1,0:T(8,128)} %shard_map.41), calls=%async_computation | async-start | bytes 4784128 | tf_op jit(solution)/shard_map/all_to_all | solution.py:227
  10.2 29.1 %all-to-all-done.x_ref = f32[8,73,8,128]{3,2,1,0:T(8,128)S(1)} async-done(((f32[8,73,8,128]{3,2,1,0:T(8,128)}), f32[8,73,8,128]{3,2,1,0:T(8,128)S(1)}, u32[]{:S(2)}, u32[]{:S(2)}) %all-to-all-start) | async-done | bytes 2392096 | tf_op jit(solution)/shard_map/all_to_all | solution.py:227
  39.3 0.0 copy-start
  39.4 0.1 min.12.bins_ref
  39.4 0.0 copy-start.5
  39.4 0.8 %convert_reduce_fusion.counts_ref = f32[4]{0:T(128)} fusion(s32[64]{0:T(128)S(1)} %min.12.bins_ref), kind=kLoop, calls=%fused_computation.4 | loop fusion | flops 764 | bytes 272 | tf_op jit(solution)/shard_map/reduce_sum | solution.py:231
  40.3 0.5 copy-done
  40.8 0.0 copy-done.5
  40.8 3.9 %shard_map.42 = (f32[9,4,3,8,128]{4,3,2,1,0:T(8,128)}, f32[6,3,3,8,128]{4,3,2,1,0:T(8,128)}, f32[6,3,3,8,128]{4,3,2,1,0:T(8,128)}) custom-call(s32[64]{0:T(128)} %copy-done.5, f32[4]{0:T(128)} %convert_reduce_fusion.counts_ref, f32[8,73,8,128]{3,2,1,0:T(8,128)} %copy-done), custom_call_target="tpu_custom_call" | custom-call | flops 2949120 | bytes 2834432 | tf_op jit(solution)/shard_map/pallas_call | solution.py:60
  44.6 2.8 %collective-permute-start = (f32[9,4,3,8,128]{4,3,2,1,0:T(8,128)}, f32[9,4,3,8,128]{4,3,2,1,0:T(8,128)S(1)}, u32[]{:S(2)}, u32[]{:S(2)}) collective-permute-start(f32[9,4,3,8,128]{4,3,2,1,0:T(8,128)} %get-tuple-element.5.f_ref), channel_id=1, source_target_pairs={{0,64},{64,128},{128,192},{192,256},{256,320},{320,384},{384,448},... | collective-permute-start | bytes 1327112 | tf_op jit(solution)/shard_map/ppermute | solution.py:198
  47.4 4.6 %collective-permute-start.1 = (f32[9,4,3,8,128]{4,3,2,1,0:T(8,128)}, f32[9,4,3,8,128]{4,3,2,1,0:T(8,128)S(1)}, u32[]{:S(2)}, u32[]{:S(2)}) collective-permute-start(f32[9,4,3,8,128]{4,3,2,1,0:T(8,128)} %get-tuple-element.5.f_ref), channel_id=1, source_target_pairs={{0,448},{64,0},{128,64},{192,128},{256,192},{320,256},{384,320},{4... | collective-permute-start | bytes 1327112 | tf_op jit(solution)/shard_map/ppermute | solution.py:199
  52.0 7.4 %collective-permute-start.2 = (f32[6,3,3,8,128]{4,3,2,1,0:T(8,128)}, f32[6,3,3,8,128]{4,3,2,1,0:T(8,128)S(1)}, u32[]{:S(2)}, u32[]{:S(2)}) collective-permute-start(f32[6,3,3,8,128]{4,3,2,1,0:T(8,128)} %get-tuple-element.6), channel_id=1, source_target_pairs={{0,1},{1,2},{2,3},{3,4},{4,5},{5,6},{6,7},{7,8},{8,9},{9,10},{10,1... | collective-permute-start | bytes 663560 | tf_op jit(solution)/shard_map/ppermute | solution.py:200
  59.4 1.9 %collective-permute-start.3 = (f32[6,3,3,8,128]{4,3,2,1,0:T(8,128)}, f32[6,3,3,8,128]{4,3,2,1,0:T(8,128)S(1)}, u32[]{:S(2)}, u32[]{:S(2)}) collective-permute-start(f32[6,3,3,8,128]{4,3,2,1,0:T(8,128)} %get-tuple-element.7), channel_id=1, source_target_pairs={{0,63},{1,0},{2,1},{3,2},{4,3},{5,4},{6,5},{7,6},{8,7},{9,8},{10,9... | collective-permute-start | bytes 663560 | tf_op jit(solution)/shard_map/ppermute | solution.py:201
  61.3 1.3 %collective-permute-done.2.rp_ref = f32[6,3,3,8,128]{4,3,2,1,0:T(8,128)S(1)} collective-permute-done((f32[6,3,3,8,128]{4,3,2,1,0:T(8,128)}, f32[6,3,3,8,128]{4,3,2,1,0:T(8,128)S(1)}, u32[]{:S(2)}, u32[]{:S(2)}) %collective-permute-start.2) | collective-permute-done | bytes 221216 | tf_op jit(solution)/shard_map/ppermute | solution.py:200
  62.6 0.0 copy-start.3
  62.6 9.0 %collective-permute-done.3.rn_ref = f32[6,3,3,8,128]{4,3,2,1,0:T(8,128)S(1)} collective-permute-done((f32[6,3,3,8,128]{4,3,2,1,0:T(8,128)}, f32[6,3,3,8,128]{4,3,2,1,0:T(8,128)S(1)}, u32[]{:S(2)}, u32[]{:S(2)}) %collective-permute-start.3) | collective-permute-done | bytes 221216 | tf_op jit(solution)/shard_map/ppermute | solution.py:201
  71.6 0.0 copy-start.4
  71.6 0.0 collective-permute-done.fl_ref
  71.6 0.0 copy-start.1
  71.6 0.0 collective-permute-done.1.fr_ref
  71.6 0.0 copy-done.3
  71.6 0.7 copy-done.4
  72.3 0.2 copy-done.1
  72.4 0.0 copy-start.2
  72.4 0.8 copy-done.2
  73.2 3.4 %shard_map.43 = (f32[4,6,4,3,8,128]{5,4,3,2,1,0:T(8,128)}, f32[3,4,3,8,128]{4,3,2,1,0:T(8,128)}) custom-call(f32[9,4,3,8,128]{4,3,2,1,0:T(8,128)} %get-tuple-element.5.f_ref, f32[9,4,3,8,128]{4,3,2,1,0:T(8,128)} %copy-done.1, f32[9,4,3,8,128]{4,3,2,1,0:T(8,128)} %copy-done.2, f32[6,3,3,8,128]{4,3,2,1,0:T(8,128)} %copy-done.3, f32[6,3,3,8,128]{4,3,2,1,0:T(8,128)} %copy-done.4), custom_call_target="tpu_custom_call" | custom-call | flops 8601600 | bytes 3096576 | tf_op jit(solution)/shard_map/pallas_call | solution.py:204
  (1 shorter events, 0.0 us)
Async XLA Ops:
  5.0 34.3 %all-to-all-start = ((f32[8,73,8,128]{3,2,1,0:T(8,128)}), f32[8,73,8,128]{3,2,1,0:T(8,128)S(1)}, u32[]{:S(2)}, u32[]{:S(2)}) async-start(f32[8,73,8,128]{3,2,1,0:T(8,128)} %shard_map.41), calls=%async_computation | async-start | bytes 4784128 | tf_op jit(solution)/shard_map/all_to_all | solution.py:227
  39.3 1.4 %copy-start = (f32[8,73,8,128]{3,2,1,0:T(8,128)}, f32[8,73,8,128]{3,2,1,0:T(8,128)S(1)}, u32[]{:S(2)}) copy-start(f32[8,73,8,128]{3,2,1,0:T(8,128)S(1)} %all-to-all-done.x_ref) | copy-start | bytes 7176196
  39.4 1.3 %copy-start.5 = (s32[64]{0:T(128)}, s32[64]{0:T(128)S(1)}, u32[]{:S(2)}) copy-start(s32[64]{0:T(128)S(1)} %min.12.bins_ref) | copy-start | bytes 772
  44.6 27.0 %collective-permute-start = (f32[9,4,3,8,128]{4,3,2,1,0:T(8,128)}, f32[9,4,3,8,128]{4,3,2,1,0:T(8,128)S(1)}, u32[]{:S(2)}, u32[]{:S(2)}) collective-permute-start(f32[9,4,3,8,128]{4,3,2,1,0:T(8,128)} %get-tuple-element.5.f_ref), channel_id=1, source_target_pairs={{0,64},{64,128},{128,192},{192,256},{256,320},{320,384},{384,448},... | collective-permute-start | bytes 1327112 | tf_op jit(solution)/shard_map/ppermute | solution.py:198
  47.4 24.2 %collective-permute-start.1 = (f32[9,4,3,8,128]{4,3,2,1,0:T(8,128)}, f32[9,4,3,8,128]{4,3,2,1,0:T(8,128)S(1)}, u32[]{:S(2)}, u32[]{:S(2)}) collective-permute-start(f32[9,4,3,8,128]{4,3,2,1,0:T(8,128)} %get-tuple-element.5.f_ref), channel_id=1, source_target_pairs={{0,448},{64,0},{128,64},{192,128},{256,192},{320,256},{384,320},{4... | collective-permute-start | bytes 1327112 | tf_op jit(solution)/shard_map/ppermute | solution.py:199
  52.0 10.6 %collective-permute-start.2 = (f32[6,3,3,8,128]{4,3,2,1,0:T(8,128)}, f32[6,3,3,8,128]{4,3,2,1,0:T(8,128)S(1)}, u32[]{:S(2)}, u32[]{:S(2)}) collective-permute-start(f32[6,3,3,8,128]{4,3,2,1,0:T(8,128)} %get-tuple-element.6), channel_id=1, source_target_pairs={{0,1},{1,2},{2,3},{3,4},{4,5},{5,6},{6,7},{7,8},{8,9},{9,10},{10,1... | collective-permute-start | bytes 663560 | tf_op jit(solution)/shard_map/ppermute | solution.py:200
  59.4 12.2 %collective-permute-start.3 = (f32[6,3,3,8,128]{4,3,2,1,0:T(8,128)}, f32[6,3,3,8,128]{4,3,2,1,0:T(8,128)S(1)}, u32[]{:S(2)}, u32[]{:S(2)}) collective-permute-start(f32[6,3,3,8,128]{4,3,2,1,0:T(8,128)} %get-tuple-element.7), channel_id=1, source_target_pairs={{0,63},{1,0},{2,1},{3,2},{4,3},{5,4},{6,5},{7,6},{8,7},{9,8},{10,9... | collective-permute-start | bytes 663560 | tf_op jit(solution)/shard_map/ppermute | solution.py:201
  62.6 9.0 %copy-start.3 = (f32[6,3,3,8,128]{4,3,2,1,0:T(8,128)}, f32[6,3,3,8,128]{4,3,2,1,0:T(8,128)S(1)}, u32[]{:S(2)}) copy-start(f32[6,3,3,8,128]{4,3,2,1,0:T(8,128)S(1)} %collective-permute-done.2.rp_ref) | copy-start | bytes 663556
  71.6 0.7 copy-start.4
  71.6 0.8 %copy-start.1 = (f32[9,4,3,8,128]{4,3,2,1,0:T(8,128)}, f32[9,4,3,8,128]{4,3,2,1,0:T(8,128)S(1)}, u32[]{:S(2)}) copy-start(f32[9,4,3,8,128]{4,3,2,1,0:T(8,128)S(1)} %collective-permute-done.fl_ref) | copy-start | bytes 1327108
  72.4 0.8 copy-start.2

commit v6 on v3

--- a/solution.py
+++ b/solution.py
@@ -105,7 +105,38 @@
     return [(i, (i + step) % count) for i in range(count)]
 
 
-def stencil_kernel(f_ref, fl_ref, fr_ref, rp_ref, rn_ref, terms_ref, vel_ref):
+def halo_free_kernel(f_ref, part_ref):
+    _, bins, planes, ny, nz = f_ref.shape
+
+    def rolled(value, axis, size):
+        table = {k: pltpu.roll(value, (-k) % size, axis) for k in (1, 2, 3, -1, -2, -3)}
+        return lambda amount: table[amount]
+
+    for b in range(bins):
+        for x in range(planes):
+            velocity = [f_ref[c, b, x] for c in range(3)]
+            stresses = [f_ref[3 + m, b, x] for m in range(6)]
+            grad_u = [
+                [None, first_diff(rolled(velocity[c], 0, ny)), first_diff(rolled(velocity[c], 1, nz))]
+                for c in range(3)
+            ]
+            for slot, (first, second) in enumerate(stress_pairs):
+                stress = stresses[slot]
+                along_y = rolled(stress, 0, ny)
+                along_z = rolled(stress, 1, nz)
+                part_ref[0, slot, b, x] = velocity[1] * first_diff(along_y) + velocity[2] * first_diff(along_z)
+                summed = None
+                for dim in (1, 2):
+                    pair_sum = (
+                        stresses[pair_index(first, dim)] * grad_u[second][dim]
+                        + stresses[pair_index(second, dim)] * grad_u[first][dim]
+                    )
+                    summed = pair_sum if summed is None else summed + pair_sum
+                part_ref[1, slot, b, x] = summed
+                part_ref[2, slot, b, x] = second_diff(along_y, stress) + second_diff(along_z, stress)
+
+
+def halo_kernel(f_ref, fl_ref, fr_ref, rp_ref, rn_ref, part_ref, terms_ref, vel_ref):
     _, bins, planes, ny, nz = f_ref.shape
 
     def at(comp, b, x):
@@ -119,47 +150,26 @@
             return fl_ref[comp, b, x + planes]
         return fr_ref[comp, b, x - planes]
 
-    def rolled(value, axis, size):
-        table = {k: pltpu.roll(value, (-k) % size, axis) for k in (1, 2, 3, -1, -2, -3)}
-        return lambda amount: table[amount]
-
     for b in range(bins):
         for x in range(planes):
             velocity = [f_ref[c, b, x] for c in range(3)]
             stresses = [f_ref[3 + m, b, x] for m in range(6)]
             for c in range(3):
                 vel_ref[c, b, x] = velocity[c]
-            grad_u = [
-                [
-                    first_diff(lambda k, c=c: at(c, b, x + k)),
-                    first_diff(rolled(velocity[c], 0, ny)),
-                    first_diff(rolled(velocity[c], 1, nz)),
-                ]
-                for c in range(3)
-            ]
+            grad_x = [first_diff(lambda k, c=c: at(c, b, x + k)) for c in range(3)]
             for slot, (first, second) in enumerate(stress_pairs):
                 comp = 3 + slot
                 stress = stresses[slot]
                 along_x = lambda k, comp=comp: at(comp, b, x + k)
-                along_y = rolled(stress, 0, ny)
-                along_z = rolled(stress, 1, nz)
                 terms_ref[0, slot, b, x] = first_diff(lambda k, comp=comp: at(comp, b + k, x))
-                grads = [first_diff(along_x), first_diff(along_y), first_diff(along_z)]
-                terms_ref[1, slot, b, x] = (
-                    velocity[0] * grads[0] + velocity[1] * grads[1] + velocity[2] * grads[2]
+                terms_ref[1, slot, b, x] = velocity[0] * first_diff(along_x) + part_ref[0, slot, b, x]
+                terms_ref[2, slot, b, x] = -(
+                    stresses[pair_index(first, 0)] * grad_x[second]
+                    + stresses[pair_index(second, 0)] * grad_x[first]
+                    + part_ref[1, slot, b, x]
                 )
-                summed = jnp.zeros_like(stress)
-                for dim in range(3):
-                    summed = (
-                        summed
-                        + stresses[pair_index(first, dim)] * grad_u[second][dim]
-                        + stresses[pair_index(second, dim)] * grad_u[first][dim]
-                    )
-                terms_ref[2, slot, b, x] = -summed
                 terms_ref[3, slot, b, x] = viscosity * (
-                    second_diff(along_x, stress)
-                    + second_diff(along_y, stress)
-                    + second_diff(along_z, stress)
+                    second_diff(along_x, stress) + part_ref[2, slot, b, x]
                 )
 
 
@@ -171,20 +181,29 @@
     from_next = lax.ppermute(head, "bin", ring("bin", -1))
     cells = bins_dev * planes * ny * nz
     vmem = pl.BlockSpec(memory_space=pltpu.VMEM)
+    part = pl.pallas_call(
+        halo_free_kernel,
+        out_shape=jax.ShapeDtypeStruct((3, 6, bins_dev, planes, ny, nz), jnp.float32),
+        in_specs=[vmem],
+        out_specs=vmem,
+        cost_estimate=pl.CostEstimate(
+            flops=cells * 400, bytes_accessed=(9 + 18) * cells * 4, transcendentals=0
+        ),
+    )(fields)
     return pl.pallas_call(
-        stencil_kernel,
+        halo_kernel,
         out_shape=(
             jax.ShapeDtypeStruct((4, 6, bins_dev, planes, ny, nz), jnp.float32),
             jax.ShapeDtypeStruct((3, bins_dev, planes, ny, nz), jnp.float32),
         ),
-        in_specs=[vmem] * 5,
+        in_specs=[vmem] * 6,
         out_specs=(vmem, vmem),
         cost_estimate=pl.CostEstimate(
-            flops=cells * 700,
-            bytes_accessed=(3 * fields.size + 2 * head.size + 27 * cells) * 4,
+            flops=cells * 300,
+            bytes_accessed=(3 * fields.size + 2 * head.size + 45 * cells) * 4,
             transcendentals=0,
         ),
-    )(fields, from_left, from_right, from_prev, from_next)
+    )(fields, from_left, from_right, from_prev, from_next, part)
 
 
 def shards(snapshots, phase_index):

time: 76 us -> 75.8 us (level)
  the two profiles are of different devices: /device:TPU:249 before, /device:TPU:233 now
where the time goes in v6:
time: 75.8 us; the launch traced here: 75.4 us
  waiting for transfers between devices  36.7 us (48%)
  starting transfers between devices  21.9 us (29%)
  Pallas kernels  9.7 us (13%)
  local copies, waits for them, and re-layouts  4.07 us (5%)
  other arithmetic  2.37 us (3%)
    all_to_all x1, waiting for transfers between devices, shards(): received = lax.all_to_all(payload, 'rev', 0, 0, tiled=True)  29.1 us
    ppermute x1, waiting for transfers between devices, finish_terms(): from_next = lax.ppermute(head, 'bin', ring('bin', -1))  7.56 us
    ppermute x1, starting transfers between devices, finish_terms(): from_prev = lax.ppermute(tail, 'bin', ring('bin', 1))  7.36 us
    all_to_all x1, starting transfers between devices, shards(): received = lax.all_to_all(payload, 'rev', 0, 0, tiled=True)  5.2 us
    ppermute x1, starting transfers between devices, finish_terms(): from_right = lax.ppermute(fields, 'rev', ring('rev', -1))  4.61 us
    pallas_call x1, Pallas kernels, binned_fields(): pl.pallas_call(bin_kernel, out_shape=(jax.ShapeDtypeStruct((9, bins, plan...  3.86 us
    pallas_call x1, Pallas kernels, finish_terms(): pl.pallas_call(halo_kernel, out_shape=(jax.ShapeDtypeStruct((4, 6, bins_d...  3.13 us
    ppermute x1, starting transfers between devices, finish_terms(): from_left = lax.ppermute(fields, 'rev', ring('rev', 1))  2.77 us
  transfers between devices with their start and end apart: 5, of which 2 were waited for; matrix products, arithmetic and copies ran while one was open for 0% of the time, Pallas kernels for 4%

profile of v6, /device:TPU:233, one launch (start us, length us, event | category | flops | bytes accessed | tf_op | source)
XLA Modules:
  0.0 75.4 jit_solution(4366513407606173978)
XLA Ops:
  0.6 0.0 copy-start.6
  0.6 1.8 %copy.5 = f32[8,3,8,3,8,128]{5,4,3,1,0,2:T(8,128)S(1)} copy(f32[8,3,8,3,8,128]{5,4,3,2,1,0:T(8,128)} %bitcast.7) | data formatting | bytes 4718592 | tf_op jit(solution)/shard_map/reshape;squeeze | solution.py:215
  2.5 0.0 copy-done.6
  2.5 1.6 %pad_maximum_fusion = f32[8,73,8,128]{3,2,1,0:T(8,128)} fusion(f32[8,1,8,128]{3,2,1,0:T(8,128)S(1)} %broadcast_in_dim.2, f32[8,72,8,128]{3,2,1,0:T(8,128)S(1)} %bitcast.6), kind=kLoop, calls=%fused_computation | loop fusion | flops 598016 | bytes 4784128 | tf_op jit(solution)/shard_map/concatenate | solution.py:219
  4.1 5.2 %all-to-all-start = ((f32[8,73,8,128]{3,2,1,0:T(8,128)}), f32[8,73,8,128]{3,2,1,0:T(8,128)S(1)}, u32[]{:S(2)}, u32[]{:S(2)}) async-start(f32[8,73,8,128]{3,2,1,0:T(8,128)} %pad_maximum_fusion), calls=%async_computation | async-start | bytes 4784128 | tf_op jit(solution)/shard_map/all_to_all | solution.py:220
  9.3 29.1 %all-to-all-done.x_ref = f32[8,73,8,128]{3,2,1,0:T(8,128)S(1)} async-done(((f32[8,73,8,128]{3,2,1,0:T(8,128)}), f32[8,73,8,128]{3,2,1,0:T(8,128)S(1)}, u32[]{:S(2)}, u32[]{:S(2)}) %all-to-all-start) | async-done | bytes 2392096 | tf_op jit(solution)/shard_map/all_to_all | solution.py:220
  38.4 0.0 copy-start
  38.4 0.1 min.12.bins_ref
  38.5 0.0 copy-start.5
  38.5 0.8 %convert_reduce_fusion.counts_ref = f32[4]{0:T(128)} fusion(s32[64]{0:T(128)S(1)} %min.12.bins_ref), kind=kLoop, calls=%fused_computation.5 | loop fusion | flops 764 | bytes 272 | tf_op jit(solution)/shard_map/reduce_sum | solution.py:224
  39.3 0.5 copy-done
  39.8 0.0 copy-done.5
  39.8 3.9 %shard_map.41 = (f32[9,4,3,8,128]{4,3,2,1,0:T(8,128)}, f32[6,3,3,8,128]{4,3,2,1,0:T(8,128)}, f32[6,3,3,8,128]{4,3,2,1,0:T(8,128)}) custom-call(s32[64]{0:T(128)} %copy-done.5, f32[4]{0:T(128)} %convert_reduce_fusion.counts_ref, f32[8,73,8,128]{3,2,1,0:T(8,128)} %copy-done), custom_call_target="tpu_custom_call" | custom-call | flops 2949120 | bytes 2834432 | tf_op jit(solution)/shard_map/pallas_call | solution.py:60
  43.7 2.8 %collective-permute-start = (f32[9,4,3,8,128]{4,3,2,1,0:T(8,128)}, f32[9,4,3,8,128]{4,3,2,1,0:T(8,128)S(1)}, u32[]{:S(2)}, u32[]{:S(2)}) collective-permute-start(f32[9,4,3,8,128]{4,3,2,1,0:T(8,128)} %get-tuple-element.5.f_ref), channel_id=1, source_target_pairs={{0,64},{64,128},{128,192},{192,256},{256,320},{320,384},{384,448},... | collective-permute-start | bytes 1327112 | tf_op jit(solution)/shard_map/ppermute | solution.py:178
  46.4 4.6 %collective-permute-start.1 = (f32[9,4,3,8,128]{4,3,2,1,0:T(8,128)}, f32[9,4,3,8,128]{4,3,2,1,0:T(8,128)S(1)}, u32[]{:S(2)}, u32[]{:S(2)}) collective-permute-start(f32[9,4,3,8,128]{4,3,2,1,0:T(8,128)} %get-tuple-element.5.f_ref), channel_id=1, source_target_pairs={{0,448},{64,0},{128,64},{192,128},{256,192},{320,256},{384,320},{4... | collective-permute-start | bytes 1327112 | tf_op jit(solution)/shard_map/ppermute | solution.py:179
  51.1 7.4 %collective-permute-start.2 = (f32[6,3,3,8,128]{4,3,2,1,0:T(8,128)}, f32[6,3,3,8,128]{4,3,2,1,0:T(8,128)S(1)}, u32[]{:S(2)}, u32[]{:S(2)}) collective-permute-start(f32[6,3,3,8,128]{4,3,2,1,0:T(8,128)} %get-tuple-element.6), channel_id=1, source_target_pairs={{0,1},{1,2},{2,3},{3,4},{4,5},{5,6},{6,7},{7,8},{8,9},{9,10},{10,1... | collective-permute-start | bytes 663560 | tf_op jit(solution)/shard_map/ppermute | solution.py:180
  58.4 1.9 %collective-permute-start.3 = (f32[6,3,3,8,128]{4,3,2,1,0:T(8,128)}, f32[6,3,3,8,128]{4,3,2,1,0:T(8,128)S(1)}, u32[]{:S(2)}, u32[]{:S(2)}) collective-permute-start(f32[6,3,3,8,128]{4,3,2,1,0:T(8,128)} %get-tuple-element.7), channel_id=1, source_target_pairs={{0,63},{1,0},{2,1},{3,2},{4,3},{5,4},{6,5},{7,6},{8,7},{9,8},{10,9... | collective-permute-start | bytes 663560 | tf_op jit(solution)/shard_map/ppermute | solution.py:181
  60.4 2.7 %shard_map.42.part_ref = f32[3,6,4,3,8,128]{5,4,3,2,1,0:T(8,128)} custom-call(f32[9,4,3,8,128]{4,3,2,1,0:T(8,128)} %get-tuple-element.5.f_ref), custom_call_target="tpu_custom_call" | custom-call | flops 4915200 | bytes 1327104 | tf_op jit(solution)/shard_map/pallas_call | solution.py:184
  63.1 0.0 collective-permute-done.2.rp_ref
  63.1 0.0 copy-start.3
  63.1 7.6 %collective-permute-done.3.rn_ref = f32[6,3,3,8,128]{4,3,2,1,0:T(8,128)S(1)} collective-permute-done((f32[6,3,3,8,128]{4,3,2,1,0:T(8,128)}, f32[6,3,3,8,128]{4,3,2,1,0:T(8,128)S(1)}, u32[]{:S(2)}, u32[]{:S(2)}) %collective-permute-start.3) | collective-permute-done | bytes 221216 | tf_op jit(solution)/shard_map/ppermute | solution.py:181
  70.6 0.0 copy-start.4
  70.6 0.0 collective-permute-done.fl_ref
  70.6 0.0 copy-start.1
  70.6 0.0 collective-permute-done.1.fr_ref
  70.6 0.0 copy-done.3
  70.7 0.7 copy-done.4
  71.4 0.1 copy-done.1
  71.5 0.0 copy-start.2
  71.5 0.8 %copy-done.2 = f32[9,4,3,8,128]{4,3,2,1,0:T(8,128)} copy-done((f32[9,4,3,8,128]{4,3,2,1,0:T(8,128)}, f32[9,4,3,8,128]{4,3,2,1,0:T(8,128)S(1)}, u32[]{:S(2)}) %copy-start.2) | copy-done | bytes 442392
  72.2 3.1 %shard_map.43 = (f32[4,6,4,3,8,128]{5,4,3,2,1,0:T(8,128)}, f32[3,4,3,8,128]{4,3,2,1,0:T(8,128)}) custom-call(f32[9,4,3,8,128]{4,3,2,1,0:T(8,128)} %get-tuple-element.5.f_ref, f32[9,4,3,8,128]{4,3,2,1,0:T(8,128)} %copy-done.1, f32[9,4,3,8,128]{4,3,2,1,0:T(8,128)} %copy-done.2, f32[6,3,3,8,128]{4,3,2,1,0:T(8,128)} %copy-done.3, ...), custom_call_target="tpu_custom_call" | custom-call | flops 3686400 | bytes 3981312 | tf_op jit(solution)/shard_map/pallas_call | solution.py:193
  (4 shorter events, 0.0 us)
Async XLA Ops:
  0.6 1.9 %copy-start.6 = (s32[1,8]{1,0:T(1,128)S(1)}, s32[1,8]{1,0:T(1,128)}, u32[]{:S(2)}) copy-start(s32[1,8]{1,0:T(1,128)} %param.3) | copy-start | bytes 100
  4.1 34.3 %all-to-all-start = ((f32[8,73,8,128]{3,2,1,0:T(8,128)}), f32[8,73,8,128]{3,2,1,0:T(8,128)S(1)}, u32[]{:S(2)}, u32[]{:S(2)}) async-start(f32[8,73,8,128]{3,2,1,0:T(8,128)} %pad_maximum_fusion), calls=%async_computation | async-start | bytes 4784128 | tf_op jit(solution)/shard_map/all_to_all | solution.py:220
  38.4 1.4 %copy-start = (f32[8,73,8,128]{3,2,1,0:T(8,128)}, f32[8,73,8,128]{3,2,1,0:T(8,128)S(1)}, u32[]{:S(2)}) copy-start(f32[8,73,8,128]{3,2,1,0:T(8,128)S(1)} %all-to-all-done.x_ref) | copy-start | bytes 7176196
  38.5 1.3 %copy-start.5 = (s32[64]{0:T(128)}, s32[64]{0:T(128)S(1)}, u32[]{:S(2)}) copy-start(s32[64]{0:T(128)S(1)} %min.12.bins_ref) | copy-start | bytes 772
  43.7 27.0 %collective-permute-start = (f32[9,4,3,8,128]{4,3,2,1,0:T(8,128)}, f32[9,4,3,8,128]{4,3,2,1,0:T(8,128)S(1)}, u32[]{:S(2)}, u32[]{:S(2)}) collective-permute-start(f32[9,4,3,8,128]{4,3,2,1,0:T(8,128)} %get-tuple-element.5.f_ref), channel_id=1, source_target_pairs={{0,64},{64,128},{128,192},{192,256},{256,320},{320,384},{384,448},... | collective-permute-start | bytes 1327112 | tf_op jit(solution)/shard_map/ppermute | solution.py:178
  46.4 24.2 %collective-permute-start.1 = (f32[9,4,3,8,128]{4,3,2,1,0:T(8,128)}, f32[9,4,3,8,128]{4,3,2,1,0:T(8,128)S(1)}, u32[]{:S(2)}, u32[]{:S(2)}) collective-permute-start(f32[9,4,3,8,128]{4,3,2,1,0:T(8,128)} %get-tuple-element.5.f_ref), channel_id=1, source_target_pairs={{0,448},{64,0},{128,64},{192,128},{256,192},{320,256},{384,320},{4... | collective-permute-start | bytes 1327112 | tf_op jit(solution)/shard_map/ppermute | solution.py:179
  51.1 12.0 %collective-permute-start.2 = (f32[6,3,3,8,128]{4,3,2,1,0:T(8,128)}, f32[6,3,3,8,128]{4,3,2,1,0:T(8,128)S(1)}, u32[]{:S(2)}, u32[]{:S(2)}) collective-permute-start(f32[6,3,3,8,128]{4,3,2,1,0:T(8,128)} %get-tuple-element.6), channel_id=1, source_target_pairs={{0,1},{1,2},{2,3},{3,4},{4,5},{5,6},{6,7},{7,8},{8,9},{9,10},{10,1... | collective-permute-start | bytes 663560 | tf_op jit(solution)/shard_map/ppermute | solution.py:180
  58.4 12.2 %collective-permute-start.3 = (f32[6,3,3,8,128]{4,3,2,1,0:T(8,128)}, f32[6,3,3,8,128]{4,3,2,1,0:T(8,128)S(1)}, u32[]{:S(2)}, u32[]{:S(2)}) collective-permute-start(f32[6,3,3,8,128]{4,3,2,1,0:T(8,128)} %get-tuple-element.7), channel_id=1, source_target_pairs={{0,63},{1,0},{2,1},{3,2},{4,3},{5,4},{6,5},{7,6},{8,7},{9,8},{10,9... | collective-permute-start | bytes 663560 | tf_op jit(solution)/shard_map/ppermute | solution.py:181
  63.1 7.6 %copy-start.3 = (f32[6,3,3,8,128]{4,3,2,1,0:T(8,128)}, f32[6,3,3,8,128]{4,3,2,1,0:T(8,128)S(1)}, u32[]{:S(2)}) copy-start(f32[6,3,3,8,128]{4,3,2,1,0:T(8,128)S(1)} %collective-permute-done.2.rp_ref) | copy-start | bytes 663556
  70.6 0.7 copy-start.4
  70.6 0.8 %copy-start.1 = (f32[9,4,3,8,128]{4,3,2,1,0:T(8,128)}, f32[9,4,3,8,128]{4,3,2,1,0:T(8,128)S(1)}, u32[]{:S(2)}) copy-start(f32[9,4,3,8,128]{4,3,2,1,0:T(8,128)S(1)} %collective-permute-done.fl_ref) | copy-start | bytes 1327108
  71.5 0.8 %copy-start.2 = (f32[9,4,3,8,128]{4,3,2,1,0:T(8,128)}, f32[9,4,3,8,128]{4,3,2,1,0:T(8,128)S(1)}, u32[]{:S(2)}) copy-start(f32[9,4,3,8,128]{4,3,2,1,0:T(8,128)S(1)} %collective-permute-done.1.fr_ref) | copy-start | bytes 1327108

commit v7 on v6

--- a/solution.py
+++ b/solution.py
@@ -17,7 +17,7 @@
     return stress_pairs.index((low, high))
 
 
-def bin_kernel(bins_ref, counts_ref, x_ref, o_ref, head_ref, tail_ref, acc_ref):
+def bin_kernel(bins_ref, x_ref, o_ref, head_ref, tail_ref, acc_ref):
     bins, _, planes = acc_ref.shape[0], acc_ref.shape[1], acc_ref.shape[2]
     per_src = (x_ref.shape[1] - 1) // (3 * planes)
     snaps = x_ref.shape[0] * per_src
@@ -34,12 +34,13 @@
             moments = (u, v, w, u * u, u * v, u * w, v * v, v * w, w * w)
             for k in range(9):
                 acc_ref[b, k, p] = acc_ref[b, k, p] + moments[k]
+        acc_ref[b, 9, 0] = acc_ref[b, 9, 0] + 1.0
         return carry
 
     lax.fori_loop(0, snaps, body, 0)
 
     for b in range(bins):
-        count = counts_ref[b]
+        count = acc_ref[b, 9, 0]
         for p in range(planes):
             vel = [acc_ref[b, c, p] / count for c in range(3)]
             for c in range(3):
@@ -53,9 +54,8 @@
                     tail_ref[slot, b - (bins - HALO), p] = stress
 
 
-def binned_fields(received, local_bins, counts, planes):
+def binned_fields(received, local_bins, bins, planes):
     n_src, rows, ny, nz = received.shape
-    bins = counts.shape[0]
     snaps = local_bins.shape[0]
     return pl.pallas_call(
         bin_kernel,
@@ -64,23 +64,19 @@
             jax.ShapeDtypeStruct((6, HALO, planes, ny, nz), jnp.float32),
             jax.ShapeDtypeStruct((6, HALO, planes, ny, nz), jnp.float32),
         ),
-        in_specs=[
-            pl.BlockSpec(memory_space=pltpu.SMEM),
-            pl.BlockSpec(memory_space=pltpu.SMEM),
-            pl.BlockSpec(memory_space=pltpu.VMEM),
-        ],
+        in_specs=[pl.BlockSpec(memory_space=pltpu.SMEM), pl.BlockSpec(memory_space=pltpu.VMEM)],
         out_specs=(
             pl.BlockSpec(memory_space=pltpu.VMEM),
             pl.BlockSpec(memory_space=pltpu.VMEM),
             pl.BlockSpec(memory_space=pltpu.VMEM),
         ),
-        scratch_shapes=[pltpu.VMEM((bins, 9, planes, ny, nz), jnp.float32)],
+        scratch_shapes=[pltpu.VMEM((bins, 10, planes, ny, nz), jnp.float32)],
         cost_estimate=pl.CostEstimate(
             flops=snaps * planes * ny * nz * 15,
             bytes_accessed=received.size * 4 + 9 * bins * planes * ny * nz * 4,
             transcendentals=0,
         ),
-    )(local_bins, counts, received)
+    )(local_bins, received)
 
 
 def first_diff(shifted):
@@ -220,9 +216,7 @@
     received = lax.all_to_all(payload, "rev", 0, 0, tiled=True)
     phases = received[:, -1, 0, :snaps].reshape(-1).astype(jnp.int32)
     local_bins = jnp.clip(phases - lax.axis_index("bin") * bins_dev, 0, bins_dev - 1)
-    one_hot = local_bins[None, :] == jnp.arange(bins_dev, dtype=jnp.int32)[:, None]
-    counts = jnp.sum(one_hot.astype(jnp.float32), axis=1)
-    fields, head, tail = binned_fields(received, local_bins, counts, planes)
+    fields, head, tail = binned_fields(received, local_bins, bins_dev, planes)
     return finish_terms(fields, head, tail)
 
 

time: 75.8 us -> 75.8 us (level)
  the two profiles are of different devices: /device:TPU:233 before, /device:TPU:249 now
where the time goes in v7:
time: 75.8 us; the launch traced here: 75.4 us
  waiting for transfers between devices  36.7 us (48%)
  starting transfers between devices  21.9 us (29%)
  Pallas kernels  9.7 us (13%)
  local copies, waits for them, and re-layouts  4.87 us (6%)
  other arithmetic  1.61 us (2%)
    all_to_all x1, waiting for transfers between devices, shards(): received = lax.all_to_all(payload, 'rev', 0, 0, tiled=True)  29.1 us
    ppermute x1, waiting for transfers between devices, finish_terms(): from_next = lax.ppermute(head, 'bin', ring('bin', -1))  7.57 us
    ppermute x1, starting transfers between devices, finish_terms(): from_prev = lax.ppermute(tail, 'bin', ring('bin', 1))  7.36 us
    all_to_all x1, starting transfers between devices, shards(): received = lax.all_to_all(payload, 'rev', 0, 0, tiled=True)  5.2 us
    ppermute x1, starting transfers between devices, finish_terms(): from_right = lax.ppermute(fields, 'rev', ring('rev', -1))  4.61 us
    pallas_call x1, Pallas kernels, binned_fields(): pl.pallas_call(bin_kernel, out_shape=(jax.ShapeDtypeStruct((9, bins, plan...  3.87 us
    pallas_call x1, Pallas kernels, finish_terms(): pl.pallas_call(halo_kernel, out_shape=(jax.ShapeDtypeStruct((4, 6, bins_d...  3.13 us
    ppermute x1, starting transfers between devices, finish_terms(): from_left = lax.ppermute(fields, 'rev', ring('rev', 1))  2.77 us
  transfers between devices with their start and end apart: 5, of which 2 were waited for; matrix products, arithmetic and copies ran while one was open for 0% of the time, Pallas kernels for 4%

profile of v7, /device:TPU:249, one launch (start us, length us, event | category | flops | bytes accessed | tf_op | source)
XLA Modules:
  0.0 75.4 jit_solution(1618493795884059409)
XLA Ops:
  0.6 0.0 copy-start.5
  0.6 1.8 %copy.4 = f32[8,3,8,3,8,128]{5,4,3,1,0,2:T(8,128)S(1)} copy(f32[8,3,8,3,8,128]{5,4,3,2,1,0:T(8,128)} %bitcast.7) | data formatting | bytes 4718592 | tf_op jit(solution)/shard_map/reshape;squeeze | solution.py:211
  2.5 0.0 copy-done.5
  2.5 1.6 %pad_maximum_fusion = f32[8,73,8,128]{3,2,1,0:T(8,128)} fusion(f32[8,1,8,128]{3,2,1,0:T(8,128)S(1)} %broadcast_in_dim.2, f32[8,72,8,128]{3,2,1,0:T(8,128)S(1)} %bitcast.6), kind=kLoop, calls=%fused_computation | loop fusion | flops 598016 | bytes 4784128 | tf_op jit(solution)/shard_map/concatenate | solution.py:215
  4.1 5.2 %all-to-all-start = ((f32[8,73,8,128]{3,2,1,0:T(8,128)}), f32[8,73,8,128]{3,2,1,0:T(8,128)S(1)}, u32[]{:S(2)}, u32[]{:S(2)}) async-start(f32[8,73,8,128]{3,2,1,0:T(8,128)} %pad_maximum_fusion), calls=%async_computation | async-start | bytes 4784128 | tf_op jit(solution)/shard_map/all_to_all | solution.py:216
  9.3 29.1 %all-to-all-done.x_ref = f32[8,73,8,128]{3,2,1,0:T(8,128)S(1)} async-done(((f32[8,73,8,128]{3,2,1,0:T(8,128)}), f32[8,73,8,128]{3,2,1,0:T(8,128)S(1)}, u32[]{:S(2)}, u32[]{:S(2)}) %all-to-all-start) | async-done | bytes 2392096 | tf_op jit(solution)/shard_map/all_to_all | solution.py:216
  38.4 0.0 copy-start
  38.4 0.7 min.12.bins_ref
  39.1 0.7 copy-done
  39.8 3.9 %shard_map.41 = (f32[9,4,3,8,128]{4,3,2,1,0:T(8,128)}, f32[6,3,3,8,128]{4,3,2,1,0:T(8,128)}, f32[6,3,3,8,128]{4,3,2,1,0:T(8,128)}) custom-call(s32[64]{0:T(128)} %min.12.bins_ref, f32[8,73,8,128]{3,2,1,0:T(8,128)} %copy-done), custom_call_target="tpu_custom_call" | custom-call | flops 2949120 | bytes 2834432 | tf_op jit(solution)/shard_map/pallas_call | solution.py:60
  43.7 2.8 %collective-permute-start = (f32[9,4,3,8,128]{4,3,2,1,0:T(8,128)}, f32[9,4,3,8,128]{4,3,2,1,0:T(8,128)S(1)}, u32[]{:S(2)}, u32[]{:S(2)}) collective-permute-start(f32[9,4,3,8,128]{4,3,2,1,0:T(8,128)} %get-tuple-element.5.f_ref), channel_id=1, source_target_pairs={{0,64},{64,128},{128,192},{192,256},{256,320},{320,384},{384,448},... | collective-permute-start | bytes 1327112 | tf_op jit(solution)/shard_map/ppermute | solution.py:174
  46.5 4.6 %collective-permute-start.1 = (f32[9,4,3,8,128]{4,3,2,1,0:T(8,128)}, f32[9,4,3,8,128]{4,3,2,1,0:T(8,128)S(1)}, u32[]{:S(2)}, u32[]{:S(2)}) collective-permute-start(f32[9,4,3,8,128]{4,3,2,1,0:T(8,128)} %get-tuple-element.5.f_ref), channel_id=1, source_target_pairs={{0,448},{64,0},{128,64},{192,128},{256,192},{320,256},{384,320},{4... | collective-permute-start | bytes 1327112 | tf_op jit(solution)/shard_map/ppermute | solution.py:175
  51.1 7.4 %collective-permute-start.2 = (f32[6,3,3,8,128]{4,3,2,1,0:T(8,128)}, f32[6,3,3,8,128]{4,3,2,1,0:T(8,128)S(1)}, u32[]{:S(2)}, u32[]{:S(2)}) collective-permute-start(f32[6,3,3,8,128]{4,3,2,1,0:T(8,128)} %get-tuple-element.6), channel_id=1, source_target_pairs={{0,1},{1,2},{2,3},{3,4},{4,5},{5,6},{6,7},{7,8},{8,9},{9,10},{10,1... | collective-permute-start | bytes 663560 | tf_op jit(solution)/shard_map/ppermute | solution.py:176
  58.5 1.9 %collective-permute-start.3 = (f32[6,3,3,8,128]{4,3,2,1,0:T(8,128)}, f32[6,3,3,8,128]{4,3,2,1,0:T(8,128)S(1)}, u32[]{:S(2)}, u32[]{:S(2)}) collective-permute-start(f32[6,3,3,8,128]{4,3,2,1,0:T(8,128)} %get-tuple-element.7), channel_id=1, source_target_pairs={{0,63},{1,0},{2,1},{3,2},{4,3},{5,4},{6,5},{7,6},{8,7},{9,8},{10,9... | collective-permute-start | bytes 663560 | tf_op jit(solution)/shard_map/ppermute | solution.py:177
  60.4 2.7 %shard_map.42.part_ref = f32[3,6,4,3,8,128]{5,4,3,2,1,0:T(8,128)} custom-call(f32[9,4,3,8,128]{4,3,2,1,0:T(8,128)} %get-tuple-element.5.f_ref), custom_call_target="tpu_custom_call" | custom-call | flops 4915200 | bytes 1327104 | tf_op jit(solution)/shard_map/pallas_call | solution.py:180
  63.1 0.0 collective-permute-done.2.rp_ref
  63.1 0.0 copy-start.3
  63.1 7.6 %collective-permute-done.3.rn_ref = f32[6,3,3,8,128]{4,3,2,1,0:T(8,128)S(1)} collective-permute-done((f32[6,3,3,8,128]{4,3,2,1,0:T(8,128)}, f32[6,3,3,8,128]{4,3,2,1,0:T(8,128)S(1)}, u32[]{:S(2)}, u32[]{:S(2)}) %collective-permute-start.3) | collective-permute-done | bytes 221216 | tf_op jit(solution)/shard_map/ppermute | solution.py:177
  70.7 0.0 copy-start.4
  70.7 0.0 collective-permute-done.fl_ref
  70.7 0.0 copy-start.1
  70.7 0.0 collective-permute-done.1.fr_ref
  70.7 0.0 copy-done.3
  70.7 0.7 copy-done.4
  71.4 0.2 copy-done.1
  71.5 0.0 copy-start.2
  71.5 0.8 %copy-done.2 = f32[9,4,3,8,128]{4,3,2,1,0:T(8,128)} copy-done((f32[9,4,3,8,128]{4,3,2,1,0:T(8,128)}, f32[9,4,3,8,128]{4,3,2,1,0:T(8,128)S(1)}, u32[]{:S(2)}) %copy-start.2) | copy-done | bytes 442392
  72.3 3.1 %shard_map.43 = (f32[4,6,4,3,8,128]{5,4,3,2,1,0:T(8,128)}, f32[3,4,3,8,128]{4,3,2,1,0:T(8,128)}) custom-call(f32[9,4,3,8,128]{4,3,2,1,0:T(8,128)} %get-tuple-element.5.f_ref, f32[9,4,3,8,128]{4,3,2,1,0:T(8,128)} %copy-done.1, f32[9,4,3,8,128]{4,3,2,1,0:T(8,128)} %copy-done.2, f32[6,3,3,8,128]{4,3,2,1,0:T(8,128)} %copy-done.3, ...), custom_call_target="tpu_custom_call" | custom-call | flops 3686400 | bytes 3981312 | tf_op jit(solution)/shard_map/pallas_call | solution.py:189
  (4 shorter events, 0.0 us)
Async XLA Ops:
  0.6 1.9 %copy-start.5 = (s32[1,8]{1,0:T(1,128)S(1)}, s32[1,8]{1,0:T(1,128)}, u32[]{:S(2)}) copy-start(s32[1,8]{1,0:T(1,128)} %param.3) | copy-start | bytes 100
  4.1 34.3 %all-to-all-start = ((f32[8,73,8,128]{3,2,1,0:T(8,128)}), f32[8,73,8,128]{3,2,1,0:T(8,128)S(1)}, u32[]{:S(2)}, u32[]{:S(2)}) async-start(f32[8,73,8,128]{3,2,1,0:T(8,128)} %pad_maximum_fusion), calls=%async_computation | async-start | bytes 4784128 | tf_op jit(solution)/shard_map/all_to_all | solution.py:216
  38.4 1.4 %copy-start = (f32[8,73,8,128]{3,2,1,0:T(8,128)}, f32[8,73,8,128]{3,2,1,0:T(8,128)S(1)}, u32[]{:S(2)}) copy-start(f32[8,73,8,128]{3,2,1,0:T(8,128)S(1)} %all-to-all-done.x_ref) | copy-start | bytes 7176196
  43.7 27.0 %collective-permute-start = (f32[9,4,3,8,128]{4,3,2,1,0:T(8,128)}, f32[9,4,3,8,128]{4,3,2,1,0:T(8,128)S(1)}, u32[]{:S(2)}, u32[]{:S(2)}) collective-permute-start(f32[9,4,3,8,128]{4,3,2,1,0:T(8,128)} %get-tuple-element.5.f_ref), channel_id=1, source_target_pairs={{0,64},{64,128},{128,192},{192,256},{256,320},{320,384},{384,448},... | collective-permute-start | bytes 1327112 | tf_op jit(solution)/shard_map/ppermute | solution.py:174
  46.5 24.2 %collective-permute-start.1 = (f32[9,4,3,8,128]{4,3,2,1,0:T(8,128)}, f32[9,4,3,8,128]{4,3,2,1,0:T(8,128)S(1)}, u32[]{:S(2)}, u32[]{:S(2)}) collective-permute-start(f32[9,4,3,8,128]{4,3,2,1,0:T(8,128)} %get-tuple-element.5.f_ref), channel_id=1, source_target_pairs={{0,448},{64,0},{128,64},{192,128},{256,192},{320,256},{384,320},{4... | collective-permute-start | bytes 1327112 | tf_op jit(solution)/shard_map/ppermute | solution.py:175
  51.1 12.0 %collective-permute-start.2 = (f32[6,3,3,8,128]{4,3,2,1,0:T(8,128)}, f32[6,3,3,8,128]{4,3,2,1,0:T(8,128)S(1)}, u32[]{:S(2)}, u32[]{:S(2)}) collective-permute-start(f32[6,3,3,8,128]{4,3,2,1,0:T(8,128)} %get-tuple-element.6), channel_id=1, source_target_pairs={{0,1},{1,2},{2,3},{3,4},{4,5},{5,6},{6,7},{7,8},{8,9},{9,10},{10,1... | collective-permute-start | bytes 663560 | tf_op jit(solution)/shard_map/ppermute | solution.py:176
  58.5 12.2 %collective-permute-start.3 = (f32[6,3,3,8,128]{4,3,2,1,0:T(8,128)}, f32[6,3,3,8,128]{4,3,2,1,0:T(8,128)S(1)}, u32[]{:S(2)}, u32[]{:S(2)}) collective-permute-start(f32[6,3,3,8,128]{4,3,2,1,0:T(8,128)} %get-tuple-element.7), channel_id=1, source_target_pairs={{0,63},{1,0},{2,1},{3,2},{4,3},{5,4},{6,5},{7,6},{8,7},{9,8},{10,9... | collective-permute-start | bytes 663560 | tf_op jit(solution)/shard_map/ppermute | solution.py:177
  63.1 7.6 %copy-start.3 = (f32[6,3,3,8,128]{4,3,2,1,0:T(8,128)}, f32[6,3,3,8,128]{4,3,2,1,0:T(8,128)S(1)}, u32[]{:S(2)}) copy-start(f32[6,3,3,8,128]{4,3,2,1,0:T(8,128)S(1)} %collective-permute-done.2.rp_ref) | copy-start | bytes 663556
  70.7 0.7 copy-start.4
  70.7 0.9 %copy-start.1 = (f32[9,4,3,8,128]{4,3,2,1,0:T(8,128)}, f32[9,4,3,8,128]{4,3,2,1,0:T(8,128)S(1)}, u32[]{:S(2)}) copy-start(f32[9,4,3,8,128]{4,3,2,1,0:T(8,128)S(1)} %collective-permute-done.fl_ref) | copy-start | bytes 1327108
  71.5 0.8 %copy-start.2 = (f32[9,4,3,8,128]{4,3,2,1,0:T(8,128)}, f32[9,4,3,8,128]{4,3,2,1,0:T(8,128)S(1)}, u32[]{:S(2)}) copy-start(f32[9,4,3,8,128]{4,3,2,1,0:T(8,128)S(1)} %collective-permute-done.1.fr_ref) | copy-start | bytes 1327108

commit v8 on v7

--- a/solution.py
+++ b/solution.py
@@ -5,6 +5,7 @@
 from jax.experimental.pallas import tpu as pltpu
 from jax.sharding import PartitionSpec as P
 
+
 PHASES = 256
 HALO = 3
 
@@ -18,7 +19,7 @@
 
 
 def bin_kernel(bins_ref, x_ref, o_ref, head_ref, tail_ref, acc_ref):
-    bins, _, planes = acc_ref.shape[0], acc_ref.shape[1], acc_ref.shape[2]
+    bins, planes = acc_ref.shape[0], acc_ref.shape[2]
     per_src = (x_ref.shape[1] - 1) // (3 * planes)
     snaps = x_ref.shape[0] * per_src
     acc_ref[...] = jnp.zeros(acc_ref.shape, jnp.float32)
@@ -55,7 +56,7 @@
 
 
 def binned_fields(received, local_bins, bins, planes):
-    n_src, rows, ny, nz = received.shape
+    _, _, ny, nz = received.shape
     snaps = local_bins.shape[0]
     return pl.pallas_call(
         bin_kernel,
@@ -133,7 +134,7 @@
 
 
 def halo_kernel(f_ref, fl_ref, fr_ref, rp_ref, rn_ref, part_ref, terms_ref, vel_ref):
-    _, bins, planes, ny, nz = f_ref.shape
+    _, bins, planes, _, _ = f_ref.shape
 
     def at(comp, b, x):
         if 0 <= x < planes:
@@ -171,10 +172,10 @@
 
 def finish_terms(fields, head, tail):
     _, bins_dev, planes, ny, nz = fields.shape
+    from_prev = lax.ppermute(tail, "bin", ring("bin", 1))
+    from_next = lax.ppermute(head, "bin", ring("bin", -1))
     from_left = lax.ppermute(fields, "rev", ring("rev", 1))
     from_right = lax.ppermute(fields, "rev", ring("rev", -1))
-    from_prev = lax.ppermute(tail, "bin", ring("bin", 1))
-    from_next = lax.ppermute(head, "bin", ring("bin", -1))
     cells = bins_dev * planes * ny * nz
     vmem = pl.BlockSpec(memory_space=pltpu.VMEM)
     part = pl.pallas_call(

time: 75.8 us -> 75.8 us (level)
  no operation moved by 1% of the time
where the time goes in v8:
time: 75.8 us; the launch traced here: 75.4 us
  waiting for transfers between devices  36.7 us (48%)
  starting transfers between devices  21.9 us (29%)
  Pallas kernels  9.7 us (13%)
  local copies, waits for them, and re-layouts  4.87 us (6%)
  other arithmetic  1.61 us (2%)
    all_to_all x1, waiting for transfers between devices, shards(): received = lax.all_to_all(payload, 'rev', 0, 0, tiled=True)  29.1 us
    ppermute x1, waiting for transfers between devices, finish_terms(): from_next = lax.ppermute(head, 'bin', ring('bin', -1))  7.57 us
    ppermute x1, starting transfers between devices, finish_terms(): from_prev = lax.ppermute(tail, 'bin', ring('bin', 1))  7.36 us
    all_to_all x1, starting transfers between devices, shards(): received = lax.all_to_all(payload, 'rev', 0, 0, tiled=True)  5.2 us
    ppermute x1, starting transfers between devices, finish_terms(): from_right = lax.ppermute(fields, 'rev', ring('rev', -1))  4.61 us
    pallas_call x1, Pallas kernels, binned_fields(): pl.pallas_call(bin_kernel, out_shape=(jax.ShapeDtypeStruct((9, bins, plan...  3.87 us
    pallas_call x1, Pallas kernels, finish_terms(): pl.pallas_call(halo_kernel, out_shape=(jax.ShapeDtypeStruct((4, 6, bins_d...  3.13 us
    ppermute x1, starting transfers between devices, finish_terms(): from_left = lax.ppermute(fields, 'rev', ring('rev', 1))  2.77 us
  transfers between devices with their start and end apart: 5, of which 2 were waited for; matrix products, arithmetic and copies ran while one was open for 0% of the time, Pallas kernels for 4%

profile of v8, /device:TPU:249, one launch (start us, length us, event | category | flops | bytes accessed | tf_op | source)
XLA Modules:
  0.0 75.4 jit_solution(1618493795884059409)
XLA Ops:
  0.6 0.0 copy-start.5
  0.6 1.8 %copy.4 = f32[8,3,8,3,8,128]{5,4,3,1,0,2:T(8,128)S(1)} copy(f32[8,3,8,3,8,128]{5,4,3,2,1,0:T(8,128)} %bitcast.7) | data formatting | bytes 4718592 | tf_op jit(solution)/shard_map/reshape;squeeze | solution.py:212
  2.5 0.0 copy-done.5
  2.5 1.6 %pad_maximum_fusion = f32[8,73,8,128]{3,2,1,0:T(8,128)} fusion(f32[8,1,8,128]{3,2,1,0:T(8,128)S(1)} %broadcast_in_dim.2, f32[8,72,8,128]{3,2,1,0:T(8,128)S(1)} %bitcast.6), kind=kLoop, calls=%fused_computation | loop fusion | flops 598016 | bytes 4784128 | tf_op jit(solution)/shard_map/concatenate | solution.py:216
  4.1 5.2 %all-to-all-start = ((f32[8,73,8,128]{3,2,1,0:T(8,128)}), f32[8,73,8,128]{3,2,1,0:T(8,128)S(1)}, u32[]{:S(2)}, u32[]{:S(2)}) async-start(f32[8,73,8,128]{3,2,1,0:T(8,128)} %pad_maximum_fusion), calls=%async_computation | async-start | bytes 4784128 | tf_op jit(solution)/shard_map/all_to_all | solution.py:217
  9.3 29.1 %all-to-all-done.x_ref = f32[8,73,8,128]{3,2,1,0:T(8,128)S(1)} async-done(((f32[8,73,8,128]{3,2,1,0:T(8,128)}), f32[8,73,8,128]{3,2,1,0:T(8,128)S(1)}, u32[]{:S(2)}, u32[]{:S(2)}) %all-to-all-start) | async-done | bytes 2392096 | tf_op jit(solution)/shard_map/all_to_all | solution.py:217
  38.4 0.0 copy-start
  38.4 0.7 min.12.bins_ref
  39.1 0.7 copy-done
  39.8 3.9 %shard_map.41 = (f32[9,4,3,8,128]{4,3,2,1,0:T(8,128)}, f32[6,3,3,8,128]{4,3,2,1,0:T(8,128)}, f32[6,3,3,8,128]{4,3,2,1,0:T(8,128)}) custom-call(s32[64]{0:T(128)} %min.12.bins_ref, f32[8,73,8,128]{3,2,1,0:T(8,128)} %copy-done), custom_call_target="tpu_custom_call" | custom-call | flops 2949120 | bytes 2834432 | tf_op jit(solution)/shard_map/pallas_call | solution.py:61
  43.7 2.8 %collective-permute-start = (f32[9,4,3,8,128]{4,3,2,1,0:T(8,128)}, f32[9,4,3,8,128]{4,3,2,1,0:T(8,128)S(1)}, u32[]{:S(2)}, u32[]{:S(2)}) collective-permute-start(f32[9,4,3,8,128]{4,3,2,1,0:T(8,128)} %get-tuple-element.5.f_ref), channel_id=1, source_target_pairs={{0,64},{64,128},{128,192},{192,256},{256,320},{320,384},{384,448},... | collective-permute-start | bytes 1327112 | tf_op jit(solution)/shard_map/ppermute | solution.py:177
  46.5 4.6 %collective-permute-start.1 = (f32[9,4,3,8,128]{4,3,2,1,0:T(8,128)}, f32[9,4,3,8,128]{4,3,2,1,0:T(8,128)S(1)}, u32[]{:S(2)}, u32[]{:S(2)}) collective-permute-start(f32[9,4,3,8,128]{4,3,2,1,0:T(8,128)} %get-tuple-element.5.f_ref), channel_id=1, source_target_pairs={{0,448},{64,0},{128,64},{192,128},{256,192},{320,256},{384,320},{4... | collective-permute-start | bytes 1327112 | tf_op jit(solution)/shard_map/ppermute | solution.py:178
  51.1 7.4 %collective-permute-start.2 = (f32[6,3,3,8,128]{4,3,2,1,0:T(8,128)}, f32[6,3,3,8,128]{4,3,2,1,0:T(8,128)S(1)}, u32[]{:S(2)}, u32[]{:S(2)}) collective-permute-start(f32[6,3,3,8,128]{4,3,2,1,0:T(8,128)} %get-tuple-element.6), channel_id=1, source_target_pairs={{0,1},{1,2},{2,3},{3,4},{4,5},{5,6},{6,7},{7,8},{8,9},{9,10},{10,1... | collective-permute-start | bytes 663560 | tf_op jit(solution)/shard_map/ppermute | solution.py:175
  58.5 1.9 %collective-permute-start.3 = (f32[6,3,3,8,128]{4,3,2,1,0:T(8,128)}, f32[6,3,3,8,128]{4,3,2,1,0:T(8,128)S(1)}, u32[]{:S(2)}, u32[]{:S(2)}) collective-permute-start(f32[6,3,3,8,128]{4,3,2,1,0:T(8,128)} %get-tuple-element.7), channel_id=1, source_target_pairs={{0,63},{1,0},{2,1},{3,2},{4,3},{5,4},{6,5},{7,6},{8,7},{9,8},{10,9... | collective-permute-start | bytes 663560 | tf_op jit(solution)/shard_map/ppermute | solution.py:176
  60.4 2.7 %shard_map.42.part_ref = f32[3,6,4,3,8,128]{5,4,3,2,1,0:T(8,128)} custom-call(f32[9,4,3,8,128]{4,3,2,1,0:T(8,128)} %get-tuple-element.5.f_ref), custom_call_target="tpu_custom_call" | custom-call | flops 4915200 | bytes 1327104 | tf_op jit(solution)/shard_map/pallas_call | solution.py:181
  63.1 0.0 collective-permute-done.2.rp_ref
  63.1 0.0 copy-start.3
  63.1 7.6 %collective-permute-done.3.rn_ref = f32[6,3,3,8,128]{4,3,2,1,0:T(8,128)S(1)} collective-permute-done((f32[6,3,3,8,128]{4,3,2,1,0:T(8,128)}, f32[6,3,3,8,128]{4,3,2,1,0:T(8,128)S(1)}, u32[]{:S(2)}, u32[]{:S(2)}) %collective-permute-start.3) | collective-permute-done | bytes 221216 | tf_op jit(solution)/shard_map/ppermute | solution.py:176
  70.7 0.0 copy-start.4
  70.7 0.0 collective-permute-done.fl_ref
  70.7 0.0 copy-start.1
  70.7 0.0 collective-permute-done.1.fr_ref
  70.7 0.0 copy-done.3
  70.7 0.7 copy-done.4
  71.4 0.2 copy-done.1
  71.5 0.0 copy-start.2
  71.5 0.8 %copy-done.2 = f32[9,4,3,8,128]{4,3,2,1,0:T(8,128)} copy-done((f32[9,4,3,8,128]{4,3,2,1,0:T(8,128)}, f32[9,4,3,8,128]{4,3,2,1,0:T(8,128)S(1)}, u32[]{:S(2)}) %copy-start.2) | copy-done | bytes 442392
  72.3 3.1 %shard_map.43 = (f32[4,6,4,3,8,128]{5,4,3,2,1,0:T(8,128)}, f32[3,4,3,8,128]{4,3,2,1,0:T(8,128)}) custom-call(f32[9,4,3,8,128]{4,3,2,1,0:T(8,128)} %get-tuple-element.5.f_ref, f32[9,4,3,8,128]{4,3,2,1,0:T(8,128)} %copy-done.1, f32[9,4,3,8,128]{4,3,2,1,0:T(8,128)} %copy-done.2, f32[6,3,3,8,128]{4,3,2,1,0:T(8,128)} %copy-done.3, ...), custom_call_target="tpu_custom_call" | custom-call | flops 3686400 | bytes 3981312 | tf_op jit(solution)/shard_map/pallas_call | solution.py:190
  (4 shorter events, 0.0 us)
Async XLA Ops:
  0.6 1.9 %copy-start.5 = (s32[1,8]{1,0:T(1,128)S(1)}, s32[1,8]{1,0:T(1,128)}, u32[]{:S(2)}) copy-start(s32[1,8]{1,0:T(1,128)} %param.3) | copy-start | bytes 100
  4.1 34.3 %all-to-all-start = ((f32[8,73,8,128]{3,2,1,0:T(8,128)}), f32[8,73,8,128]{3,2,1,0:T(8,128)S(1)}, u32[]{:S(2)}, u32[]{:S(2)}) async-start(f32[8,73,8,128]{3,2,1,0:T(8,128)} %pad_maximum_fusion), calls=%async_computation | async-start | bytes 4784128 | tf_op jit(solution)/shard_map/all_to_all | solution.py:217
  38.4 1.4 %copy-start = (f32[8,73,8,128]{3,2,1,0:T(8,128)}, f32[8,73,8,128]{3,2,1,0:T(8,128)S(1)}, u32[]{:S(2)}) copy-start(f32[8,73,8,128]{3,2,1,0:T(8,128)S(1)} %all-to-all-done.x_ref) | copy-start | bytes 7176196
  43.7 27.0 %collective-permute-start = (f32[9,4,3,8,128]{4,3,2,1,0:T(8,128)}, f32[9,4,3,8,128]{4,3,2,1,0:T(8,128)S(1)}, u32[]{:S(2)}, u32[]{:S(2)}) collective-permute-start(f32[9,4,3,8,128]{4,3,2,1,0:T(8,128)} %get-tuple-element.5.f_ref), channel_id=1, source_target_pairs={{0,64},{64,128},{128,192},{192,256},{256,320},{320,384},{384,448},... | collective-permute-start | bytes 1327112 | tf_op jit(solution)/shard_map/ppermute | solution.py:177
  46.5 24.2 %collective-permute-start.1 = (f32[9,4,3,8,128]{4,3,2,1,0:T(8,128)}, f32[9,4,3,8,128]{4,3,2,1,0:T(8,128)S(1)}, u32[]{:S(2)}, u32[]{:S(2)}) collective-permute-start(f32[9,4,3,8,128]{4,3,2,1,0:T(8,128)} %get-tuple-element.5.f_ref), channel_id=1, source_target_pairs={{0,448},{64,0},{128,64},{192,128},{256,192},{320,256},{384,320},{4... | collective-permute-start | bytes 1327112 | tf_op jit(solution)/shard_map/ppermute | solution.py:178
  51.1 12.0 %collective-permute-start.2 = (f32[6,3,3,8,128]{4,3,2,1,0:T(8,128)}, f32[6,3,3,8,128]{4,3,2,1,0:T(8,128)S(1)}, u32[]{:S(2)}, u32[]{:S(2)}) collective-permute-start(f32[6,3,3,8,128]{4,3,2,1,0:T(8,128)} %get-tuple-element.6), channel_id=1, source_target_pairs={{0,1},{1,2},{2,3},{3,4},{4,5},{5,6},{6,7},{7,8},{8,9},{9,10},{10,1... | collective-permute-start | bytes 663560 | tf_op jit(solution)/shard_map/ppermute | solution.py:175
  58.5 12.2 %collective-permute-start.3 = (f32[6,3,3,8,128]{4,3,2,1,0:T(8,128)}, f32[6,3,3,8,128]{4,3,2,1,0:T(8,128)S(1)}, u32[]{:S(2)}, u32[]{:S(2)}) collective-permute-start(f32[6,3,3,8,128]{4,3,2,1,0:T(8,128)} %get-tuple-element.7), channel_id=1, source_target_pairs={{0,63},{1,0},{2,1},{3,2},{4,3},{5,4},{6,5},{7,6},{8,7},{9,8},{10,9... | collective-permute-start | bytes 663560 | tf_op jit(solution)/shard_map/ppermute | solution.py:176
  63.1 7.6 %copy-start.3 = (f32[6,3,3,8,128]{4,3,2,1,0:T(8,128)}, f32[6,3,3,8,128]{4,3,2,1,0:T(8,128)S(1)}, u32[]{:S(2)}) copy-start(f32[6,3,3,8,128]{4,3,2,1,0:T(8,128)S(1)} %collective-permute-done.2.rp_ref) | copy-start | bytes 663556
  70.7 0.7 copy-start.4
  70.7 0.9 %copy-start.1 = (f32[9,4,3,8,128]{4,3,2,1,0:T(8,128)}, f32[9,4,3,8,128]{4,3,2,1,0:T(8,128)S(1)}, u32[]{:S(2)}) copy-start(f32[9,4,3,8,128]{4,3,2,1,0:T(8,128)S(1)} %collective-permute-done.fl_ref) | copy-start | bytes 1327108
  71.5 0.8 %copy-start.2 = (f32[9,4,3,8,128]{4,3,2,1,0:T(8,128)}, f32[9,4,3,8,128]{4,3,2,1,0:T(8,128)S(1)}, u32[]{:S(2)}) copy-start(f32[9,4,3,8,128]{4,3,2,1,0:T(8,128)S(1)} %collective-permute-done.1.fr_ref) | copy-start | bytes 1327108

commit v9 on v7

--- a/solution.py
+++ b/solution.py
@@ -101,7 +101,7 @@
     return [(i, (i + step) % count) for i in range(count)]
 
 
-def halo_free_kernel(f_ref, part_ref):
+def halo_free_kernel(f_ref, part_ref, vel_ref):
     _, bins, planes, ny, nz = f_ref.shape
 
     def rolled(value, axis, size):
@@ -112,6 +112,8 @@
         for x in range(planes):
             velocity = [f_ref[c, b, x] for c in range(3)]
             stresses = [f_ref[3 + m, b, x] for m in range(6)]
+            for c in range(3):
+                vel_ref[c, b, x] = velocity[c]
             grad_u = [
                 [None, first_diff(rolled(velocity[c], 0, ny)), first_diff(rolled(velocity[c], 1, nz))]
                 for c in range(3)
@@ -132,41 +134,42 @@
                 part_ref[2, slot, b, x] = second_diff(along_y, stress) + second_diff(along_z, stress)
 
 
-def halo_kernel(f_ref, fl_ref, fr_ref, rp_ref, rn_ref, part_ref, terms_ref, vel_ref):
+def halo_kernel(f_ref, fl_ref, fr_ref, rp_ref, rn_ref, part_ref, terms_ref, ext_ref):
     _, bins, planes, ny, nz = f_ref.shape
-
-    def at(comp, b, x):
+    b = pl.program_id(0)
+
+    @pl.when(b == 0)
+    def _():
+        for m in range(6):
+            for j in range(HALO):
+                ext_ref[m, j] = rp_ref[m, j]
+                ext_ref[m, HALO + bins + j] = rn_ref[m, j]
+            for j in range(bins):
+                ext_ref[m, HALO + j] = f_ref[3 + m, j]
+
+    def at(comp, x):
         if 0 <= x < planes:
-            if 0 <= b < bins:
-                return f_ref[comp, b, x]
-            if b < 0:
-                return rp_ref[comp - 3, b + HALO, x]
-            return rn_ref[comp - 3, b - bins, x]
+            return f_ref[comp, b, x]
         if x < 0:
-            return fl_ref[comp, b, x + planes]
-        return fr_ref[comp, b, x - planes]
-
-    for b in range(bins):
-        for x in range(planes):
-            velocity = [f_ref[c, b, x] for c in range(3)]
-            stresses = [f_ref[3 + m, b, x] for m in range(6)]
-            for c in range(3):
-                vel_ref[c, b, x] = velocity[c]
-            grad_x = [first_diff(lambda k, c=c: at(c, b, x + k)) for c in range(3)]
-            for slot, (first, second) in enumerate(stress_pairs):
-                comp = 3 + slot
-                stress = stresses[slot]
-                along_x = lambda k, comp=comp: at(comp, b, x + k)
-                terms_ref[0, slot, b, x] = first_diff(lambda k, comp=comp: at(comp, b + k, x))
-                terms_ref[1, slot, b, x] = velocity[0] * first_diff(along_x) + part_ref[0, slot, b, x]
-                terms_ref[2, slot, b, x] = -(
-                    stresses[pair_index(first, 0)] * grad_x[second]
-                    + stresses[pair_index(second, 0)] * grad_x[first]
-                    + part_ref[1, slot, b, x]
-                )
-                terms_ref[3, slot, b, x] = viscosity * (
-                    second_diff(along_x, stress) + part_ref[2, slot, b, x]
-                )
+            return fl_ref[comp, 0, x + planes]
+        return fr_ref[comp, 0, x - planes]
+
+    for x in range(planes):
+        velocity = [f_ref[c, b, x] for c in range(3)]
+        stresses = [f_ref[3 + m, b, x] for m in range(6)]
+        grad_x = [first_diff(lambda k, c=c: at(c, x + k)) for c in range(3)]
+        for slot, (first, second) in enumerate(stress_pairs):
+            comp = 3 + slot
+            stress = stresses[slot]
+            along_x = lambda k, comp=comp: at(comp, x + k)
+            terms_ref[0, slot, 0, x] = first_diff(lambda k, slot=slot: ext_ref[slot, b + HALO + k, x])
+            terms_ref[1, slot, 0, x] = velocity[0] * first_diff(along_x) + part_ref[0, slot, 0, x]
+            terms_ref[2, slot, 0, x] = -(
+                stresses[pair_index(first, 0)] * grad_x[second]
+                + stresses[pair_index(second, 0)] * grad_x[first]
+                + part_ref[1, slot, 0, x]
+            )
+            terms_ref[3, slot, 0, x] = viscosity * (second_diff(along_x, stress) + part_ref[2, slot, 0, x])
 
 
 def finish_terms(fields, head, tail):
@@ -177,29 +180,43 @@
     from_next = lax.ppermute(head, "bin", ring("bin", -1))
     cells = bins_dev * planes * ny * nz
     vmem = pl.BlockSpec(memory_space=pltpu.VMEM)
-    part = pl.pallas_call(
+    part, mean_velocity = pl.pallas_call(
         halo_free_kernel,
-        out_shape=jax.ShapeDtypeStruct((3, 6, bins_dev, planes, ny, nz), jnp.float32),
+        out_shape=(
+            jax.ShapeDtypeStruct((3, 6, bins_dev, planes, ny, nz), jnp.float32),
+            jax.ShapeDtypeStruct((3, bins_dev, planes, ny, nz), jnp.float32),
+        ),
         in_specs=[vmem],
-        out_specs=vmem,
-        cost_estimate=pl.CostEstimate(
-            flops=cells * 400, bytes_accessed=(9 + 18) * cells * 4, transcendentals=0
-        ),
-    )(fields)
-    return pl.pallas_call(
-        halo_kernel,
-        out_shape=(
-            jax.ShapeDtypeStruct((4, 6, bins_dev, planes, ny, nz), jnp.float32),
-            jax.ShapeDtypeStruct((3, bins_dev, planes, ny, nz), jnp.float32),
-        ),
-        in_specs=[vmem] * 6,
         out_specs=(vmem, vmem),
         cost_estimate=pl.CostEstimate(
+            flops=cells * 400, bytes_accessed=(9 + 21) * cells * 4, transcendentals=0
+        ),
+    )(fields)
+    whole = lambda shape: pl.BlockSpec(shape, lambda b: (0,) * len(shape))
+    one_bin = lambda shape, axis: pl.BlockSpec(
+        shape, lambda b: tuple(b if i == axis else 0 for i in range(len(shape)))
+    )
+    terms = pl.pallas_call(
+        halo_kernel,
+        grid=(bins_dev,),
+        out_shape=jax.ShapeDtypeStruct((4, 6, bins_dev, planes, ny, nz), jnp.float32),
+        in_specs=[
+            whole(fields.shape),
+            one_bin((9, 1, planes, ny, nz), 1),
+            one_bin((9, 1, planes, ny, nz), 1),
+            whole(head.shape),
+            whole(head.shape),
+            one_bin((3, 6, 1, planes, ny, nz), 2),
+        ],
+        out_specs=one_bin((4, 6, 1, planes, ny, nz), 2),
+        scratch_shapes=[pltpu.VMEM((6, bins_dev + 2 * HALO, planes, ny, nz), jnp.float32)],
+        cost_estimate=pl.CostEstimate(
             flops=cells * 300,
-            bytes_accessed=(3 * fields.size + 2 * head.size + 45 * cells) * 4,
+            bytes_accessed=(3 * fields.size + 2 * head.size + 42 * cells) * 4,
             transcendentals=0,
         ),
     )(fields, from_left, from_right, from_prev, from_next, part)
+    return terms, mean_velocity
 
 
 def shards(snapshots, phase_index):

time: 75.8 us -> 76.3 us (level)
  Pallas kernels: 9.7 us -> 10.7 us
    pallas_call x2, Pallas kernels: 5.83 us -> 6.86 us  [the longest x1 4.16 us: finish_terms(): pl.pallas_call(halo_kernel, grid=(bins_dev,), out_shape=jax.ShapeDtypeStr...]
where the time goes in v9:
time: 76.3 us; the launch traced here: 75.9 us
  waiting for transfers between devices  36.7 us (48%)
  starting transfers between devices  21.9 us (29%)
  Pallas kernels  10.7 us (14%)
  local copies, waits for them, and re-layouts  4.25 us (6%)
  other arithmetic  1.61 us (2%)
    all_to_all x1, waiting for transfers between devices, shards(): received = lax.all_to_all(payload, 'rev', 0, 0, tiled=True)  29.1 us
    ppermute x1, waiting for transfers between devices, finish_terms(): from_next = lax.ppermute(head, 'bin', ring('bin', -1))  7.57 us
    ppermute x1, starting transfers between devices, finish_terms(): from_prev = lax.ppermute(tail, 'bin', ring('bin', 1))  7.36 us
    all_to_all x1, starting transfers between devices, shards(): received = lax.all_to_all(payload, 'rev', 0, 0, tiled=True)  5.2 us
    ppermute x1, starting transfers between devices, finish_terms(): from_right = lax.ppermute(fields, 'rev', ring('rev', -1))  4.61 us
    pallas_call x1, Pallas kernels, finish_terms(): pl.pallas_call(halo_kernel, grid=(bins_dev,), out_shape=jax.ShapeDtypeStr...  4.16 us
    pallas_call x1, Pallas kernels, binned_fields(): pl.pallas_call(bin_kernel, out_shape=(jax.ShapeDtypeStruct((9, bins, plan...  3.88 us
    ppermute x1, starting transfers between devices, finish_terms(): from_left = lax.ppermute(fields, 'rev', ring('rev', 1))  2.77 us
  transfers between devices with their start and end apart: 5, of which 2 were waited for; matrix products, arithmetic and copies ran while one was open for 0% of the time, Pallas kernels for 4%

profile of v9, /device:TPU:249, one launch (start us, length us, event | category | flops | bytes accessed | tf_op | source)
XLA Modules:
  0.0 75.9 jit_solution(2892949999378921749)
XLA Ops:
  0.6 0.0 copy-start.5
  0.6 1.8 %copy.4 = f32[8,3,8,3,8,128]{5,4,3,1,0,2:T(8,128)S(1)} copy(f32[8,3,8,3,8,128]{5,4,3,2,1,0:T(8,128)} %bitcast.7) | data formatting | bytes 4718592 | tf_op jit(solution)/shard_map/reshape;squeeze | solution.py:228
  2.5 0.0 copy-done.5
  2.5 1.6 %pad_maximum_fusion = f32[8,73,8,128]{3,2,1,0:T(8,128)} fusion(f32[8,1,8,128]{3,2,1,0:T(8,128)S(1)} %broadcast_in_dim.2, f32[8,72,8,128]{3,2,1,0:T(8,128)S(1)} %bitcast.6), kind=kLoop, calls=%fused_computation | loop fusion | flops 598016 | bytes 4784128 | tf_op jit(solution)/shard_map/concatenate | solution.py:232
  4.1 5.2 %all-to-all-start = ((f32[8,73,8,128]{3,2,1,0:T(8,128)}), f32[8,73,8,128]{3,2,1,0:T(8,128)S(1)}, u32[]{:S(2)}, u32[]{:S(2)}) async-start(f32[8,73,8,128]{3,2,1,0:T(8,128)} %pad_maximum_fusion), calls=%async_computation | async-start | bytes 4784128 | tf_op jit(solution)/shard_map/all_to_all | solution.py:233
  9.3 29.1 %all-to-all-done.x_ref = f32[8,73,8,128]{3,2,1,0:T(8,128)S(1)} async-done(((f32[8,73,8,128]{3,2,1,0:T(8,128)}), f32[8,73,8,128]{3,2,1,0:T(8,128)S(1)}, u32[]{:S(2)}, u32[]{:S(2)}) %all-to-all-start) | async-done | bytes 2392096 | tf_op jit(solution)/shard_map/all_to_all | solution.py:233
  38.4 0.0 copy-start
  38.4 0.7 min.12.bins_ref
  39.1 0.7 copy-done
  39.8 3.9 %shard_map.41 = (f32[9,4,3,8,128]{4,3,2,1,0:T(8,128)}, f32[6,3,3,8,128]{4,3,2,1,0:T(8,128)}, f32[6,3,3,8,128]{4,3,2,1,0:T(8,128)}) custom-call(s32[64]{0:T(128)} %min.12.bins_ref, f32[8,73,8,128]{3,2,1,0:T(8,128)} %copy-done), custom_call_target="tpu_custom_call" | custom-call | flops 2949120 | bytes 2834432 | tf_op jit(solution)/shard_map/pallas_call | solution.py:60
  43.7 2.8 %collective-permute-start = (f32[9,4,3,8,128]{4,3,2,1,0:T(8,128)}, f32[9,4,3,8,128]{4,3,2,1,0:T(8,128)S(1)}, u32[]{:S(2)}, u32[]{:S(2)}) collective-permute-start(f32[9,4,3,8,128]{4,3,2,1,0:T(8,128)} %get-tuple-element.7.f_ref), channel_id=1, source_target_pairs={{0,64},{64,128},{128,192},{192,256},{256,320},{320,384},{384,448},... | collective-permute-start | bytes 1327112 | tf_op jit(solution)/shard_map/ppermute | solution.py:177
  46.5 4.6 %collective-permute-start.1 = (f32[9,4,3,8,128]{4,3,2,1,0:T(8,128)}, f32[9,4,3,8,128]{4,3,2,1,0:T(8,128)S(1)}, u32[]{:S(2)}, u32[]{:S(2)}) collective-permute-start(f32[9,4,3,8,128]{4,3,2,1,0:T(8,128)} %get-tuple-element.7.f_ref), channel_id=1, source_target_pairs={{0,448},{64,0},{128,64},{192,128},{256,192},{320,256},{384,320},{4... | collective-permute-start | bytes 1327112 | tf_op jit(solution)/shard_map/ppermute | solution.py:178
  51.1 7.4 %collective-permute-start.2 = (f32[6,3,3,8,128]{4,3,2,1,0:T(8,128)}, f32[6,3,3,8,128]{4,3,2,1,0:T(8,128)S(1)}, u32[]{:S(2)}, u32[]{:S(2)}) collective-permute-start(f32[6,3,3,8,128]{4,3,2,1,0:T(8,128)} %get-tuple-element.8), channel_id=1, source_target_pairs={{0,1},{1,2},{2,3},{3,4},{4,5},{5,6},{6,7},{7,8},{8,9},{9,10},{10,1... | collective-permute-start | bytes 663560 | tf_op jit(solution)/shard_map/ppermute | solution.py:179
  58.5 1.9 %collective-permute-start.3 = (f32[6,3,3,8,128]{4,3,2,1,0:T(8,128)}, f32[6,3,3,8,128]{4,3,2,1,0:T(8,128)S(1)}, u32[]{:S(2)}, u32[]{:S(2)}) collective-permute-start(f32[6,3,3,8,128]{4,3,2,1,0:T(8,128)} %get-tuple-element.9), channel_id=1, source_target_pairs={{0,63},{1,0},{2,1},{3,2},{4,3},{5,4},{6,5},{7,6},{8,7},{9,8},{10,9... | collective-permute-start | bytes 663560 | tf_op jit(solution)/shard_map/ppermute | solution.py:180
  60.4 2.7 %shard_map.42 = (f32[3,6,4,3,8,128]{5,4,3,2,1,0:T(8,128)}, f32[3,4,3,8,128]{4,3,2,1,0:T(8,128)}) custom-call(f32[9,4,3,8,128]{4,3,2,1,0:T(8,128)} %get-tuple-element.7.f_ref), custom_call_target="tpu_custom_call" | custom-call | flops 4915200 | bytes 1474560 | tf_op jit(solution)/shard_map/pallas_call | solution.py:183
  63.1 0.0 collective-permute-done.2.rp_ref
  63.1 0.0 copy-start.3
  63.1 7.6 %collective-permute-done.3.rn_ref = f32[6,3,3,8,128]{4,3,2,1,0:T(8,128)S(1)} collective-permute-done((f32[6,3,3,8,128]{4,3,2,1,0:T(8,128)}, f32[6,3,3,8,128]{4,3,2,1,0:T(8,128)S(1)}, u32[]{:S(2)}, u32[]{:S(2)}) %collective-permute-start.3) | collective-permute-done | bytes 221216 | tf_op jit(solution)/shard_map/ppermute | solution.py:180
  70.7 0.0 copy-start.4
  70.7 0.0 collective-permute-done.fl_ref
  70.7 0.0 copy-start.1
  70.7 0.0 collective-permute-done.1.fr_ref
  70.7 0.0 copy-start.2
  70.7 0.0 copy-done.3
  70.7 0.7 copy-done.4
  71.4 0.2 copy-done.1
  71.5 0.2 copy-done.2
  71.7 4.2 %shard_map.43 = f32[4,6,4,3,8,128]{5,4,3,2,1,0:T(8,128)} custom-call(f32[9,4,3,8,128]{4,3,2,1,0:T(8,128)} %get-tuple-element.7.f_ref, f32[9,4,3,8,128]{4,3,2,1,0:T(8,128)} %copy-done.1, f32[9,4,3,8,128]{4,3,2,1,0:T(8,128)} %copy-done.2, f32[6,3,3,8,128]{4,3,2,1,0:T(8,128)} %copy-done.3, f32[6,3,3,8,128]{4,3,2,1,0:T(8,128)} %copy-done.4, ...), custom_call_target="tpu_custom_call" | custom-call | flops 3686400 | bytes 3833856 | tf_op jit(solution)/shard_map/pallas_call | solution.py:199
  (4 shorter events, 0.0 us)
Async XLA Ops:
  0.6 1.9 %copy-start.5 = (s32[1,8]{1,0:T(1,128)S(1)}, s32[1,8]{1,0:T(1,128)}, u32[]{:S(2)}) copy-start(s32[1,8]{1,0:T(1,128)} %param.3) | copy-start | bytes 100
  4.1 34.3 %all-to-all-start = ((f32[8,73,8,128]{3,2,1,0:T(8,128)}), f32[8,73,8,128]{3,2,1,0:T(8,128)S(1)}, u32[]{:S(2)}, u32[]{:S(2)}) async-start(f32[8,73,8,128]{3,2,1,0:T(8,128)} %pad_maximum_fusion), calls=%async_computation | async-start | bytes 4784128 | tf_op jit(solution)/shard_map/all_to_all | solution.py:233
  38.4 1.4 %copy-start = (f32[8,73,8,128]{3,2,1,0:T(8,128)}, f32[8,73,8,128]{3,2,1,0:T(8,128)S(1)}, u32[]{:S(2)}) copy-start(f32[8,73,8,128]{3,2,1,0:T(8,128)S(1)} %all-to-all-done.x_ref) | copy-start | bytes 7176196
  43.7 27.0 %collective-permute-start = (f32[9,4,3,8,128]{4,3,2,1,0:T(8,128)}, f32[9,4,3,8,128]{4,3,2,1,0:T(8,128)S(1)}, u32[]{:S(2)}, u32[]{:S(2)}) collective-permute-start(f32[9,4,3,8,128]{4,3,2,1,0:T(8,128)} %get-tuple-element.7.f_ref), channel_id=1, source_target_pairs={{0,64},{64,128},{128,192},{192,256},{256,320},{320,384},{384,448},... | collective-permute-start | bytes 1327112 | tf_op jit(solution)/shard_map/ppermute | solution.py:177
  46.5 24.2 %collective-permute-start.1 = (f32[9,4,3,8,128]{4,3,2,1,0:T(8,128)}, f32[9,4,3,8,128]{4,3,2,1,0:T(8,128)S(1)}, u32[]{:S(2)}, u32[]{:S(2)}) collective-permute-start(f32[9,4,3,8,128]{4,3,2,1,0:T(8,128)} %get-tuple-element.7.f_ref), channel_id=1, source_target_pairs={{0,448},{64,0},{128,64},{192,128},{256,192},{320,256},{384,320},{4... | collective-permute-start | bytes 1327112 | tf_op jit(solution)/shard_map/ppermute | solution.py:178
  51.1 12.0 %collective-permute-start.2 = (f32[6,3,3,8,128]{4,3,2,1,0:T(8,128)}, f32[6,3,3,8,128]{4,3,2,1,0:T(8,128)S(1)}, u32[]{:S(2)}, u32[]{:S(2)}) collective-permute-start(f32[6,3,3,8,128]{4,3,2,1,0:T(8,128)} %get-tuple-element.8), channel_id=1, source_target_pairs={{0,1},{1,2},{2,3},{3,4},{4,5},{5,6},{6,7},{7,8},{8,9},{9,10},{10,1... | collective-permute-start | bytes 663560 | tf_op jit(solution)/shard_map/ppermute | solution.py:179
  58.5 12.2 %collective-permute-start.3 = (f32[6,3,3,8,128]{4,3,2,1,0:T(8,128)}, f32[6,3,3,8,128]{4,3,2,1,0:T(8,128)S(1)}, u32[]{:S(2)}, u32[]{:S(2)}) collective-permute-start(f32[6,3,3,8,128]{4,3,2,1,0:T(8,128)} %get-tuple-element.9), channel_id=1, source_target_pairs={{0,63},{1,0},{2,1},{3,2},{4,3},{5,4},{6,5},{7,6},{8,7},{9,8},{10,9... | collective-permute-start | bytes 663560 | tf_op jit(solution)/shard_map/ppermute | solution.py:180
  63.1 7.6 %copy-start.3 = (f32[6,3,3,8,128]{4,3,2,1,0:T(8,128)}, f32[6,3,3,8,128]{4,3,2,1,0:T(8,128)S(1)}, u32[]{:S(2)}) copy-start(f32[6,3,3,8,128]{4,3,2,1,0:T(8,128)S(1)} %collective-permute-done.2.rp_ref) | copy-start | bytes 663556
  70.7 0.7 copy-start.4
  70.7 0.9 %copy-start.1 = (f32[9,4,3,8,128]{4,3,2,1,0:T(8,128)}, f32[9,4,3,8,128]{4,3,2,1,0:T(8,128)S(1)}, u32[]{:S(2)}) copy-start(f32[9,4,3,8,128]{4,3,2,1,0:T(8,128)S(1)} %collective-permute-done.fl_ref) | copy-start | bytes 1327108
  70.7 1.0 %copy-start.2 = (f32[9,4,3,8,128]{4,3,2,1,0:T(8,128)}, f32[9,4,3,8,128]{4,3,2,1,0:T(8,128)S(1)}, u32[]{:S(2)}) copy-start(f32[9,4,3,8,128]{4,3,2,1,0:T(8,128)S(1)} %collective-permute-done.1.fr_ref) | copy-start | bytes 1327108

commit v10 on v7

--- a/solution.py
+++ b/solution.py
@@ -18,57 +18,66 @@
 
 
 def bin_kernel(bins_ref, x_ref, o_ref, head_ref, tail_ref, acc_ref):
-    bins, _, planes = acc_ref.shape[0], acc_ref.shape[1], acc_ref.shape[2]
+    bins, planes = acc_ref.shape[0], acc_ref.shape[2]
     per_src = (x_ref.shape[1] - 1) // (3 * planes)
-    snaps = x_ref.shape[0] * per_src
-    acc_ref[...] = jnp.zeros(acc_ref.shape, jnp.float32)
-
-    def body(s, carry):
-        b = bins_ref[s]
-        src = s // per_src
-        base = (s % per_src) * (3 * planes)
+    src = pl.program_id(0)
+
+    @pl.when(src == 0)
+    def _():
+        acc_ref[...] = jnp.zeros(acc_ref.shape, jnp.float32)
+
+    def body(j, carry):
+        b = bins_ref[src * per_src + j]
+        base = j * (3 * planes)
         for p in range(planes):
-            u = x_ref[src, base + p]
-            v = x_ref[src, base + planes + p]
-            w = x_ref[src, base + 2 * planes + p]
+            u = x_ref[0, base + p]
+            v = x_ref[0, base + planes + p]
+            w = x_ref[0, base + 2 * planes + p]
             moments = (u, v, w, u * u, u * v, u * w, v * v, v * w, w * w)
             for k in range(9):
                 acc_ref[b, k, p] = acc_ref[b, k, p] + moments[k]
         acc_ref[b, 9, 0] = acc_ref[b, 9, 0] + 1.0
         return carry
 
-    lax.fori_loop(0, snaps, body, 0)
-
-    for b in range(bins):
-        count = acc_ref[b, 9, 0]
-        for p in range(planes):
-            vel = [acc_ref[b, c, p] / count for c in range(3)]
-            for c in range(3):
-                o_ref[c, b, p] = vel[c]
-            for slot, (i, j) in enumerate(stress_pairs):
-                stress = acc_ref[b, 3 + slot, p] / count - vel[i] * vel[j]
-                o_ref[3 + slot, b, p] = stress
-                if b < HALO:
-                    head_ref[slot, b, p] = stress
-                if b >= bins - HALO:
-                    tail_ref[slot, b - (bins - HALO), p] = stress
+    lax.fori_loop(0, per_src, body, 0)
+
+    @pl.when(src == pl.num_programs(0) - 1)
+    def _():
+        for b in range(bins):
+            count = acc_ref[b, 9, 0]
+            for p in range(planes):
+                vel = [acc_ref[b, c, p] / count for c in range(3)]
+                for c in range(3):
+                    o_ref[c, b, p] = vel[c]
+                for slot, (i, j) in enumerate(stress_pairs):
+                    stress = acc_ref[b, 3 + slot, p] / count - vel[i] * vel[j]
+                    o_ref[3 + slot, b, p] = stress
+                    if b < HALO:
+                        head_ref[slot, b, p] = stress
+                    if b >= bins - HALO:
+                        tail_ref[slot, b - (bins - HALO), p] = stress
 
 
 def binned_fields(received, local_bins, bins, planes):
     n_src, rows, ny, nz = received.shape
     snaps = local_bins.shape[0]
+    whole = lambda shape: pl.BlockSpec(shape, lambda i: (0,) * len(shape))
     return pl.pallas_call(
         bin_kernel,
+        grid=(n_src,),
         out_shape=(
             jax.ShapeDtypeStruct((9, bins, planes, ny, nz), jnp.float32),
             jax.ShapeDtypeStruct((6, HALO, planes, ny, nz), jnp.float32),
             jax.ShapeDtypeStruct((6, HALO, planes, ny, nz), jnp.float32),
         ),
-        in_specs=[pl.BlockSpec(memory_space=pltpu.SMEM), pl.BlockSpec(memory_space=pltpu.VMEM)],
+        in_specs=[
+            pl.BlockSpec(memory_space=pltpu.SMEM),
+            pl.BlockSpec((1, rows, ny, nz), lambda i: (i, 0, 0, 0)),
+        ],
         out_specs=(
-            pl.BlockSpec(memory_space=pltpu.VMEM),
-            pl.BlockSpec(memory_space=pltpu.VMEM),
-            pl.BlockSpec(memory_space=pltpu.VMEM),
+            whole((9, bins, planes, ny, nz)),
+            whole((6, HALO, planes, ny, nz)),
+            whole((6, HALO, planes, ny, nz)),
         ),
         scratch_shapes=[pltpu.VMEM((bins, 10, planes, ny, nz), jnp.float32)],
         cost_estimate=pl.CostEstimate(

time: 75.8 us -> 77.7 us (1.025)
  Pallas kernels: 9.7 us -> 11.5 us
    pallas_call x1, Pallas kernels: 3.87 us -> 5.7 us  [binned_fields(): pl.pallas_call(bin_kernel, grid=(n_src,), out_shape=(jax.ShapeDtypeStruct...]
  transfers between devices with their start and end apart: 5 -> 5, of which waited for: 2 -> 2; matrix products, arithmetic and copies ran while one was open for 0% -> 0% of each run, Pallas kernels for 4% -> 3%
where the time goes in v10:
time: 77.7 us; the launch traced here: 77.3 us
  waiting for transfers between devices  36.7 us (47%)
  starting transfers between devices  21.9 us (28%)
  Pallas kernels  11.5 us (15%)
  local copies, waits for them, and re-layouts  4.87 us (6%)
  other arithmetic  1.61 us (2%)
    all_to_all x1, waiting for transfers between devices, shards(): received = lax.all_to_all(payload, 'rev', 0, 0, tiled=True)  29.1 us
    ppermute x1, waiting for transfers between devices, finish_terms(): from_next = lax.ppermute(head, 'bin', ring('bin', -1))  7.57 us
    ppermute x1, starting transfers between devices, finish_terms(): from_prev = lax.ppermute(tail, 'bin', ring('bin', 1))  7.36 us
    pallas_call x1, Pallas kernels, binned_fields(): pl.pallas_call(bin_kernel, grid=(n_src,), out_shape=(jax.ShapeDtypeStruct...  5.7 us
    all_to_all x1, starting transfers between devices, shards(): received = lax.all_to_all(payload, 'rev', 0, 0, tiled=True)  5.2 us
    ppermute x1, starting transfers between devices, finish_terms(): from_right = lax.ppermute(fields, 'rev', ring('rev', -1))  4.61 us
    pallas_call x1, Pallas kernels, finish_terms(): pl.pallas_call(halo_kernel, out_shape=(jax.ShapeDtypeStruct((4, 6, bins_d...  3.13 us
    ppermute x1, starting transfers between devices, finish_terms(): from_left = lax.ppermute(fields, 'rev', ring('rev', 1))  2.77 us
  transfers between devices with their start and end apart: 5, of which 2 were waited for; matrix products, arithmetic and copies ran while one was open for 0% of the time, Pallas kernels for 3%

profile of v10, /device:TPU:249, one launch (start us, length us, event | category | flops | bytes accessed | tf_op | source)
XLA Modules:
  0.0 77.3 jit_solution(4422341249681701563)
XLA Ops:
  0.6 0.0 copy-start.5
  0.6 1.8 %copy.4 = f32[8,3,8,3,8,128]{5,4,3,1,0,2:T(8,128)S(1)} copy(f32[8,3,8,3,8,128]{5,4,3,2,1,0:T(8,128)} %bitcast.7) | data formatting | bytes 4718592 | tf_op jit(solution)/shard_map/reshape;squeeze | solution.py:220
  2.5 0.0 copy-done.5
  2.5 1.6 %pad_maximum_fusion = f32[8,73,8,128]{3,2,1,0:T(8,128)} fusion(f32[8,1,8,128]{3,2,1,0:T(8,128)S(1)} %broadcast_in_dim.2, f32[8,72,8,128]{3,2,1,0:T(8,128)S(1)} %bitcast.6), kind=kLoop, calls=%fused_computation | loop fusion | flops 598016 | bytes 4784128 | tf_op jit(solution)/shard_map/concatenate | solution.py:224
  4.1 5.2 %all-to-all-start = ((f32[8,73,8,128]{3,2,1,0:T(8,128)}), f32[8,73,8,128]{3,2,1,0:T(8,128)S(1)}, u32[]{:S(2)}, u32[]{:S(2)}) async-start(f32[8,73,8,128]{3,2,1,0:T(8,128)} %pad_maximum_fusion), calls=%async_computation | async-start | bytes 4784128 | tf_op jit(solution)/shard_map/all_to_all | solution.py:225
  9.3 29.1 %all-to-all-done.x_ref = f32[8,73,8,128]{3,2,1,0:T(8,128)S(1)} async-done(((f32[8,73,8,128]{3,2,1,0:T(8,128)}), f32[8,73,8,128]{3,2,1,0:T(8,128)S(1)}, u32[]{:S(2)}, u32[]{:S(2)}) %all-to-all-start) | async-done | bytes 2392096 | tf_op jit(solution)/shard_map/all_to_all | solution.py:225
  38.4 0.0 copy-start
  38.4 0.7 min.12.bins_ref
  39.1 0.7 copy-done
  39.8 5.7 %shard_map.41 = (f32[9,4,3,8,128]{4,3,2,1,0:T(8,128)}, f32[6,3,3,8,128]{4,3,2,1,0:T(8,128)}, f32[6,3,3,8,128]{4,3,2,1,0:T(8,128)}) custom-call(s32[64]{0:T(128)} %min.12.bins_ref, f32[8,73,8,128]{3,2,1,0:T(8,128)} %copy-done), custom_call_target="tpu_custom_call" | custom-call | flops 2949120 | bytes 2834432 | tf_op jit(solution)/shard_map/pallas_call | solution.py:65
  45.5 2.8 %collective-permute-start = (f32[9,4,3,8,128]{4,3,2,1,0:T(8,128)}, f32[9,4,3,8,128]{4,3,2,1,0:T(8,128)S(1)}, u32[]{:S(2)}, u32[]{:S(2)}) collective-permute-start(f32[9,4,3,8,128]{4,3,2,1,0:T(8,128)} %get-tuple-element.5.f_ref), channel_id=1, source_target_pairs={{0,64},{64,128},{128,192},{192,256},{256,320},{320,384},{384,448},... | collective-permute-start | bytes 1327112 | tf_op jit(solution)/shard_map/ppermute | solution.py:183
  48.3 4.6 %collective-permute-start.1 = (f32[9,4,3,8,128]{4,3,2,1,0:T(8,128)}, f32[9,4,3,8,128]{4,3,2,1,0:T(8,128)S(1)}, u32[]{:S(2)}, u32[]{:S(2)}) collective-permute-start(f32[9,4,3,8,128]{4,3,2,1,0:T(8,128)} %get-tuple-element.5.f_ref), channel_id=1, source_target_pairs={{0,448},{64,0},{128,64},{192,128},{256,192},{320,256},{384,320},{4... | collective-permute-start | bytes 1327112 | tf_op jit(solution)/shard_map/ppermute | solution.py:184
  52.9 7.4 %collective-permute-start.2 = (f32[6,3,3,8,128]{4,3,2,1,0:T(8,128)}, f32[6,3,3,8,128]{4,3,2,1,0:T(8,128)S(1)}, u32[]{:S(2)}, u32[]{:S(2)}) collective-permute-start(f32[6,3,3,8,128]{4,3,2,1,0:T(8,128)} %get-tuple-element.6), channel_id=1, source_target_pairs={{0,1},{1,2},{2,3},{3,4},{4,5},{5,6},{6,7},{7,8},{8,9},{9,10},{10,1... | collective-permute-start | bytes 663560 | tf_op jit(solution)/shard_map/ppermute | solution.py:185
  60.3 1.9 %collective-permute-start.3 = (f32[6,3,3,8,128]{4,3,2,1,0:T(8,128)}, f32[6,3,3,8,128]{4,3,2,1,0:T(8,128)S(1)}, u32[]{:S(2)}, u32[]{:S(2)}) collective-permute-start(f32[6,3,3,8,128]{4,3,2,1,0:T(8,128)} %get-tuple-element.7), channel_id=1, source_target_pairs={{0,63},{1,0},{2,1},{3,2},{4,3},{5,4},{6,5},{7,6},{8,7},{9,8},{10,9... | collective-permute-start | bytes 663560 | tf_op jit(solution)/shard_map/ppermute | solution.py:186
  62.2 2.7 %shard_map.42.part_ref = f32[3,6,4,3,8,128]{5,4,3,2,1,0:T(8,128)} custom-call(f32[9,4,3,8,128]{4,3,2,1,0:T(8,128)} %get-tuple-element.5.f_ref), custom_call_target="tpu_custom_call" | custom-call | flops 4915200 | bytes 1327104 | tf_op jit(solution)/shard_map/pallas_call | solution.py:189
  64.9 0.0 collective-permute-done.2.rp_ref
  64.9 0.0 copy-start.3
  64.9 7.6 %collective-permute-done.3.rn_ref = f32[6,3,3,8,128]{4,3,2,1,0:T(8,128)S(1)} collective-permute-done((f32[6,3,3,8,128]{4,3,2,1,0:T(8,128)}, f32[6,3,3,8,128]{4,3,2,1,0:T(8,128)S(1)}, u32[]{:S(2)}, u32[]{:S(2)}) %collective-permute-start.3) | collective-permute-done | bytes 221216 | tf_op jit(solution)/shard_map/ppermute | solution.py:186
  72.5 0.0 copy-start.4
  72.5 0.0 collective-permute-done.fl_ref
  72.5 0.0 copy-start.1
  72.5 0.0 collective-permute-done.1.fr_ref
  72.5 0.0 copy-done.3
  72.5 0.7 copy-done.4
  73.2 0.2 copy-done.1
  73.4 0.0 copy-start.2
  73.4 0.8 copy-done.2
  74.1 3.1 %shard_map.43 = (f32[4,6,4,3,8,128]{5,4,3,2,1,0:T(8,128)}, f32[3,4,3,8,128]{4,3,2,1,0:T(8,128)}) custom-call(f32[9,4,3,8,128]{4,3,2,1,0:T(8,128)} %get-tuple-element.5.f_ref, f32[9,4,3,8,128]{4,3,2,1,0:T(8,128)} %copy-done.1, f32[9,4,3,8,128]{4,3,2,1,0:T(8,128)} %copy-done.2, f32[6,3,3,8,128]{4,3,2,1,0:T(8,128)} %copy-done.3, ...), custom_call_target="tpu_custom_call" | custom-call | flops 3686400 | bytes 3981312 | tf_op jit(solution)/shard_map/pallas_call | solution.py:198
  (4 shorter events, 0.0 us)
Async XLA Ops:
  0.6 1.9 %copy-start.5 = (s32[1,8]{1,0:T(1,128)S(1)}, s32[1,8]{1,0:T(1,128)}, u32[]{:S(2)}) copy-start(s32[1,8]{1,0:T(1,128)} %param.3) | copy-start | bytes 100
  4.1 34.3 %all-to-all-start = ((f32[8,73,8,128]{3,2,1,0:T(8,128)}), f32[8,73,8,128]{3,2,1,0:T(8,128)S(1)}, u32[]{:S(2)}, u32[]{:S(2)}) async-start(f32[8,73,8,128]{3,2,1,0:T(8,128)} %pad_maximum_fusion), calls=%async_computation | async-start | bytes 4784128 | tf_op jit(solution)/shard_map/all_to_all | solution.py:225
  38.4 1.4 %copy-start = (f32[8,73,8,128]{3,2,1,0:T(8,128)}, f32[8,73,8,128]{3,2,1,0:T(8,128)S(1)}, u32[]{:S(2)}) copy-start(f32[8,73,8,128]{3,2,1,0:T(8,128)S(1)} %all-to-all-done.x_ref) | copy-start | bytes 7176196
  45.5 27.0 %collective-permute-start = (f32[9,4,3,8,128]{4,3,2,1,0:T(8,128)}, f32[9,4,3,8,128]{4,3,2,1,0:T(8,128)S(1)}, u32[]{:S(2)}, u32[]{:S(2)}) collective-permute-start(f32[9,4,3,8,128]{4,3,2,1,0:T(8,128)} %get-tuple-element.5.f_ref), channel_id=1, source_target_pairs={{0,64},{64,128},{128,192},{192,256},{256,320},{320,384},{384,448},... | collective-permute-start | bytes 1327112 | tf_op jit(solution)/shard_map/ppermute | solution.py:183
  48.3 24.2 %collective-permute-start.1 = (f32[9,4,3,8,128]{4,3,2,1,0:T(8,128)}, f32[9,4,3,8,128]{4,3,2,1,0:T(8,128)S(1)}, u32[]{:S(2)}, u32[]{:S(2)}) collective-permute-start(f32[9,4,3,8,128]{4,3,2,1,0:T(8,128)} %get-tuple-element.5.f_ref), channel_id=1, source_target_pairs={{0,448},{64,0},{128,64},{192,128},{256,192},{320,256},{384,320},{4... | collective-permute-start | bytes 1327112 | tf_op jit(solution)/shard_map/ppermute | solution.py:184
  52.9 12.0 %collective-permute-start.2 = (f32[6,3,3,8,128]{4,3,2,1,0:T(8,128)}, f32[6,3,3,8,128]{4,3,2,1,0:T(8,128)S(1)}, u32[]{:S(2)}, u32[]{:S(2)}) collective-permute-start(f32[6,3,3,8,128]{4,3,2,1,0:T(8,128)} %get-tuple-element.6), channel_id=1, source_target_pairs={{0,1},{1,2},{2,3},{3,4},{4,5},{5,6},{6,7},{7,8},{8,9},{9,10},{10,1... | collective-permute-start | bytes 663560 | tf_op jit(solution)/shard_map/ppermute | solution.py:185
  60.3 12.2 %collective-permute-start.3 = (f32[6,3,3,8,128]{4,3,2,1,0:T(8,128)}, f32[6,3,3,8,128]{4,3,2,1,0:T(8,128)S(1)}, u32[]{:S(2)}, u32[]{:S(2)}) collective-permute-start(f32[6,3,3,8,128]{4,3,2,1,0:T(8,128)} %get-tuple-element.7), channel_id=1, source_target_pairs={{0,63},{1,0},{2,1},{3,2},{4,3},{5,4},{6,5},{7,6},{8,7},{9,8},{10,9... | collective-permute-start | bytes 663560 | tf_op jit(solution)/shard_map/ppermute | solution.py:186
  64.9 7.6 %copy-start.3 = (f32[6,3,3,8,128]{4,3,2,1,0:T(8,128)}, f32[6,3,3,8,128]{4,3,2,1,0:T(8,128)S(1)}, u32[]{:S(2)}) copy-start(f32[6,3,3,8,128]{4,3,2,1,0:T(8,128)S(1)} %collective-permute-done.2.rp_ref) | copy-start | bytes 663556
  72.5 0.7 copy-start.4
  72.5 0.9 %copy-start.1 = (f32[9,4,3,8,128]{4,3,2,1,0:T(8,128)}, f32[9,4,3,8,128]{4,3,2,1,0:T(8,128)S(1)}, u32[]{:S(2)}) copy-start(f32[9,4,3,8,128]{4,3,2,1,0:T(8,128)S(1)} %collective-permute-done.fl_ref) | copy-start | bytes 1327108
  73.4 0.8 copy-start.2

commit v11 on v7

--- a/solution.py
+++ b/solution.py
@@ -37,7 +37,7 @@
         acc_ref[b, 9, 0] = acc_ref[b, 9, 0] + 1.0
         return carry
 
-    lax.fori_loop(0, snaps, body, 0)
+    lax.fori_loop(0, snaps, body, 0, unroll=2)
 
     for b in range(bins):
         count = acc_ref[b, 9, 0]

time: 75.8 us -> 75.6 us (level)
  the two profiles are of different devices: /device:TPU:249 before, /device:TPU:241 now
where the time goes in v11:
time: 75.6 us; the launch traced here: 75.2 us
  waiting for transfers between devices  36.7 us (49%)
  starting transfers between devices  21.9 us (29%)
  Pallas kernels  9.45 us (12%)
  local copies, waits for them, and re-layouts  4.87 us (6%)
  other arithmetic  1.61 us (2%)
    all_to_all x1, waiting for transfers between devices, shards(): received = lax.all_to_all(payload, 'rev', 0, 0, tiled=True)  29.1 us
    ppermute x1, waiting for transfers between devices, finish_terms(): from_next = lax.ppermute(head, 'bin', ring('bin', -1))  7.57 us
    ppermute x1, starting transfers between devices, finish_terms(): from_prev = lax.ppermute(tail, 'bin', ring('bin', 1))  7.36 us
    all_to_all x1, starting transfers between devices, shards(): received = lax.all_to_all(payload, 'rev', 0, 0, tiled=True)  5.2 us
    ppermute x1, starting transfers between devices, finish_terms(): from_right = lax.ppermute(fields, 'rev', ring('rev', -1))  4.61 us
    pallas_call x1, Pallas kernels, binned_fields(): pl.pallas_call(bin_kernel, out_shape=(jax.ShapeDtypeStruct((9, bins, plan...  3.61 us
    pallas_call x1, Pallas kernels, finish_terms(): pl.pallas_call(halo_kernel, out_shape=(jax.ShapeDtypeStruct((4, 6, bins_d...  3.13 us
    ppermute x1, starting transfers between devices, finish_terms(): from_left = lax.ppermute(fields, 'rev', ring('rev', 1))  2.77 us
  transfers between devices with their start and end apart: 5, of which 2 were waited for; matrix products, arithmetic and copies ran while one was open for 0% of the time, Pallas kernels for 4%

profile of v11, /device:TPU:241, one launch (start us, length us, event | category | flops | bytes accessed | tf_op | source)
XLA Modules:
  0.0 75.2 jit_solution(4366980076925814627)
XLA Ops:
  0.6 0.0 copy-start.5
  0.6 1.8 %copy.4 = f32[8,3,8,3,8,128]{5,4,3,1,0,2:T(8,128)S(1)} copy(f32[8,3,8,3,8,128]{5,4,3,2,1,0:T(8,128)} %bitcast.7) | data formatting | bytes 4718592 | tf_op jit(solution)/shard_map/reshape;squeeze | solution.py:211
  2.5 0.0 copy-done.5
  2.5 1.6 %pad_maximum_fusion = f32[8,73,8,128]{3,2,1,0:T(8,128)} fusion(f32[8,1,8,128]{3,2,1,0:T(8,128)S(1)} %broadcast_in_dim.2, f32[8,72,8,128]{3,2,1,0:T(8,128)S(1)} %bitcast.6), kind=kLoop, calls=%fused_computation | loop fusion | flops 598016 | bytes 4784128 | tf_op jit(solution)/shard_map/concatenate | solution.py:215
  4.1 5.2 %all-to-all-start = ((f32[8,73,8,128]{3,2,1,0:T(8,128)}), f32[8,73,8,128]{3,2,1,0:T(8,128)S(1)}, u32[]{:S(2)}, u32[]{:S(2)}) async-start(f32[8,73,8,128]{3,2,1,0:T(8,128)} %pad_maximum_fusion), calls=%async_computation | async-start | bytes 4784128 | tf_op jit(solution)/shard_map/all_to_all | solution.py:216
  9.3 29.1 %all-to-all-done.x_ref = f32[8,73,8,128]{3,2,1,0:T(8,128)S(1)} async-done(((f32[8,73,8,128]{3,2,1,0:T(8,128)}), f32[8,73,8,128]{3,2,1,0:T(8,128)S(1)}, u32[]{:S(2)}, u32[]{:S(2)}) %all-to-all-start) | async-done | bytes 2392096 | tf_op jit(solution)/shard_map/all_to_all | solution.py:216
  38.4 0.0 copy-start
  38.4 0.7 min.12.bins_ref
  39.1 0.7 copy-done
  39.8 3.6 %shard_map.41 = (f32[9,4,3,8,128]{4,3,2,1,0:T(8,128)}, f32[6,3,3,8,128]{4,3,2,1,0:T(8,128)}, f32[6,3,3,8,128]{4,3,2,1,0:T(8,128)}) custom-call(s32[64]{0:T(128)} %min.12.bins_ref, f32[8,73,8,128]{3,2,1,0:T(8,128)} %copy-done), custom_call_target="tpu_custom_call" | custom-call | flops 2949120 | bytes 2834432 | tf_op jit(solution)/shard_map/pallas_call | solution.py:60
  43.5 2.8 %collective-permute-start = (f32[9,4,3,8,128]{4,3,2,1,0:T(8,128)}, f32[9,4,3,8,128]{4,3,2,1,0:T(8,128)S(1)}, u32[]{:S(2)}, u32[]{:S(2)}) collective-permute-start(f32[9,4,3,8,128]{4,3,2,1,0:T(8,128)} %get-tuple-element.5.f_ref), channel_id=1, source_target_pairs={{0,64},{64,128},{128,192},{192,256},{256,320},{320,384},{384,448},... | collective-permute-start | bytes 1327112 | tf_op jit(solution)/shard_map/ppermute | solution.py:174
  46.2 4.6 %collective-permute-start.1 = (f32[9,4,3,8,128]{4,3,2,1,0:T(8,128)}, f32[9,4,3,8,128]{4,3,2,1,0:T(8,128)S(1)}, u32[]{:S(2)}, u32[]{:S(2)}) collective-permute-start(f32[9,4,3,8,128]{4,3,2,1,0:T(8,128)} %get-tuple-element.5.f_ref), channel_id=1, source_target_pairs={{0,448},{64,0},{128,64},{192,128},{256,192},{320,256},{384,320},{4... | collective-permute-start | bytes 1327112 | tf_op jit(solution)/shard_map/ppermute | solution.py:175
  50.8 7.4 %collective-permute-start.2 = (f32[6,3,3,8,128]{4,3,2,1,0:T(8,128)}, f32[6,3,3,8,128]{4,3,2,1,0:T(8,128)S(1)}, u32[]{:S(2)}, u32[]{:S(2)}) collective-permute-start(f32[6,3,3,8,128]{4,3,2,1,0:T(8,128)} %get-tuple-element.6), channel_id=1, source_target_pairs={{0,1},{1,2},{2,3},{3,4},{4,5},{5,6},{6,7},{7,8},{8,9},{9,10},{10,1... | collective-permute-start | bytes 663560 | tf_op jit(solution)/shard_map/ppermute | solution.py:176
  58.2 1.9 %collective-permute-start.3 = (f32[6,3,3,8,128]{4,3,2,1,0:T(8,128)}, f32[6,3,3,8,128]{4,3,2,1,0:T(8,128)S(1)}, u32[]{:S(2)}, u32[]{:S(2)}) collective-permute-start(f32[6,3,3,8,128]{4,3,2,1,0:T(8,128)} %get-tuple-element.7), channel_id=1, source_target_pairs={{0,63},{1,0},{2,1},{3,2},{4,3},{5,4},{6,5},{7,6},{8,7},{9,8},{10,9... | collective-permute-start | bytes 663560 | tf_op jit(solution)/shard_map/ppermute | solution.py:177
  60.1 2.7 %shard_map.42.part_ref = f32[3,6,4,3,8,128]{5,4,3,2,1,0:T(8,128)} custom-call(f32[9,4,3,8,128]{4,3,2,1,0:T(8,128)} %get-tuple-element.5.f_ref), custom_call_target="tpu_custom_call" | custom-call | flops 4915200 | bytes 1327104 | tf_op jit(solution)/shard_map/pallas_call | solution.py:180
  62.8 0.0 collective-permute-done.2.rp_ref
  62.8 0.0 copy-start.3
  62.8 7.6 %collective-permute-done.3.rn_ref = f32[6,3,3,8,128]{4,3,2,1,0:T(8,128)S(1)} collective-permute-done((f32[6,3,3,8,128]{4,3,2,1,0:T(8,128)}, f32[6,3,3,8,128]{4,3,2,1,0:T(8,128)S(1)}, u32[]{:S(2)}, u32[]{:S(2)}) %collective-permute-start.3) | collective-permute-done | bytes 221216 | tf_op jit(solution)/shard_map/ppermute | solution.py:177
  70.4 0.0 copy-start.4
  70.4 0.0 collective-permute-done.fl_ref
  70.4 0.0 copy-start.1
  70.4 0.0 collective-permute-done.1.fr_ref
  70.4 0.0 copy-done.3
  70.4 0.7 copy-done.4
  71.1 0.2 copy-done.1
  71.3 0.0 copy-start.2
  71.3 0.8 %copy-done.2 = f32[9,4,3,8,128]{4,3,2,1,0:T(8,128)} copy-done((f32[9,4,3,8,128]{4,3,2,1,0:T(8,128)}, f32[9,4,3,8,128]{4,3,2,1,0:T(8,128)S(1)}, u32[]{:S(2)}) %copy-start.2) | copy-done | bytes 442392
  72.0 3.1 %shard_map.43 = (f32[4,6,4,3,8,128]{5,4,3,2,1,0:T(8,128)}, f32[3,4,3,8,128]{4,3,2,1,0:T(8,128)}) custom-call(f32[9,4,3,8,128]{4,3,2,1,0:T(8,128)} %get-tuple-element.5.f_ref, f32[9,4,3,8,128]{4,3,2,1,0:T(8,128)} %copy-done.1, f32[9,4,3,8,128]{4,3,2,1,0:T(8,128)} %copy-done.2, f32[6,3,3,8,128]{4,3,2,1,0:T(8,128)} %copy-done.3, ...), custom_call_target="tpu_custom_call" | custom-call | flops 3686400 | bytes 3981312 | tf_op jit(solution)/shard_map/pallas_call | solution.py:189
  (4 shorter events, 0.0 us)
Async XLA Ops:
  0.6 1.9 %copy-start.5 = (s32[1,8]{1,0:T(1,128)S(1)}, s32[1,8]{1,0:T(1,128)}, u32[]{:S(2)}) copy-start(s32[1,8]{1,0:T(1,128)} %param.3) | copy-start | bytes 100
  4.1 34.3 %all-to-all-start = ((f32[8,73,8,128]{3,2,1,0:T(8,128)}), f32[8,73,8,128]{3,2,1,0:T(8,128)S(1)}, u32[]{:S(2)}, u32[]{:S(2)}) async-start(f32[8,73,8,128]{3,2,1,0:T(8,128)} %pad_maximum_fusion), calls=%async_computation | async-start | bytes 4784128 | tf_op jit(solution)/shard_map/all_to_all | solution.py:216
  38.4 1.4 %copy-start = (f32[8,73,8,128]{3,2,1,0:T(8,128)}, f32[8,73,8,128]{3,2,1,0:T(8,128)S(1)}, u32[]{:S(2)}) copy-start(f32[8,73,8,128]{3,2,1,0:T(8,128)S(1)} %all-to-all-done.x_ref) | copy-start | bytes 7176196
  43.5 27.0 %collective-permute-start = (f32[9,4,3,8,128]{4,3,2,1,0:T(8,128)}, f32[9,4,3,8,128]{4,3,2,1,0:T(8,128)S(1)}, u32[]{:S(2)}, u32[]{:S(2)}) collective-permute-start(f32[9,4,3,8,128]{4,3,2,1,0:T(8,128)} %get-tuple-element.5.f_ref), channel_id=1, source_target_pairs={{0,64},{64,128},{128,192},{192,256},{256,320},{320,384},{384,448},... | collective-permute-start | bytes 1327112 | tf_op jit(solution)/shard_map/ppermute | solution.py:174
  46.2 24.2 %collective-permute-start.1 = (f32[9,4,3,8,128]{4,3,2,1,0:T(8,128)}, f32[9,4,3,8,128]{4,3,2,1,0:T(8,128)S(1)}, u32[]{:S(2)}, u32[]{:S(2)}) collective-permute-start(f32[9,4,3,8,128]{4,3,2,1,0:T(8,128)} %get-tuple-element.5.f_ref), channel_id=1, source_target_pairs={{0,448},{64,0},{128,64},{192,128},{256,192},{320,256},{384,320},{4... | collective-permute-start | bytes 1327112 | tf_op jit(solution)/shard_map/ppermute | solution.py:175
  50.8 12.0 %collective-permute-start.2 = (f32[6,3,3,8,128]{4,3,2,1,0:T(8,128)}, f32[6,3,3,8,128]{4,3,2,1,0:T(8,128)S(1)}, u32[]{:S(2)}, u32[]{:S(2)}) collective-permute-start(f32[6,3,3,8,128]{4,3,2,1,0:T(8,128)} %get-tuple-element.6), channel_id=1, source_target_pairs={{0,1},{1,2},{2,3},{3,4},{4,5},{5,6},{6,7},{7,8},{8,9},{9,10},{10,1... | collective-permute-start | bytes 663560 | tf_op jit(solution)/shard_map/ppermute | solution.py:176
  58.2 12.2 %collective-permute-start.3 = (f32[6,3,3,8,128]{4,3,2,1,0:T(8,128)}, f32[6,3,3,8,128]{4,3,2,1,0:T(8,128)S(1)}, u32[]{:S(2)}, u32[]{:S(2)}) collective-permute-start(f32[6,3,3,8,128]{4,3,2,1,0:T(8,128)} %get-tuple-element.7), channel_id=1, source_target_pairs={{0,63},{1,0},{2,1},{3,2},{4,3},{5,4},{6,5},{7,6},{8,7},{9,8},{10,9... | collective-permute-start | bytes 663560 | tf_op jit(solution)/shard_map/ppermute | solution.py:177
  62.8 7.6 %copy-start.3 = (f32[6,3,3,8,128]{4,3,2,1,0:T(8,128)}, f32[6,3,3,8,128]{4,3,2,1,0:T(8,128)S(1)}, u32[]{:S(2)}) copy-start(f32[6,3,3,8,128]{4,3,2,1,0:T(8,128)S(1)} %collective-permute-done.2.rp_ref) | copy-start | bytes 663556
  70.4 0.7 copy-start.4
  70.4 0.9 %copy-start.1 = (f32[9,4,3,8,128]{4,3,2,1,0:T(8,128)}, f32[9,4,3,8,128]{4,3,2,1,0:T(8,128)S(1)}, u32[]{:S(2)}) copy-start(f32[9,4,3,8,128]{4,3,2,1,0:T(8,128)S(1)} %collective-permute-done.fl_ref) | copy-start | bytes 1327108
  71.3 0.8 %copy-start.2 = (f32[9,4,3,8,128]{4,3,2,1,0:T(8,128)}, f32[9,4,3,8,128]{4,3,2,1,0:T(8,128)S(1)}, u32[]{:S(2)}) copy-start(f32[9,4,3,8,128]{4,3,2,1,0:T(8,128)S(1)} %collective-permute-done.1.fr_ref) | copy-start | bytes 1327108

commit v12 on v11

--- a/solution.py
+++ b/solution.py
@@ -71,6 +71,7 @@
             pl.BlockSpec(memory_space=pltpu.VMEM),
         ),
         scratch_shapes=[pltpu.VMEM((bins, 10, planes, ny, nz), jnp.float32)],
+        compiler_params=pltpu.CompilerParams(vmem_limit_bytes=16 * 1024 * 1024),
         cost_estimate=pl.CostEstimate(
             flops=snaps * planes * ny * nz * 15,
             bytes_accessed=received.size * 4 + 9 * bins * planes * ny * nz * 4,
@@ -182,6 +183,7 @@
         out_shape=jax.ShapeDtypeStruct((3, 6, bins_dev, planes, ny, nz), jnp.float32),
         in_specs=[vmem],
         out_specs=vmem,
+        compiler_params=pltpu.CompilerParams(vmem_limit_bytes=16 * 1024 * 1024),
         cost_estimate=pl.CostEstimate(
             flops=cells * 400, bytes_accessed=(9 + 18) * cells * 4, transcendentals=0
         ),
@@ -194,6 +196,7 @@
         ),
         in_specs=[vmem] * 6,
         out_specs=(vmem, vmem),
+        compiler_params=pltpu.CompilerParams(vmem_limit_bytes=16 * 1024 * 1024),
         cost_estimate=pl.CostEstimate(
             flops=cells * 300,
             bytes_accessed=(3 * fields.size + 2 * head.size + 45 * cells) * 4,

time: 75.6 us -> 68.5 us (0.906)
  Pallas kernels: 9.45 us -> 3.72 us
  local copies, waits for them, and re-layouts: 4.87 us -> 1.93 us
  waiting for transfers between devices: 36.7 us -> 38.4 us
    unnamed x12 -> x2, local copies, waits for them, and re-layouts: 2.33 us -> 0.01 us
    pallas_call x1, Pallas kernels: 3.61 us -> 1.55 us  [binned_fields(): pl.pallas_call(bin_kernel, out_shape=(jax.ShapeDtypeStruct((9, bins, plan...]
    pallas_call x1, Pallas kernels: 2.7 us -> 0.75 us  [finish_terms(): pl.pallas_call(halo_free_kernel, out_shape=jax.ShapeDtypeStruct((3, 6, bi...]
    pallas_call x1, Pallas kernels: 3.13 us -> 1.41 us  [finish_terms(): pl.pallas_call(halo_kernel, out_shape=(jax.ShapeDtypeStruct((4, 6, bins_d...]
    ppermute x1, waiting for transfers between devices: 7.57 us -> 9.14 us  [finish_terms(): from_next = lax.ppermute(head, 'bin', ring('bin', -1))]
  transfers between devices with their start and end apart: 5 -> 5, of which waited for: 2 -> 3; matrix products, arithmetic and copies ran while one was open for 0% -> 0% of each run, Pallas kernels for 4% -> 1%
where the time goes in v12:
time: 68.5 us; the launch traced here: 68.2 us
  waiting for transfers between devices  38.4 us (56%)
  starting transfers between devices  21.9 us (32%)
  Pallas kernels  3.72 us (5%)
  local copies, waits for them, and re-layouts  1.93 us (3%)
  other arithmetic  1.59 us (2%)
  between operations  0.73 us (1%)
    all_to_all x1, waiting for transfers between devices, shards(): received = lax.all_to_all(payload, 'rev', 0, 0, tiled=True)  29.1 us
    ppermute x1, waiting for transfers between devices, finish_terms(): from_next = lax.ppermute(head, 'bin', ring('bin', -1))  9.14 us
    ppermute x1, starting transfers between devices, finish_terms(): from_prev = lax.ppermute(tail, 'bin', ring('bin', 1))  7.36 us
    all_to_all x1, starting transfers between devices, shards(): received = lax.all_to_all(payload, 'rev', 0, 0, tiled=True)  5.2 us
    ppermute x1, starting transfers between devices, finish_terms(): from_right = lax.ppermute(fields, 'rev', ring('rev', -1))  4.61 us
    ppermute x1, starting transfers between devices, finish_terms(): from_left = lax.ppermute(fields, 'rev', ring('rev', 1))  2.78 us
    ppermute x1, starting transfers between devices, finish_terms(): from_next = lax.ppermute(head, 'bin', ring('bin', -1))  1.92 us
    another operation x1, local copies, waits for them, and re-layouts, shards(): by_dest = frames.reshape(snaps, comps, n_rev, planes, ny, nz)  1.84 us
  transfers between devices with their start and end apart: 5, of which 3 were waited for; matrix products, arithmetic and copies ran while one was open for 0% of the time, Pallas kernels for 1%

profile of v12, /device:TPU:241, one launch (start us, length us, event | category | flops | bytes accessed | tf_op | source)
XLA Modules:
  0.0 68.2 jit_solution(5238747727352180388)
XLA Ops:
  0.6 0.0 copy-start
  0.6 1.8 %copy.4 = f32[8,3,8,3,8,128]{5,4,3,1,0,2:T(8,128)S(1)} copy(f32[8,3,8,3,8,128]{5,4,3,2,1,0:T(8,128)} %bitcast.7) | data formatting | bytes 4718592 | tf_op jit(solution)/shard_map/reshape;squeeze | solution.py:214
  2.5 0.0 copy-done
  2.5 1.6 %pad_maximum_fusion = f32[8,73,8,128]{3,2,1,0:T(8,128)} fusion(f32[8,1,8,128]{3,2,1,0:T(8,128)S(1)} %broadcast_in_dim.2, f32[8,72,8,128]{3,2,1,0:T(8,128)S(1)} %bitcast.6), kind=kLoop, calls=%fused_computation | loop fusion | flops 598016 | bytes 4784128 | tf_op jit(solution)/shard_map/concatenate | solution.py:218
  4.1 5.2 %all-to-all-start = ((f32[8,73,8,128]{3,2,1,0:T(8,128)}), f32[8,73,8,128]{3,2,1,0:T(8,128)S(1)}, u32[]{:S(2)}, u32[]{:S(2)}) async-start(f32[8,73,8,128]{3,2,1,0:T(8,128)} %pad_maximum_fusion), calls=%async_computation | async-start | bytes 4784128 | tf_op jit(solution)/shard_map/all_to_all | solution.py:219
  9.3 29.1 %all-to-all-done.x_ref = f32[8,73,8,128]{3,2,1,0:T(8,128)S(1)} async-done(((f32[8,73,8,128]{3,2,1,0:T(8,128)}), f32[8,73,8,128]{3,2,1,0:T(8,128)S(1)}, u32[]{:S(2)}, u32[]{:S(2)}) %all-to-all-start) | async-done | bytes 2392096 | tf_op jit(solution)/shard_map/all_to_all | solution.py:219
  38.4 0.1 min.12.bins_ref
  38.5 1.6 %shard_map.41 = (f32[9,4,3,8,128]{4,3,2,1,0:T(8,128)S(1)}, f32[6,3,3,8,128]{4,3,2,1,0:T(8,128)S(1)}, f32[6,3,3,8,128]{4,3,2,1,0:T(8,128)S(1)}) custom-call(s32[64]{0:T(128)S(1)} %min.12.bins_ref, f32[8,73,8,128]{3,2,1,0:T(8,128)S(1)} %all-to-all-done.x_ref), custom_call_target="tpu_custom_call" | custom-call | flops 2949120 | bytes 2834432 | tf_op jit(solution)/shard_map/pallas_call | solution.py:60
  40.0 2.8 %collective-permute-start = (f32[9,4,3,8,128]{4,3,2,1,0:T(8,128)S(1)}, f32[9,4,3,8,128]{4,3,2,1,0:T(8,128)S(1)}, u32[]{:S(2)}, u32[]{:S(2)}) collective-permute-start(f32[9,4,3,8,128]{4,3,2,1,0:T(8,128)S(1)} %get-tuple-element.5.f_ref), channel_id=1, source_target_pairs={{0,64},{64,128},{128,192},{192,256},{256,320},{320,384},{384,448},... | collective-permute-start | bytes 1327112 | tf_op jit(solution)/shard_map/ppermute | solution.py:175
  42.8 4.6 %collective-permute-start.1 = (f32[9,4,3,8,128]{4,3,2,1,0:T(8,128)S(1)}, f32[9,4,3,8,128]{4,3,2,1,0:T(8,128)S(1)}, u32[]{:S(2)}, u32[]{:S(2)}) collective-permute-start(f32[9,4,3,8,128]{4,3,2,1,0:T(8,128)S(1)} %get-tuple-element.5.f_ref), channel_id=1, source_target_pairs={{0,448},{64,0},{128,64},{192,128},{256,192},{320,256},{384,320},{4... | collective-permute-start | bytes 1327112 | tf_op jit(solution)/shard_map/ppermute | solution.py:176
  47.5 7.4 %collective-permute-start.2 = (f32[6,3,3,8,128]{4,3,2,1,0:T(8,128)S(1)}, f32[6,3,3,8,128]{4,3,2,1,0:T(8,128)S(1)}, u32[]{:S(2)}, u32[]{:S(2)}) collective-permute-start(f32[6,3,3,8,128]{4,3,2,1,0:T(8,128)S(1)} %get-tuple-element.6), channel_id=1, source_target_pairs={{0,1},{1,2},{2,3},{3,4},{4,5},{5,6},{6,7},{7,8},{8,9},{9,10},{10,1... | collective-permute-start | bytes 663560 | tf_op jit(solution)/shard_map/ppermute | solution.py:177
  54.8 1.9 %collective-permute-start.3 = (f32[6,3,3,8,128]{4,3,2,1,0:T(8,128)S(1)}, f32[6,3,3,8,128]{4,3,2,1,0:T(8,128)S(1)}, u32[]{:S(2)}, u32[]{:S(2)}) collective-permute-start(f32[6,3,3,8,128]{4,3,2,1,0:T(8,128)S(1)} %get-tuple-element.7), channel_id=1, source_target_pairs={{0,63},{1,0},{2,1},{3,2},{4,3},{5,4},{6,5},{7,6},{8,7},{9,8},{10,9... | collective-permute-start | bytes 663560 | tf_op jit(solution)/shard_map/ppermute | solution.py:178
  56.8 0.8 %shard_map.42.part_ref = f32[3,6,4,3,8,128]{5,4,3,2,1,0:T(8,128)S(1)} custom-call(f32[9,4,3,8,128]{4,3,2,1,0:T(8,128)S(1)} %get-tuple-element.5.f_ref), custom_call_target="tpu_custom_call" | custom-call | flops 4915200 | bytes 1327104 | tf_op jit(solution)/shard_map/pallas_call | solution.py:181
  57.5 0.2 collective-permute-done.2.rp_ref
  57.7 9.1 %collective-permute-done.3.rn_ref = f32[6,3,3,8,128]{4,3,2,1,0:T(8,128)S(1)} collective-permute-done((f32[6,3,3,8,128]{4,3,2,1,0:T(8,128)S(1)}, f32[6,3,3,8,128]{4,3,2,1,0:T(8,128)S(1)}, u32[]{:S(2)}, u32[]{:S(2)}) %collective-permute-start.3) | collective-permute-done | bytes 221216 | tf_op jit(solution)/shard_map/ppermute | solution.py:178
  66.8 0.0 collective-permute-done.fl_ref
  66.8 0.0 collective-permute-done.1.fr_ref
  66.8 1.4 %shard_map.43 = (f32[4,6,4,3,8,128]{5,4,3,2,1,0:T(8,128)}, f32[3,4,3,8,128]{4,3,2,1,0:T(8,128)}) custom-call(f32[9,4,3,8,128]{4,3,2,1,0:T(8,128)S(1)} %get-tuple-element.5.f_ref, f32[9,4,3,8,128]{4,3,2,1,0:T(8,128)S(1)} %collective-permute-done.fl_ref, f32[9,4,3,8,128]{4,3,2,1,0:T(8,128)S(1)} %collective-permute-done.1.fr_ref, ...), custom_call_target="tpu_custom_call" | custom-call | flops 3686400 | bytes 3981312 | tf_op jit(solution)/shard_map/pallas_call | solution.py:191
  (4 shorter events, 0.0 us)
Async XLA Ops:
  0.6 1.9 %copy-start = (s32[1,8]{1,0:T(1,128)S(1)}, s32[1,8]{1,0:T(1,128)}, u32[]{:S(2)}) copy-start(s32[1,8]{1,0:T(1,128)} %param.3) | copy-start | bytes 100
  4.1 34.3 %all-to-all-start = ((f32[8,73,8,128]{3,2,1,0:T(8,128)}), f32[8,73,8,128]{3,2,1,0:T(8,128)S(1)}, u32[]{:S(2)}, u32[]{:S(2)}) async-start(f32[8,73,8,128]{3,2,1,0:T(8,128)} %pad_maximum_fusion), calls=%async_computation | async-start | bytes 4784128 | tf_op jit(solution)/shard_map/all_to_all | solution.py:219
  40.0 26.8 %collective-permute-start = (f32[9,4,3,8,128]{4,3,2,1,0:T(8,128)S(1)}, f32[9,4,3,8,128]{4,3,2,1,0:T(8,128)S(1)}, u32[]{:S(2)}, u32[]{:S(2)}) collective-permute-start(f32[9,4,3,8,128]{4,3,2,1,0:T(8,128)S(1)} %get-tuple-element.5.f_ref), channel_id=1, source_target_pairs={{0,64},{64,128},{128,192},{192,256},{256,320},{320,384},{384,448},... | collective-permute-start | bytes 1327112 | tf_op jit(solution)/shard_map/ppermute | solution.py:175
  42.8 24.0 %collective-permute-start.1 = (f32[9,4,3,8,128]{4,3,2,1,0:T(8,128)S(1)}, f32[9,4,3,8,128]{4,3,2,1,0:T(8,128)S(1)}, u32[]{:S(2)}, u32[]{:S(2)}) collective-permute-start(f32[9,4,3,8,128]{4,3,2,1,0:T(8,128)S(1)} %get-tuple-element.5.f_ref), channel_id=1, source_target_pairs={{0,448},{64,0},{128,64},{192,128},{256,192},{320,256},{384,320},{4... | collective-permute-start | bytes 1327112 | tf_op jit(solution)/shard_map/ppermute | solution.py:176
  47.5 10.2 %collective-permute-start.2 = (f32[6,3,3,8,128]{4,3,2,1,0:T(8,128)S(1)}, f32[6,3,3,8,128]{4,3,2,1,0:T(8,128)S(1)}, u32[]{:S(2)}, u32[]{:S(2)}) collective-permute-start(f32[6,3,3,8,128]{4,3,2,1,0:T(8,128)S(1)} %get-tuple-element.6), channel_id=1, source_target_pairs={{0,1},{1,2},{2,3},{3,4},{4,5},{5,6},{6,7},{7,8},{8,9},{9,10},{10,1... | collective-permute-start | bytes 663560 | tf_op jit(solution)/shard_map/ppermute | solution.py:177
  54.8 12.0 %collective-permute-start.3 = (f32[6,3,3,8,128]{4,3,2,1,0:T(8,128)S(1)}, f32[6,3,3,8,128]{4,3,2,1,0:T(8,128)S(1)}, u32[]{:S(2)}, u32[]{:S(2)}) collective-permute-start(f32[6,3,3,8,128]{4,3,2,1,0:T(8,128)S(1)} %get-tuple-element.7), channel_id=1, source_target_pairs={{0,63},{1,0},{2,1},{3,2},{4,3},{5,4},{6,5},{7,6},{8,7},{9,8},{10,9... | collective-permute-start | bytes 663560 | tf_op jit(solution)/shard_map/ppermute | solution.py:178

commit v13 on v12

--- a/solution.py
+++ b/solution.py
@@ -78,6 +78,37 @@
             transcendentals=0,
         ),
     )(local_bins, received)
+
+
+def pack_kernel(phase_ref, x_ref, o_ref):
+    snaps, comps, _, ny, nz = x_ref.shape
+    n_dest, rows = o_ref.shape[0], o_ref.shape[1]
+    planes = (rows - 1) // (snaps * comps)
+    for d in range(n_dest):
+        for s in range(snaps):
+            for c in range(comps):
+                o_ref[d, pl.ds((s * comps + c) * planes, planes)] = x_ref[s, c, pl.ds(d * planes, planes)]
+    lane = lax.broadcasted_iota(jnp.int32, (ny, nz), 1)
+    row = jnp.zeros((ny, nz), jnp.float32)
+    for s in range(snaps):
+        row = jnp.where(lane == s, phase_ref[s], row)
+    for d in range(n_dest):
+        o_ref[d, rows - 1] = row
+
+
+def packed_payload(frames, phases, n_dest):
+    snaps, comps, nx, ny, nz = frames.shape
+    rows = snaps * comps * (nx // n_dest) + 1
+    return pl.pallas_call(
+        pack_kernel,
+        out_shape=jax.ShapeDtypeStruct((n_dest, rows, ny, nz), jnp.float32),
+        in_specs=[pl.BlockSpec(memory_space=pltpu.SMEM), pl.BlockSpec(memory_space=pltpu.VMEM)],
+        out_specs=pl.BlockSpec(memory_space=pltpu.VMEM),
+        compiler_params=pltpu.CompilerParams(vmem_limit_bytes=16 * 1024 * 1024),
+        cost_estimate=pl.CostEstimate(
+            flops=0, bytes_accessed=2 * frames.size * 4, transcendentals=0
+        ),
+    )(phases, frames)
 
 
 def first_diff(shifted):
@@ -211,11 +242,7 @@
     frames = snapshots[0]
     snaps, comps, nx, ny, nz = frames.shape
     planes = nx // n_rev
-    by_dest = frames.reshape(snaps, comps, n_rev, planes, ny, nz)
-    by_dest = jnp.transpose(by_dest, (2, 0, 1, 3, 4, 5)).reshape(n_rev, snaps * comps * planes, ny, nz)
-    phase_row = jnp.pad(phase_index[0].astype(jnp.float32), (0, nz - snaps))
-    phase_slab = jnp.broadcast_to(phase_row[None, None, None, :], (n_rev, 1, ny, nz))
-    payload = jnp.concatenate([by_dest, phase_slab], axis=1)
+    payload = packed_payload(frames, phase_index[0].astype(jnp.float32), n_rev)
     received = lax.all_to_all(payload, "rev", 0, 0, tiled=True)
     phases = received[:, -1, 0, :snaps].reshape(-1).astype(jnp.int32)
     local_bins = jnp.clip(phases - lax.axis_index("bin") * bins_dev, 0, bins_dev - 1)

time: 68.5 us -> 69.5 us (1.015)
  the two profiles are of different devices: /device:TPU:241 before, /device:TPU:225 now
where the time goes in v13:
time: 69.5 us; the launch traced here: 69.2 us
  waiting for transfers between devices  38.4 us (55%)
  starting transfers between devices  21.9 us (32%)
  Pallas kernels  4.41 us (6%)
  local copies, waits for them, and re-layouts  3.16 us (5%)
  between operations  0.7 us (1%)
    all_to_all x1, waiting for transfers between devices, shards(): received = lax.all_to_all(payload, 'rev', 0, 0, tiled=True)  29.1 us
    ppermute x1, waiting for transfers between devices, finish_terms(): from_next = lax.ppermute(head, 'bin', ring('bin', -1))  9.14 us
    ppermute x1, starting transfers between devices, finish_terms(): from_prev = lax.ppermute(tail, 'bin', ring('bin', 1))  7.36 us
    all_to_all x1, starting transfers between devices, shards(): received = lax.all_to_all(payload, 'rev', 0, 0, tiled=True)  5.2 us
    ppermute x1, starting transfers between devices, finish_terms(): from_right = lax.ppermute(fields, 'rev', ring('rev', -1))  4.61 us
    unnamed x4, local copies, waits for them, and re-layouts  3.08 us
    ppermute x1, starting transfers between devices, finish_terms(): from_left = lax.ppermute(fields, 'rev', ring('rev', 1))  2.78 us
    ppermute x1, starting transfers between devices, finish_terms(): from_next = lax.ppermute(head, 'bin', ring('bin', -1))  1.92 us
  transfers between devices with their start and end apart: 5, of which 3 were waited for; matrix products, arithmetic and copies ran while one was open for 0% of the time, Pallas kernels for 1%

profile of v13, /device:TPU:225, one launch (start us, length us, event | category | flops | bytes accessed | tf_op | source)
XLA Modules:
  0.0 69.2 jit_solution(11652732805513399169)
XLA Ops:
  0.6 0.7 convert_bitcast_fusion.phase_ref
  1.3 0.0 copy-start.1
  1.3 1.7 %copy-done.1 = f32[1,8,3,24,8,128]{5,4,3,2,1,0:T(8,128)S(1)} copy-done((f32[1,8,3,24,8,128]{5,4,3,2,1,0:T(8,128)S(1)}, f32[1,8,3,24,8,128]{5,4,3,2,1,0:T(8,128)}, u32[]{:S(2)}) %copy-start.1) | copy-done | bytes 2359320
  3.0 0.7 %shard_map.41 = f32[8,73,8,128]{3,2,1,0:T(8,128)S(1)} custom-call(f32[8]{0:T(128)S(1)} %convert_bitcast_fusion.phase_ref, f32[8,3,24,8,128]{4,3,2,1,0:T(8,128)S(1)} %bitcast.3), custom_call_target="tpu_custom_call" | custom-call | bytes 4718592 | tf_op jit(solution)/shard_map/pallas_call | solution.py:102
  3.7 0.0 copy-start
  3.7 1.4 %copy-done = f32[8,73,8,128]{3,2,1,0:T(8,128)} copy-done((f32[8,73,8,128]{3,2,1,0:T(8,128)}, f32[8,73,8,128]{3,2,1,0:T(8,128)S(1)}, u32[]{:S(2)}) %copy-start) | copy-done | bytes 2392088
  5.1 5.2 %all-to-all-start = ((f32[8,73,8,128]{3,2,1,0:T(8,128)}), f32[8,73,8,128]{3,2,1,0:T(8,128)S(1)}, u32[]{:S(2)}, u32[]{:S(2)}) async-start(f32[8,73,8,128]{3,2,1,0:T(8,128)} %copy-done), calls=%async_computation | async-start | bytes 4784128 | tf_op jit(solution)/shard_map/all_to_all | solution.py:246
  10.3 29.1 %all-to-all-done.x_ref = f32[8,73,8,128]{3,2,1,0:T(8,128)S(1)} async-done(((f32[8,73,8,128]{3,2,1,0:T(8,128)}), f32[8,73,8,128]{3,2,1,0:T(8,128)S(1)}, u32[]{:S(2)}, u32[]{:S(2)}) %all-to-all-start) | async-done | bytes 2392096 | tf_op jit(solution)/shard_map/all_to_all | solution.py:246
  39.4 0.1 min.12.bins_ref
  39.5 1.6 %shard_map.42 = (f32[9,4,3,8,128]{4,3,2,1,0:T(8,128)S(1)}, f32[6,3,3,8,128]{4,3,2,1,0:T(8,128)S(1)}, f32[6,3,3,8,128]{4,3,2,1,0:T(8,128)S(1)}) custom-call(s32[64]{0:T(128)S(1)} %min.12.bins_ref, f32[8,73,8,128]{3,2,1,0:T(8,128)S(1)} %all-to-all-done.x_ref), custom_call_target="tpu_custom_call" | custom-call | flops 2949120 | bytes 2834432 | tf_op jit(solution)/shard_map/pallas_call | solution.py:60
  41.0 2.8 %collective-permute-start = (f32[9,4,3,8,128]{4,3,2,1,0:T(8,128)S(1)}, f32[9,4,3,8,128]{4,3,2,1,0:T(8,128)S(1)}, u32[]{:S(2)}, u32[]{:S(2)}) collective-permute-start(f32[9,4,3,8,128]{4,3,2,1,0:T(8,128)S(1)} %get-tuple-element.5.f_ref), channel_id=1, source_target_pairs={{0,64},{64,128},{128,192},{192,256},{256,320},{320,384},{384,448},... | collective-permute-start | bytes 1327112 | tf_op jit(solution)/shard_map/ppermute | solution.py:206
  43.8 4.6 %collective-permute-start.1 = (f32[9,4,3,8,128]{4,3,2,1,0:T(8,128)S(1)}, f32[9,4,3,8,128]{4,3,2,1,0:T(8,128)S(1)}, u32[]{:S(2)}, u32[]{:S(2)}) collective-permute-start(f32[9,4,3,8,128]{4,3,2,1,0:T(8,128)S(1)} %get-tuple-element.5.f_ref), channel_id=1, source_target_pairs={{0,448},{64,0},{128,64},{192,128},{256,192},{320,256},{384,320},{4... | collective-permute-start | bytes 1327112 | tf_op jit(solution)/shard_map/ppermute | solution.py:207
  48.4 7.4 %collective-permute-start.2 = (f32[6,3,3,8,128]{4,3,2,1,0:T(8,128)S(1)}, f32[6,3,3,8,128]{4,3,2,1,0:T(8,128)S(1)}, u32[]{:S(2)}, u32[]{:S(2)}) collective-permute-start(f32[6,3,3,8,128]{4,3,2,1,0:T(8,128)S(1)} %get-tuple-element.6), channel_id=1, source_target_pairs={{0,1},{1,2},{2,3},{3,4},{4,5},{5,6},{6,7},{7,8},{8,9},{9,10},{10,1... | collective-permute-start | bytes 663560 | tf_op jit(solution)/shard_map/ppermute | solution.py:208
  55.8 1.9 %collective-permute-start.3 = (f32[6,3,3,8,128]{4,3,2,1,0:T(8,128)S(1)}, f32[6,3,3,8,128]{4,3,2,1,0:T(8,128)S(1)}, u32[]{:S(2)}, u32[]{:S(2)}) collective-permute-start(f32[6,3,3,8,128]{4,3,2,1,0:T(8,128)S(1)} %get-tuple-element.7), channel_id=1, source_target_pairs={{0,63},{1,0},{2,1},{3,2},{4,3},{5,4},{6,5},{7,6},{8,7},{9,8},{10,9... | collective-permute-start | bytes 663560 | tf_op jit(solution)/shard_map/ppermute | solution.py:209
  57.7 0.8 %shard_map.43.part_ref = f32[3,6,4,3,8,128]{5,4,3,2,1,0:T(8,128)S(1)} custom-call(f32[9,4,3,8,128]{4,3,2,1,0:T(8,128)S(1)} %get-tuple-element.5.f_ref), custom_call_target="tpu_custom_call" | custom-call | flops 4915200 | bytes 1327104 | tf_op jit(solution)/shard_map/pallas_call | solution.py:212
  58.5 0.2 collective-permute-done.2.rp_ref
  58.7 9.1 %collective-permute-done.3.rn_ref = f32[6,3,3,8,128]{4,3,2,1,0:T(8,128)S(1)} collective-permute-done((f32[6,3,3,8,128]{4,3,2,1,0:T(8,128)S(1)}, f32[6,3,3,8,128]{4,3,2,1,0:T(8,128)S(1)}, u32[]{:S(2)}, u32[]{:S(2)}) %collective-permute-start.3) | collective-permute-done | bytes 221216 | tf_op jit(solution)/shard_map/ppermute | solution.py:209
  67.8 0.0 collective-permute-done.fl_ref
  67.8 0.0 collective-permute-done.1.fr_ref
  67.8 1.4 %shard_map.44 = (f32[4,6,4,3,8,128]{5,4,3,2,1,0:T(8,128)}, f32[3,4,3,8,128]{4,3,2,1,0:T(8,128)}) custom-call(f32[9,4,3,8,128]{4,3,2,1,0:T(8,128)S(1)} %get-tuple-element.5.f_ref, f32[9,4,3,8,128]{4,3,2,1,0:T(8,128)S(1)} %collective-permute-done.fl_ref, f32[9,4,3,8,128]{4,3,2,1,0:T(8,128)S(1)} %collective-permute-done.1.fr_ref, ...), custom_call_target="tpu_custom_call" | custom-call | flops 3686400 | bytes 3981312 | tf_op jit(solution)/shard_map/pallas_call | solution.py:222
  (1 shorter events, 0.0 us)
Async XLA Ops:
  1.3 1.7 %copy-start.1 = (f32[1,8,3,24,8,128]{5,4,3,2,1,0:T(8,128)S(1)}, f32[1,8,3,24,8,128]{5,4,3,2,1,0:T(8,128)}, u32[]{:S(2)}) copy-start(f32[1,8,3,24,8,128]{5,4,3,2,1,0:T(8,128)} %param.2) | copy-start | bytes 7077892
  3.7 1.4 %copy-start = (f32[8,73,8,128]{3,2,1,0:T(8,128)}, f32[8,73,8,128]{3,2,1,0:T(8,128)S(1)}, u32[]{:S(2)}) copy-start(f32[8,73,8,128]{3,2,1,0:T(8,128)S(1)} %shard_map.41) | copy-start | bytes 7176196
  5.1 34.3 %all-to-all-start = ((f32[8,73,8,128]{3,2,1,0:T(8,128)}), f32[8,73,8,128]{3,2,1,0:T(8,128)S(1)}, u32[]{:S(2)}, u32[]{:S(2)}) async-start(f32[8,73,8,128]{3,2,1,0:T(8,128)} %copy-done), calls=%async_computation | async-start | bytes 4784128 | tf_op jit(solution)/shard_map/all_to_all | solution.py:246
  41.0 26.8 %collective-permute-start = (f32[9,4,3,8,128]{4,3,2,1,0:T(8,128)S(1)}, f32[9,4,3,8,128]{4,3,2,1,0:T(8,128)S(1)}, u32[]{:S(2)}, u32[]{:S(2)}) collective-permute-start(f32[9,4,3,8,128]{4,3,2,1,0:T(8,128)S(1)} %get-tuple-element.5.f_ref), channel_id=1, source_target_pairs={{0,64},{64,128},{128,192},{192,256},{256,320},{320,384},{384,448},... | collective-permute-start | bytes 1327112 | tf_op jit(solution)/shard_map/ppermute | solution.py:206
  43.8 24.0 %collective-permute-start.1 = (f32[9,4,3,8,128]{4,3,2,1,0:T(8,128)S(1)}, f32[9,4,3,8,128]{4,3,2,1,0:T(8,128)S(1)}, u32[]{:S(2)}, u32[]{:S(2)}) collective-permute-start(f32[9,4,3,8,128]{4,3,2,1,0:T(8,128)S(1)} %get-tuple-element.5.f_ref), channel_id=1, source_target_pairs={{0,448},{64,0},{128,64},{192,128},{256,192},{320,256},{384,320},{4... | collective-permute-start | bytes 1327112 | tf_op jit(solution)/shard_map/ppermute | solution.py:207
  48.4 10.2 %collective-permute-start.2 = (f32[6,3,3,8,128]{4,3,2,1,0:T(8,128)S(1)}, f32[6,3,3,8,128]{4,3,2,1,0:T(8,128)S(1)}, u32[]{:S(2)}, u32[]{:S(2)}) collective-permute-start(f32[6,3,3,8,128]{4,3,2,1,0:T(8,128)S(1)} %get-tuple-element.6), channel_id=1, source_target_pairs={{0,1},{1,2},{2,3},{3,4},{4,5},{5,6},{6,7},{7,8},{8,9},{9,10},{10,1... | collective-permute-start | bytes 663560 | tf_op jit(solution)/shard_map/ppermute | solution.py:208
  55.8 12.0 %collective-permute-start.3 = (f32[6,3,3,8,128]{4,3,2,1,0:T(8,128)S(1)}, f32[6,3,3,8,128]{4,3,2,1,0:T(8,128)S(1)}, u32[]{:S(2)}, u32[]{:S(2)}) collective-permute-start(f32[6,3,3,8,128]{4,3,2,1,0:T(8,128)S(1)} %get-tuple-element.7), channel_id=1, source_target_pairs={{0,63},{1,0},{2,1},{3,2},{4,3},{5,4},{6,5},{7,6},{8,7},{9,8},{10,9... | collective-permute-start | bytes 663560 | tf_op jit(solution)/shard_map/ppermute | solution.py:209

commit v14 on v12

--- a/solution.py
+++ b/solution.py
@@ -102,7 +102,7 @@
     return [(i, (i + step) % count) for i in range(count)]
 
 
-def halo_free_kernel(f_ref, part_ref):
+def halo_free_kernel(f_ref, part_ref, vel_ref):
     _, bins, planes, ny, nz = f_ref.shape
 
     def rolled(value, axis, size):
@@ -113,6 +113,8 @@
         for x in range(planes):
             velocity = [f_ref[c, b, x] for c in range(3)]
             stresses = [f_ref[3 + m, b, x] for m in range(6)]
+            for c in range(3):
+                vel_ref[c, b, x] = velocity[c]
             grad_u = [
                 [None, first_diff(rolled(velocity[c], 0, ny)), first_diff(rolled(velocity[c], 1, nz))]
                 for c in range(3)
@@ -133,7 +135,7 @@
                 part_ref[2, slot, b, x] = second_diff(along_y, stress) + second_diff(along_z, stress)
 
 
-def halo_kernel(f_ref, fl_ref, fr_ref, rp_ref, rn_ref, part_ref, terms_ref, vel_ref):
+def halo_kernel(f_ref, fl_ref, fr_ref, rp_ref, rn_ref, part_ref, terms_ref):
     _, bins, planes, ny, nz = f_ref.shape
 
     def at(comp, b, x):
@@ -151,8 +153,6 @@
         for x in range(planes):
             velocity = [f_ref[c, b, x] for c in range(3)]
             stresses = [f_ref[3 + m, b, x] for m in range(6)]
-            for c in range(3):
-                vel_ref[c, b, x] = velocity[c]
             grad_x = [first_diff(lambda k, c=c: at(c, b, x + k)) for c in range(3)]
             for slot, (first, second) in enumerate(stress_pairs):
                 comp = 3 + slot
@@ -178,24 +178,24 @@
     from_next = lax.ppermute(head, "bin", ring("bin", -1))
     cells = bins_dev * planes * ny * nz
     vmem = pl.BlockSpec(memory_space=pltpu.VMEM)
-    part = pl.pallas_call(
+    part, mean_velocity = pl.pallas_call(
         halo_free_kernel,
-        out_shape=jax.ShapeDtypeStruct((3, 6, bins_dev, planes, ny, nz), jnp.float32),
+        out_shape=(
+            jax.ShapeDtypeStruct((3, 6, bins_dev, planes, ny, nz), jnp.float32),
+            jax.ShapeDtypeStruct((3, bins_dev, planes, ny, nz), jnp.float32),
+        ),
         in_specs=[vmem],
-        out_specs=vmem,
+        out_specs=(vmem, vmem),
         compiler_params=pltpu.CompilerParams(vmem_limit_bytes=16 * 1024 * 1024),
         cost_estimate=pl.CostEstimate(
             flops=cells * 400, bytes_accessed=(9 + 18) * cells * 4, transcendentals=0
         ),
     )(fields)
-    return pl.pallas_call(
+    terms = pl.pallas_call(
         halo_kernel,
-        out_shape=(
-            jax.ShapeDtypeStruct((4, 6, bins_dev, planes, ny, nz), jnp.float32),
-            jax.ShapeDtypeStruct((3, bins_dev, planes, ny, nz), jnp.float32),
-        ),
+        out_shape=jax.ShapeDtypeStruct((4, 6, bins_dev, planes, ny, nz), jnp.float32),
         in_specs=[vmem] * 6,
-        out_specs=(vmem, vmem),
+        out_specs=vmem,
         compiler_params=pltpu.CompilerParams(vmem_limit_bytes=16 * 1024 * 1024),
         cost_estimate=pl.CostEstimate(
             flops=cells * 300,
@@ -203,6 +203,7 @@
             transcendentals=0,
         ),
     )(fields, from_left, from_right, from_prev, from_next, part)
+    return terms, mean_velocity
 
 
 def shards(snapshots, phase_index):

time: 68.5 us -> 68.6 us (level)
  transfers between devices with their start and end apart: 5 -> 5, of which waited for: 3 -> 2; matrix products, arithmetic and copies ran while one was open for 0% -> 0% of each run, Pallas kernels for 1% -> 2%
where the time goes in v14:
time: 68.6 us; the launch traced here: 68.3 us
  waiting for transfers between devices  37.9 us (55%)
  starting transfers between devices  21.9 us (32%)
  Pallas kernels  4.22 us (6%)
  local copies, waits for them, and re-layouts  1.93 us (3%)
  other arithmetic  1.61 us (2%)
  between operations  0.72 us (1%)
    all_to_all x1, waiting for transfers between devices, shards(): received = lax.all_to_all(payload, 'rev', 0, 0, tiled=True)  29.1 us
    ppermute x1, waiting for transfers between devices, finish_terms(): from_next = lax.ppermute(head, 'bin', ring('bin', -1))  8.83 us
    ppermute x1, starting transfers between devices, finish_terms(): from_prev = lax.ppermute(tail, 'bin', ring('bin', 1))  7.35 us
    all_to_all x1, starting transfers between devices, shards(): received = lax.all_to_all(payload, 'rev', 0, 0, tiled=True)  5.2 us
    ppermute x1, starting transfers between devices, finish_terms(): from_right = lax.ppermute(fields, 'rev', ring('rev', -1))  4.61 us
    ppermute x1, starting transfers between devices, finish_terms(): from_left = lax.ppermute(fields, 'rev', ring('rev', 1))  2.78 us
    ppermute x1, starting transfers between devices, finish_terms(): from_next = lax.ppermute(head, 'bin', ring('bin', -1))  1.92 us
    another operation x1, local copies, waits for them, and re-layouts, shards(): by_dest = frames.reshape(snaps, comps, n_rev, planes, ny, nz)  1.84 us
  transfers between devices with their start and end apart: 5, of which 2 were waited for; matrix products, arithmetic and copies ran while one was open for 0% of the time, Pallas kernels for 2%

profile of v14, /device:TPU:241, one launch (start us, length us, event | category | flops | bytes accessed | tf_op | source)
XLA Modules:
  0.0 68.3 jit_solution(9155948305480390138)
XLA Ops:
  0.6 0.0 copy-start
  0.6 1.8 %copy.4 = f32[8,3,8,3,8,128]{5,4,3,1,0,2:T(8,128)S(1)} copy(f32[8,3,8,3,8,128]{5,4,3,2,1,0:T(8,128)} %bitcast.7) | data formatting | bytes 4718592 | tf_op jit(solution)/shard_map/reshape;squeeze | solution.py:215
  2.5 0.0 copy-done
  2.5 1.6 %pad_maximum_fusion = f32[8,73,8,128]{3,2,1,0:T(8,128)} fusion(f32[8,1,8,128]{3,2,1,0:T(8,128)S(1)} %broadcast_in_dim.2, f32[8,72,8,128]{3,2,1,0:T(8,128)S(1)} %bitcast.6), kind=kLoop, calls=%fused_computation | loop fusion | flops 598016 | bytes 4784128 | tf_op jit(solution)/shard_map/concatenate | solution.py:219
  4.1 5.2 %all-to-all-start = ((f32[8,73,8,128]{3,2,1,0:T(8,128)}), f32[8,73,8,128]{3,2,1,0:T(8,128)S(1)}, u32[]{:S(2)}, u32[]{:S(2)}) async-start(f32[8,73,8,128]{3,2,1,0:T(8,128)} %pad_maximum_fusion), calls=%async_computation | async-start | bytes 4784128 | tf_op jit(solution)/shard_map/all_to_all | solution.py:220
  9.3 29.1 %all-to-all-done.x_ref = f32[8,73,8,128]{3,2,1,0:T(8,128)S(1)} async-done(((f32[8,73,8,128]{3,2,1,0:T(8,128)}), f32[8,73,8,128]{3,2,1,0:T(8,128)S(1)}, u32[]{:S(2)}, u32[]{:S(2)}) %all-to-all-start) | async-done | bytes 2392096 | tf_op jit(solution)/shard_map/all_to_all | solution.py:220
  38.4 0.1 min.12.bins_ref
  38.5 1.6 %shard_map.41 = (f32[9,4,3,8,128]{4,3,2,1,0:T(8,128)S(1)}, f32[6,3,3,8,128]{4,3,2,1,0:T(8,128)S(1)}, f32[6,3,3,8,128]{4,3,2,1,0:T(8,128)S(1)}) custom-call(s32[64]{0:T(128)S(1)} %min.12.bins_ref, f32[8,73,8,128]{3,2,1,0:T(8,128)S(1)} %all-to-all-done.x_ref), custom_call_target="tpu_custom_call" | custom-call | flops 2949120 | bytes 2834432 | tf_op jit(solution)/shard_map/pallas_call | solution.py:60
  40.1 2.8 %collective-permute-start = (f32[9,4,3,8,128]{4,3,2,1,0:T(8,128)S(1)}, f32[9,4,3,8,128]{4,3,2,1,0:T(8,128)S(1)}, u32[]{:S(2)}, u32[]{:S(2)}) collective-permute-start(f32[9,4,3,8,128]{4,3,2,1,0:T(8,128)S(1)} %get-tuple-element.7.f_ref), channel_id=1, source_target_pairs={{0,64},{64,128},{128,192},{192,256},{256,320},{320,384},{384,448},... | collective-permute-start | bytes 1327112 | tf_op jit(solution)/shard_map/ppermute | solution.py:175
  42.9 4.6 %collective-permute-start.1 = (f32[9,4,3,8,128]{4,3,2,1,0:T(8,128)S(1)}, f32[9,4,3,8,128]{4,3,2,1,0:T(8,128)S(1)}, u32[]{:S(2)}, u32[]{:S(2)}) collective-permute-start(f32[9,4,3,8,128]{4,3,2,1,0:T(8,128)S(1)} %get-tuple-element.7.f_ref), channel_id=1, source_target_pairs={{0,448},{64,0},{128,64},{192,128},{256,192},{320,256},{384,320},{4... | collective-permute-start | bytes 1327112 | tf_op jit(solution)/shard_map/ppermute | solution.py:176
  47.5 7.4 %collective-permute-start.2 = (f32[6,3,3,8,128]{4,3,2,1,0:T(8,128)S(1)}, f32[6,3,3,8,128]{4,3,2,1,0:T(8,128)S(1)}, u32[]{:S(2)}, u32[]{:S(2)}) collective-permute-start(f32[6,3,3,8,128]{4,3,2,1,0:T(8,128)S(1)} %get-tuple-element.8), channel_id=1, source_target_pairs={{0,1},{1,2},{2,3},{3,4},{4,5},{5,6},{6,7},{7,8},{8,9},{9,10},{10,1... | collective-permute-start | bytes 663560 | tf_op jit(solution)/shard_map/ppermute | solution.py:177
  54.8 1.9 %collective-permute-start.3 = (f32[6,3,3,8,128]{4,3,2,1,0:T(8,128)S(1)}, f32[6,3,3,8,128]{4,3,2,1,0:T(8,128)S(1)}, u32[]{:S(2)}, u32[]{:S(2)}) collective-permute-start(f32[6,3,3,8,128]{4,3,2,1,0:T(8,128)S(1)} %get-tuple-element.9), channel_id=1, source_target_pairs={{0,63},{1,0},{2,1},{3,2},{4,3},{5,4},{6,5},{7,6},{8,7},{9,8},{10,9... | collective-permute-start | bytes 663560 | tf_op jit(solution)/shard_map/ppermute | solution.py:178
  56.8 1.2 %shard_map.42 = (f32[3,6,4,3,8,128]{5,4,3,2,1,0:T(8,128)S(1)}, f32[3,4,3,8,128]{4,3,2,1,0:T(8,128)}) custom-call(f32[9,4,3,8,128]{4,3,2,1,0:T(8,128)S(1)} %get-tuple-element.7.f_ref), custom_call_target="tpu_custom_call" | custom-call | flops 4915200 | bytes 1327104 | tf_op jit(solution)/shard_map/pallas_call | solution.py:181
  58.0 0.0 collective-permute-done.2.rp_ref
  58.0 8.8 %collective-permute-done.3.rn_ref = f32[6,3,3,8,128]{4,3,2,1,0:T(8,128)S(1)} collective-permute-done((f32[6,3,3,8,128]{4,3,2,1,0:T(8,128)S(1)}, f32[6,3,3,8,128]{4,3,2,1,0:T(8,128)S(1)}, u32[]{:S(2)}, u32[]{:S(2)}) %collective-permute-start.3) | collective-permute-done | bytes 221216 | tf_op jit(solution)/shard_map/ppermute | solution.py:178
  66.8 0.0 collective-permute-done.fl_ref
  66.8 0.0 collective-permute-done.1.fr_ref
  66.8 1.4 %shard_map.43 = f32[4,6,4,3,8,128]{5,4,3,2,1,0:T(8,128)} custom-call(f32[9,4,3,8,128]{4,3,2,1,0:T(8,128)S(1)} %get-tuple-element.7.f_ref, f32[9,4,3,8,128]{4,3,2,1,0:T(8,128)S(1)} %collective-permute-done.fl_ref, f32[9,4,3,8,128]{4,3,2,1,0:T(8,128)S(1)} %collective-permute-done.1.fr_ref, f32[6,3,3,8,128]{4,3,2,1,0:T(8,128)S(1)} %collective-permute-done.2.rp_ref, ...), custom_call_target="tpu_custom_call" | custom-call | flops 3686400 | bytes 3981312 | tf_op jit(solution)/shard_map/pallas_call | solution.py:194
  (4 shorter events, 0.0 us)
Async XLA Ops:
  0.6 1.9 %copy-start = (s32[1,8]{1,0:T(1,128)S(1)}, s32[1,8]{1,0:T(1,128)}, u32[]{:S(2)}) copy-start(s32[1,8]{1,0:T(1,128)} %param.3) | copy-start | bytes 100
  4.1 34.3 %all-to-all-start = ((f32[8,73,8,128]{3,2,1,0:T(8,128)}), f32[8,73,8,128]{3,2,1,0:T(8,128)S(1)}, u32[]{:S(2)}, u32[]{:S(2)}) async-start(f32[8,73,8,128]{3,2,1,0:T(8,128)} %pad_maximum_fusion), calls=%async_computation | async-start | bytes 4784128 | tf_op jit(solution)/shard_map/all_to_all | solution.py:220
  40.1 26.8 %collective-permute-start = (f32[9,4,3,8,128]{4,3,2,1,0:T(8,128)S(1)}, f32[9,4,3,8,128]{4,3,2,1,0:T(8,128)S(1)}, u32[]{:S(2)}, u32[]{:S(2)}) collective-permute-start(f32[9,4,3,8,128]{4,3,2,1,0:T(8,128)S(1)} %get-tuple-element.7.f_ref), channel_id=1, source_target_pairs={{0,64},{64,128},{128,192},{192,256},{256,320},{320,384},{384,448},... | collective-permute-start | bytes 1327112 | tf_op jit(solution)/shard_map/ppermute | solution.py:175
  42.9 24.0 %collective-permute-start.1 = (f32[9,4,3,8,128]{4,3,2,1,0:T(8,128)S(1)}, f32[9,4,3,8,128]{4,3,2,1,0:T(8,128)S(1)}, u32[]{:S(2)}, u32[]{:S(2)}) collective-permute-start(f32[9,4,3,8,128]{4,3,2,1,0:T(8,128)S(1)} %get-tuple-element.7.f_ref), channel_id=1, source_target_pairs={{0,448},{64,0},{128,64},{192,128},{256,192},{320,256},{384,320},{4... | collective-permute-start | bytes 1327112 | tf_op jit(solution)/shard_map/ppermute | solution.py:176
  47.5 10.5 %collective-permute-start.2 = (f32[6,3,3,8,128]{4,3,2,1,0:T(8,128)S(1)}, f32[6,3,3,8,128]{4,3,2,1,0:T(8,128)S(1)}, u32[]{:S(2)}, u32[]{:S(2)}) collective-permute-start(f32[6,3,3,8,128]{4,3,2,1,0:T(8,128)S(1)} %get-tuple-element.8), channel_id=1, source_target_pairs={{0,1},{1,2},{2,3},{3,4},{4,5},{5,6},{6,7},{7,8},{8,9},{9,10},{10,1... | collective-permute-start | bytes 663560 | tf_op jit(solution)/shard_map/ppermute | solution.py:177
  54.8 12.0 %collective-permute-start.3 = (f32[6,3,3,8,128]{4,3,2,1,0:T(8,128)S(1)}, f32[6,3,3,8,128]{4,3,2,1,0:T(8,128)S(1)}, u32[]{:S(2)}, u32[]{:S(2)}) collective-permute-start(f32[6,3,3,8,128]{4,3,2,1,0:T(8,128)S(1)} %get-tuple-element.9), channel_id=1, source_target_pairs={{0,63},{1,0},{2,1},{3,2},{4,3},{5,4},{6,5},{7,6},{8,7},{9,8},{10,9... | collective-permute-start | bytes 663560 | tf_op jit(solution)/shard_map/ppermute | solution.py:178

commit v15 on v12

--- a/solution.py
+++ b/solution.py
@@ -37,7 +37,7 @@
         acc_ref[b, 9, 0] = acc_ref[b, 9, 0] + 1.0
         return carry
 
-    lax.fori_loop(0, snaps, body, 0, unroll=2)
+    lax.fori_loop(0, snaps, body, 0, unroll=4)
 
     for b in range(bins):
         count = acc_ref[b, 9, 0]

time: 68.5 us -> 68.5 us (level)
  the two profiles are of different devices: /device:TPU:241 before, /device:TPU:249 now
where the time goes in v15:
time: 68.5 us; the launch traced here: 68.1 us
  waiting for transfers between devices  38.4 us (56%)
  starting transfers between devices  21.9 us (32%)
  Pallas kernels  3.62 us (5%)
  local copies, waits for them, and re-layouts  1.93 us (3%)
  other arithmetic  1.59 us (2%)
  between operations  0.73 us (1%)
    all_to_all x1, waiting for transfers between devices, shards(): received = lax.all_to_all(payload, 'rev', 0, 0, tiled=True)  29.1 us
    ppermute x1, waiting for transfers between devices, finish_terms(): from_next = lax.ppermute(head, 'bin', ring('bin', -1))  9.14 us
    ppermute x1, starting transfers between devices, finish_terms(): from_prev = lax.ppermute(tail, 'bin', ring('bin', 1))  7.36 us
    all_to_all x1, starting transfers between devices, shards(): received = lax.all_to_all(payload, 'rev', 0, 0, tiled=True)  5.2 us
    ppermute x1, starting transfers between devices, finish_terms(): from_right = lax.ppermute(fields, 'rev', ring('rev', -1))  4.61 us
    ppermute x1, starting transfers between devices, finish_terms(): from_left = lax.ppermute(fields, 'rev', ring('rev', 1))  2.78 us
    ppermute x1, starting transfers between devices, finish_terms(): from_next = lax.ppermute(head, 'bin', ring('bin', -1))  1.92 us
    another operation x1, local copies, waits for them, and re-layouts, shards(): by_dest = frames.reshape(snaps, comps, n_rev, planes, ny, nz)  1.84 us
  transfers between devices with their start and end apart: 5, of which 3 were waited for; matrix products, arithmetic and copies ran while one was open for 0% of the time, Pallas kernels for 1%

profile of v15, /device:TPU:249, one launch (start us, length us, event | category | flops | bytes accessed | tf_op | source)
XLA Modules:
  0.0 68.1 jit_solution(4764830417276255417)
XLA Ops:
  0.6 0.0 copy-start
  0.6 1.8 %copy.4 = f32[8,3,8,3,8,128]{5,4,3,1,0,2:T(8,128)S(1)} copy(f32[8,3,8,3,8,128]{5,4,3,2,1,0:T(8,128)} %bitcast.7) | data formatting | bytes 4718592 | tf_op jit(solution)/shard_map/reshape;squeeze | solution.py:214
  2.5 0.0 copy-done
  2.5 1.6 %pad_maximum_fusion = f32[8,73,8,128]{3,2,1,0:T(8,128)} fusion(f32[8,1,8,128]{3,2,1,0:T(8,128)S(1)} %broadcast_in_dim.2, f32[8,72,8,128]{3,2,1,0:T(8,128)S(1)} %bitcast.6), kind=kLoop, calls=%fused_computation | loop fusion | flops 598016 | bytes 4784128 | tf_op jit(solution)/shard_map/concatenate | solution.py:218
  4.1 5.2 %all-to-all-start = ((f32[8,73,8,128]{3,2,1,0:T(8,128)}), f32[8,73,8,128]{3,2,1,0:T(8,128)S(1)}, u32[]{:S(2)}, u32[]{:S(2)}) async-start(f32[8,73,8,128]{3,2,1,0:T(8,128)} %pad_maximum_fusion), calls=%async_computation | async-start | bytes 4784128 | tf_op jit(solution)/shard_map/all_to_all | solution.py:219
  9.3 29.1 %all-to-all-done.x_ref = f32[8,73,8,128]{3,2,1,0:T(8,128)S(1)} async-done(((f32[8,73,8,128]{3,2,1,0:T(8,128)}), f32[8,73,8,128]{3,2,1,0:T(8,128)S(1)}, u32[]{:S(2)}, u32[]{:S(2)}) %all-to-all-start) | async-done | bytes 2392096 | tf_op jit(solution)/shard_map/all_to_all | solution.py:219
  38.4 0.1 min.12.bins_ref
  38.5 1.5 %shard_map.41 = (f32[9,4,3,8,128]{4,3,2,1,0:T(8,128)S(1)}, f32[6,3,3,8,128]{4,3,2,1,0:T(8,128)S(1)}, f32[6,3,3,8,128]{4,3,2,1,0:T(8,128)S(1)}) custom-call(s32[64]{0:T(128)S(1)} %min.12.bins_ref, f32[8,73,8,128]{3,2,1,0:T(8,128)S(1)} %all-to-all-done.x_ref), custom_call_target="tpu_custom_call" | custom-call | flops 2949120 | bytes 2834432 | tf_op jit(solution)/shard_map/pallas_call | solution.py:60
  40.0 2.8 %collective-permute-start = (f32[9,4,3,8,128]{4,3,2,1,0:T(8,128)S(1)}, f32[9,4,3,8,128]{4,3,2,1,0:T(8,128)S(1)}, u32[]{:S(2)}, u32[]{:S(2)}) collective-permute-start(f32[9,4,3,8,128]{4,3,2,1,0:T(8,128)S(1)} %get-tuple-element.5.f_ref), channel_id=1, source_target_pairs={{0,64},{64,128},{128,192},{192,256},{256,320},{320,384},{384,448},... | collective-permute-start | bytes 1327112 | tf_op jit(solution)/shard_map/ppermute | solution.py:175
  42.7 4.6 %collective-permute-start.1 = (f32[9,4,3,8,128]{4,3,2,1,0:T(8,128)S(1)}, f32[9,4,3,8,128]{4,3,2,1,0:T(8,128)S(1)}, u32[]{:S(2)}, u32[]{:S(2)}) collective-permute-start(f32[9,4,3,8,128]{4,3,2,1,0:T(8,128)S(1)} %get-tuple-element.5.f_ref), channel_id=1, source_target_pairs={{0,448},{64,0},{128,64},{192,128},{256,192},{320,256},{384,320},{4... | collective-permute-start | bytes 1327112 | tf_op jit(solution)/shard_map/ppermute | solution.py:176
  47.4 7.4 %collective-permute-start.2 = (f32[6,3,3,8,128]{4,3,2,1,0:T(8,128)S(1)}, f32[6,3,3,8,128]{4,3,2,1,0:T(8,128)S(1)}, u32[]{:S(2)}, u32[]{:S(2)}) collective-permute-start(f32[6,3,3,8,128]{4,3,2,1,0:T(8,128)S(1)} %get-tuple-element.6), channel_id=1, source_target_pairs={{0,1},{1,2},{2,3},{3,4},{4,5},{5,6},{6,7},{7,8},{8,9},{9,10},{10,1... | collective-permute-start | bytes 663560 | tf_op jit(solution)/shard_map/ppermute | solution.py:177
  54.7 1.9 %collective-permute-start.3 = (f32[6,3,3,8,128]{4,3,2,1,0:T(8,128)S(1)}, f32[6,3,3,8,128]{4,3,2,1,0:T(8,128)S(1)}, u32[]{:S(2)}, u32[]{:S(2)}) collective-permute-start(f32[6,3,3,8,128]{4,3,2,1,0:T(8,128)S(1)} %get-tuple-element.7), channel_id=1, source_target_pairs={{0,63},{1,0},{2,1},{3,2},{4,3},{5,4},{6,5},{7,6},{8,7},{9,8},{10,9... | collective-permute-start | bytes 663560 | tf_op jit(solution)/shard_map/ppermute | solution.py:178
  56.7 0.8 %shard_map.42.part_ref = f32[3,6,4,3,8,128]{5,4,3,2,1,0:T(8,128)S(1)} custom-call(f32[9,4,3,8,128]{4,3,2,1,0:T(8,128)S(1)} %get-tuple-element.5.f_ref), custom_call_target="tpu_custom_call" | custom-call | flops 4915200 | bytes 1327104 | tf_op jit(solution)/shard_map/pallas_call | solution.py:181
  57.4 0.2 collective-permute-done.2.rp_ref
  57.6 9.1 %collective-permute-done.3.rn_ref = f32[6,3,3,8,128]{4,3,2,1,0:T(8,128)S(1)} collective-permute-done((f32[6,3,3,8,128]{4,3,2,1,0:T(8,128)S(1)}, f32[6,3,3,8,128]{4,3,2,1,0:T(8,128)S(1)}, u32[]{:S(2)}, u32[]{:S(2)}) %collective-permute-start.3) | collective-permute-done | bytes 221216 | tf_op jit(solution)/shard_map/ppermute | solution.py:178
  66.7 0.0 collective-permute-done.fl_ref
  66.7 0.0 collective-permute-done.1.fr_ref
  66.7 1.4 %shard_map.43 = (f32[4,6,4,3,8,128]{5,4,3,2,1,0:T(8,128)}, f32[3,4,3,8,128]{4,3,2,1,0:T(8,128)}) custom-call(f32[9,4,3,8,128]{4,3,2,1,0:T(8,128)S(1)} %get-tuple-element.5.f_ref, f32[9,4,3,8,128]{4,3,2,1,0:T(8,128)S(1)} %collective-permute-done.fl_ref, f32[9,4,3,8,128]{4,3,2,1,0:T(8,128)S(1)} %collective-permute-done.1.fr_ref, ...), custom_call_target="tpu_custom_call" | custom-call | flops 3686400 | bytes 3981312 | tf_op jit(solution)/shard_map/pallas_call | solution.py:191
  (4 shorter events, 0.0 us)
Async XLA Ops:
  0.6 1.9 %copy-start = (s32[1,8]{1,0:T(1,128)S(1)}, s32[1,8]{1,0:T(1,128)}, u32[]{:S(2)}) copy-start(s32[1,8]{1,0:T(1,128)} %param.3) | copy-start | bytes 100
  4.1 34.3 %all-to-all-start = ((f32[8,73,8,128]{3,2,1,0:T(8,128)}), f32[8,73,8,128]{3,2,1,0:T(8,128)S(1)}, u32[]{:S(2)}, u32[]{:S(2)}) async-start(f32[8,73,8,128]{3,2,1,0:T(8,128)} %pad_maximum_fusion), calls=%async_computation | async-start | bytes 4784128 | tf_op jit(solution)/shard_map/all_to_all | solution.py:219
  40.0 26.8 %collective-permute-start = (f32[9,4,3,8,128]{4,3,2,1,0:T(8,128)S(1)}, f32[9,4,3,8,128]{4,3,2,1,0:T(8,128)S(1)}, u32[]{:S(2)}, u32[]{:S(2)}) collective-permute-start(f32[9,4,3,8,128]{4,3,2,1,0:T(8,128)S(1)} %get-tuple-element.5.f_ref), channel_id=1, source_target_pairs={{0,64},{64,128},{128,192},{192,256},{256,320},{320,384},{384,448},... | collective-permute-start | bytes 1327112 | tf_op jit(solution)/shard_map/ppermute | solution.py:175
  42.7 24.0 %collective-permute-start.1 = (f32[9,4,3,8,128]{4,3,2,1,0:T(8,128)S(1)}, f32[9,4,3,8,128]{4,3,2,1,0:T(8,128)S(1)}, u32[]{:S(2)}, u32[]{:S(2)}) collective-permute-start(f32[9,4,3,8,128]{4,3,2,1,0:T(8,128)S(1)} %get-tuple-element.5.f_ref), channel_id=1, source_target_pairs={{0,448},{64,0},{128,64},{192,128},{256,192},{320,256},{384,320},{4... | collective-permute-start | bytes 1327112 | tf_op jit(solution)/shard_map/ppermute | solution.py:176
  47.4 10.2 %collective-permute-start.2 = (f32[6,3,3,8,128]{4,3,2,1,0:T(8,128)S(1)}, f32[6,3,3,8,128]{4,3,2,1,0:T(8,128)S(1)}, u32[]{:S(2)}, u32[]{:S(2)}) collective-permute-start(f32[6,3,3,8,128]{4,3,2,1,0:T(8,128)S(1)} %get-tuple-element.6), channel_id=1, source_target_pairs={{0,1},{1,2},{2,3},{3,4},{4,5},{5,6},{6,7},{7,8},{8,9},{9,10},{10,1... | collective-permute-start | bytes 663560 | tf_op jit(solution)/shard_map/ppermute | solution.py:177
  54.7 12.0 %collective-permute-start.3 = (f32[6,3,3,8,128]{4,3,2,1,0:T(8,128)S(1)}, f32[6,3,3,8,128]{4,3,2,1,0:T(8,128)S(1)}, u32[]{:S(2)}, u32[]{:S(2)}) collective-permute-start(f32[6,3,3,8,128]{4,3,2,1,0:T(8,128)S(1)} %get-tuple-element.7), channel_id=1, source_target_pairs={{0,63},{1,0},{2,1},{3,2},{4,3},{5,4},{6,5},{7,6},{8,7},{9,8},{10,9... | collective-permute-start | bytes 663560 | tf_op jit(solution)/shard_map/ppermute | solution.py:178
